TPU v7x, 256 devices: a whole 4x4x8 slice. The times are simulated.
256 devices in a mesh: dp: 64 (over y, z, core), vocab: 4 (over x).
Axes of the slice: x: 4, y: 4, z: 8, core: 2. Of those that a mesh axis runs over, the one named last changes fastest.
Arguments:
- hidden_rows: bfloat16 [16384, 5120], P('dp'), may hold values from -300 to 300, as said below
- plan_lengths: int32 [64], replicated, may hold values from 1 to 256, 8192 in all
- shard_of_class: int32 [64], replicated, may hold values from 0 to 63, each once
- head_weight: bfloat16 [5120, 3072], P(None, 'vocab'), may hold values from -0.078125 to 0.078125
- teacher_logprobs: bfloat16 [8192, 3072], P('dp', 'vocab'), as said below
Outputs:
- row_grad: bfloat16 [16384, 5120], P('dp')
- row_kl: float32 [8192], P('dp')
Inputs may be any that keep to these rules, and one draw needn't show every extreme that they name: `plan_lengths`: the plan lengths sum to 8192 and the longest is exactly 256. `shard_of_class`: each shard is named once. `hidden_rows`: unused slots hold finite values. `teacher_logprobs`: each row is a log-softmax over the 3072 entries, rounded to bfloat16.
All inputs are finite; a program needn't handle non-finite values.
Results may differ from a plain program's by a relative error of at most 0.0046.
Values may be sent and summed in bfloat16 or wider, within the bound.
No kernel may reach another device: no remote copies, remote signals or barrier semaphores. Data moves between devices by JAX's collectives and lax.ppermute only.
A program may use at most 64 MiB of HBM per device.

v0:
```python
import jax
import jax.numpy as jnp
from jax import lax
from jax.sharding import PartitionSpec as P

loss_scale = 64.0


def divergence(row_block, teacher_block, live_rows, weight):
    logits = jnp.dot(row_block, weight, preferred_element_type=jnp.float32)
    log_teacher = teacher_block.astype(jnp.float32)
    teacher_prob = jnp.exp(log_teacher)
    own_top = jnp.max(logits, axis=1)
    own_mass = jnp.sum(teacher_prob, axis=1)
    own_cross = jnp.sum(teacher_prob * (log_teacher - logits), axis=1)
    row_top = lax.pmax(own_top, "vocab")
    own_total = jnp.sum(jnp.exp(logits - row_top[:, None]), axis=1)
    exp_total, prob_total, cross_term = lax.psum((own_total, own_mass, own_cross), "vocab")
    log_total = row_top + jnp.log(exp_total)
    row_div = (cross_term + prob_total * log_total) * live_rows
    grad_logits = (
        loss_scale
        * (prob_total[:, None] * jnp.exp(logits - log_total[:, None]) - teacher_prob)
        * live_rows[:, None]
    ).astype(jnp.bfloat16)
    partial_grad = lax.dot_general(
        grad_logits, weight, (((1,), (1,)), ((), ())), preferred_element_type=jnp.float32
    )
    hidden_grad = lax.psum(partial_grad, "vocab").astype(jnp.bfloat16)
    return (hidden_grad, row_div)


def body(hidden_rows, plan_lengths, shard_of_class, head_weight, teacher_logprobs):
    shards = lax.axis_size("dp")
    myself = lax.axis_index("dp")
    source_slots = hidden_rows.shape[0]
    feature_width = hidden_rows.shape[1]
    slot_depth = source_slots // shards
    balanced = teacher_logprobs.shape[0]
    offsets = jnp.cumsum(plan_lengths) - plan_lengths
    classes = jnp.arange(shards, dtype=jnp.int32)
    inverse = jnp.sum(
        jnp.where(shard_of_class[None, :] == classes[:, None], classes[None, :], 0), axis=1
    )
    own_offset = offsets[myself]
    column_of = (inverse - own_offset) % shards
    shard_at = shard_of_class[(own_offset + classes) % shards]
    rank_rows = jnp.arange(slot_depth, dtype=jnp.int32)[:, None]
    recv_row = rank_rows * shards + ((inverse[myself] - offsets) % shards)[None, :]
    recv_live = recv_row < plan_lengths[None, :]
    recv_slot = jnp.where(recv_live, (offsets[None, :] + recv_row) // shards, balanced)
    safe_slot = jnp.minimum(recv_slot, balanced - 1).reshape(-1)
    outgoing = jnp.take(hidden_rows.reshape(slot_depth, shards, feature_width), column_of, axis=1)
    arriving = lax.all_to_all(outgoing, "dp", split_axis=1, concat_axis=1, tiled=True)
    flattened = arriving.reshape(slot_depth * shards, feature_width)
    live_rows = recv_live.reshape(-1).astype(jnp.float32)
    teacher_slots = jnp.take(teacher_logprobs, safe_slot, axis=0)
    returning, row_div = divergence(flattened, teacher_slots, live_rows, head_weight)
    row_kl = jnp.zeros((balanced,), jnp.float32).at[recv_slot.reshape(-1)].add(row_div, mode="drop")
    share_width = returning.shape[1]
    returned = lax.all_to_all(
        returning.reshape(slot_depth, shards, share_width),
        "dp",
        split_axis=1,
        concat_axis=1,
        tiled=True,
    )
    grad_share = jnp.take(returned, shard_at, axis=1).reshape(source_slots, share_width)
    return (grad_share, row_kl)


def solution(mesh):
    return jax.shard_map(
        body,
        mesh=mesh,
        in_specs=(P("dp", None), P(), P(), P(None, "vocab"), P("dp", "vocab")),
        out_specs=(P("dp", None), P("dp")),
        check_vma=False,
    )
```

profile of v0, /device:TPU:1, one launch (start us, length us, event | category | flops | bytes accessed | tf_op | source)
XLA Modules:
  0.0 298.8 jit_solution(14799237197427120690)
XLA Ops:
  0.6 0.0 copy-start
  0.6 0.8 select_reduce_fusion
  1.5 0.8 copy.15
  2.2 0.1 reduce-window.9
  2.3 0.1 reduce
  2.4 0.6 dynamic_slice.6
  3.0 1.3 and_select_fusion.4
  4.3 0.6 dynamic_slice.7
  4.9 0.7 compare_and_fusion.1
  5.6 3.8 %copy.16 = bf16[4,64,5120]{2,0,1:T(4,128)(2,1)S(1)} copy(bf16[4,64,5120]{2,1,0:T(8,128)(2,1)} %bitcast.18) | data formatting | bytes 5242880 | tf_op jit(solution)/shard_map/reshape | solution.py:53
  9.3 4.2 %gather_fusion.2 = bf16[64,4,5120]{2,1,0:T(4,128)(2,1)} fusion(bf16[4,64,5120]{2,0,1:T(4,128)(2,1)S(1)} %copy.16, s32[1024]{0:T(1024)S(1)} %pad_clamp_fusion.1), kind=kCustom, calls=%fused_computation.clone | custom fusion | bytes 5243136 | tf_op jit(solution)/shard_map/jit(_take)/gather | solution.py:53
  13.5 4.5 %select_bitcast_fusion.1 = bf16[4,64,5120]{2,0,1:T(4,128)(2,1)} fusion(bf16[64,4,5120]{2,1,0:T(4,128)(2,1)} %gather_fusion.2, pred[64]{0:T(512)(128)(4,1)S(1)} %get-tuple-element.14), kind=kLoop, calls=%fused_computation.6 | loop fusion | flops 1310720 | bytes 5242944 | tf_op jit(solution)/shard_map/jit(_take)/select_n | solution.py:53
  18.0 0.0 copy-start.2
  18.0 13.3 %all-to-all-start = ((bf16[4,64,5120]{2,0,1:T(4,128)(2,1)}), bf16[4,64,5120]{2,0,1:T(4,128)(2,1)S(1)}, u32[]{:S(2)}, u32[]{:S(2)}) async-start(bf16[4,64,5120]{2,0,1:T(4,128)(2,1)} %select_bitcast_fusion.1), calls=%async_computation | async-start | bytes 5242880 | tf_op jit(solution)/shard_map/all_to_all | solution.py:54
  31.3 0.1 add_add_fusion
  31.4 0.1 add.183
  31.5 0.1 add.185
  31.5 0.0 copy-done.2
  31.5 0.1 add_compare_fusion
  31.6 0.1 lt.100
  31.7 0.1 lt.102
  31.8 0.0 copy-done
  31.8 1.2 gather_fusion
  33.1 60.5 %all-to-all-done = bf16[4,64,5120]{2,0,1:T(4,128)(2,1)S(1)} async-done(((bf16[4,64,5120]{2,0,1:T(4,128)(2,1)}), bf16[4,64,5120]{2,0,1:T(4,128)(2,1)S(1)}, u32[]{:S(2)}, u32[]{:S(2)}) %all-to-all-start) | async-done | bytes 2621472 | tf_op jit(solution)/shard_map/all_to_all | solution.py:54
  93.5 0.8 copy.17
  94.3 5.5 %fusion.19 = (f32[256]{0:T(256)S(1)}, f32[256,768]{1,0:T(8,128)S(1)}) fusion(bf16[256,5120]{1,0:T(8,128)(2,1)S(1)} %bitcast.21, bf16[5120,768]{1,0:T(8,128)(2,1)} %param.10), kind=kOutput, calls=%fused_computation.66 | convolution fusion | flops 2013462272 | bytes 11273216 | tf_op jit(solution)/shard_map/dot_general | solution.py:10
  99.9 8.5 %pmax.7 = f32[256]{0:T(256)S(1)} all-reduce(f32[256]{0:T(256)S(1)} %get-tuple-element.16), channel_id=1, replica_groups=mesh['dp'=64,'vocab'=4] {'vocab'}, use_global_device_ids=true, to_apply=%region_5.7 | all-reduce | flops 256 | bytes 2048 | tf_op jit(solution)/shard_map/pmax | solution.py:16
  108.3 0.6 fusion.5
  108.9 6.2 %all-reduce.1 = (f32[256]{0:T(256)S(1)}, f32[256]{0:T(256)S(1)}) all-reduce(f32[256]{0:T(256)S(1)} %get-tuple-element.4, f32[256]{0:T(256)S(1)} %get-tuple-element.5), channel_id=1, replica_groups=mesh['dp'=64,'vocab'=4] {'vocab'}, use_global_device_ids=true, to_apply=%region_7.9 | all-reduce | flops 512 | bytes 4096 | tf_op jit(solution)/shard_map/psum | solution.py:18
  115.1 8.0 %fusion.6 = f32[256,5120]{1,0:T(8,128)} fusion(bf16[5120,768]{1,0:T(8,128)(2,1)} %param.10, f32[256,768]{1,0:T(8,128)S(1)} %get-tuple-element.17, f32[256]{0:T(256)S(1)} %broadcast_select_fusion.1, f32[256]{0:T(256)S(1)} %log_add_fusion, f32[256]{0:T(256)S(1)} %get-tuple-element.9, bf16[256,768]{1,0:T(8,128)(2,1)S(1)} %gather_fusion, ...), kind=kOutput, calls=%fused_computation.16 | convolution fusion | flops 2014642176 | bytes 14290176 | tf_op jit(solution)/shard_map/dot_general | solution.py:26
  123.1 89.4 %all-reduce.3 = (bf16[256,5120]{1,0:T(8,128)(2,1)S(1)}, f32[256]{0:T(256)S(1)}) all-reduce(f32[256,5120]{1,0:T(8,128)} %fusion.6, f32[256]{0:T(256)S(1)} %get-tuple-element.3), channel_id=1, replica_groups=mesh['dp'=64,'vocab'=4] {'vocab'}, use_global_device_ids=true, to_apply=%region_8.10 | all-reduce | flops 1310976 | bytes 7866368 | tf_op jit(solution)/shard_map/psum | solution.py:29
  212.5 3.5 %copy.18 = bf16[4,64,5120]{2,0,1:T(4,128)(2,1)} copy(bf16[4,64,5120]{2,1,0:T(8,128)(2,1)S(1)} %bitcast.20) | data formatting | bytes 5242880 | tf_op jit(solution)/shard_map/reshape | solution.py:62
  216.0 0.0 copy-start.1
  216.0 11.2 %all-to-all-start.1 = ((bf16[4,64,5120]{2,0,1:T(4,128)(2,1)}), bf16[4,64,5120]{2,0,1:T(4,128)(2,1)S(1)}, u32[]{:S(2)}, u32[]{:S(2)}) async-start(bf16[4,64,5120]{2,0,1:T(4,128)(2,1)} %copy.18), calls=%async_computation.1 | async-start | bytes 5242880 | tf_op jit(solution)/shard_map/all_to_all | solution.py:61
  227.1 0.7 fusion.15
  227.8 0.0 copy-done.1
  227.8 0.8 gather_fusion.1
  228.6 2.8 scatter_custom_fusion
  231.5 57.9 %all-to-all-done.1 = bf16[4,64,5120]{2,0,1:T(4,128)(2,1)S(1)} async-done(((bf16[4,64,5120]{2,0,1:T(4,128)(2,1)}), bf16[4,64,5120]{2,0,1:T(4,128)(2,1)S(1)}, u32[]{:S(2)}, u32[]{:S(2)}) %all-to-all-start.1) | async-done | bytes 2621472 | tf_op jit(solution)/shard_map/all_to_all | solution.py:61
  289.4 4.2 %gather_fusion.3 = bf16[64,4,5120]{2,1,0:T(4,128)(2,1)} fusion(bf16[4,64,5120]{2,0,1:T(4,128)(2,1)S(1)} %all-to-all-done.1, s32[1024]{0:T(1024)S(1)} %pad_clamp_fusion), kind=kCustom, calls=%fused_computation.1.clone | custom fusion | bytes 5243136 | tf_op jit(solution)/shard_map/jit(_take)/gather | solution.py:68
  293.5 3.0 %select_bitcast_fusion = bf16[4,64,5120]{2,0,1:T(4,128)(2,1)S(1)} fusion(bf16[64,4,5120]{2,1,0:T(4,128)(2,1)} %gather_fusion.3, pred[64]{0:T(512)(128)(4,1)S(1)} %compare_and_fusion), kind=kLoop, calls=%fused_computation.5 | loop fusion | flops 1310720 | bytes 5242944 | tf_op jit(solution)/shard_map/jit(_take)/select_n | solution.py:68
  296.5 2.3 copy.19
  (13 shorter events, 0.1 us)
Async XLA Ops:
  0.6 31.2 %copy-start = (bf16[128,768]{1,0:T(8,128)(2,1)S(1)}, bf16[128,768]{1,0:T(8,128)(2,1)}, u32[]{:S(2)}) copy-start(bf16[128,768]{1,0:T(8,128)(2,1)} %param.11) | copy-start | bytes 589828
  18.0 13.5 %copy-start.2 = (s32[64]{0:T(128)S(1)}, s32[64]{0:T(128)}, u32[]{:S(2)}) copy-start(s32[64]{0:T(128)} %param.8) | copy-start | bytes 772
  18.0 75.5 %all-to-all-start = ((bf16[4,64,5120]{2,0,1:T(4,128)(2,1)}), bf16[4,64,5120]{2,0,1:T(4,128)(2,1)S(1)}, u32[]{:S(2)}, u32[]{:S(2)}) async-start(bf16[4,64,5120]{2,0,1:T(4,128)(2,1)} %select_bitcast_fusion.1), calls=%async_computation | async-start | bytes 5242880 | tf_op jit(solution)/shard_map/all_to_all | solution.py:54
  216.0 11.8 %copy-start.1 = (s32[64]{0:T(128)S(1)}, s32[64]{0:T(128)}, u32[]{:S(2)}) copy-start(s32[64]{0:T(128)} %param.9) | copy-start | bytes 772
  216.0 73.4 %all-to-all-start.1 = ((bf16[4,64,5120]{2,0,1:T(4,128)(2,1)}), bf16[4,64,5120]{2,0,1:T(4,128)(2,1)S(1)}, u32[]{:S(2)}, u32[]{:S(2)}) async-start(bf16[4,64,5120]{2,0,1:T(4,128)(2,1)} %copy.18), calls=%async_computation.1 | async-start | bytes 5242880 | tf_op jit(solution)/shard_map/all_to_all | solution.py:61
where the time goes:
time: 299 us
  waiting for transfers between devices  118 us (39%)
  blocking collectives  104 us (35%)
  starting transfers between devices  24.4 us (8%)
  local copies, waits for them, and re-layouts  22.9 us (8%)
  other arithmetic  14.8 us (5%)
  matrix products  13.5 us (5%)
    psum x1, blocking collectives, divergence(): hidden_grad = lax.psum(partial_grad, 'vocab').astype(jnp.bfloat16)  89.4 us
    all_to_all x1, waiting for transfers between devices, body(): lax.all_to_all(outgoing, 'dp', split_axis=1, concat_axis=1, tiled=True)  60.5 us
    all_to_all x1, waiting for transfers between devices, body(): lax.all_to_all(returning.reshape(slot_depth, shards, share_width), 'dp',...  57.9 us
    all_to_all x1, starting transfers between devices, body(): lax.all_to_all(outgoing, 'dp', split_axis=1, concat_axis=1, tiled=True)  13.3 us
    all_to_all x1, starting transfers between devices, body(): lax.all_to_all(returning.reshape(slot_depth, shards, share_width), 'dp',...  11.2 us
    pmax x1, blocking collectives, divergence(): row_top = lax.pmax(own_top, 'vocab')  8.47 us
    dot_general x1, matrix products, divergence(): lax.dot_general(grad_logits, weight, (((1,), (1,)), ((), ())), preferred_...  7.99 us
    psum x1, blocking collectives, divergence(): lax.psum((own_total, own_mass, own_cross), 'vocab')  6.18 us
  transfers between devices with their start and end apart: 2, of which 2 were waited for; matrix products, arithmetic and copies ran while one was open for 2% of the time, Pallas kernels for 0%

commit v1 on v0

v1 whole, which is shorter than its diff:
```python
import jax
import jax.numpy as jnp
from jax import lax
from jax.sharding import PartitionSpec as P

loss_scale = 64.0


def divergence(row_block, teacher_block, live, weight):
    logits = jnp.dot(row_block, weight, preferred_element_type=jnp.float32)
    log_teacher = teacher_block.astype(jnp.float32)
    teacher_prob = jnp.exp(log_teacher)
    own_top = jnp.max(logits, axis=1)
    own_total = jnp.sum(jnp.exp(logits - own_top[:, None]), axis=1)
    own_mass = jnp.sum(teacher_prob, axis=1)
    own_cross = jnp.sum(teacher_prob * (log_teacher - logits), axis=1)
    stats = lax.all_gather(jnp.stack([own_top, own_total, own_mass, own_cross]), "vocab")
    tops, totals, masses, crosses = stats[:, 0], stats[:, 1], stats[:, 2], stats[:, 3]
    row_top = jnp.max(tops, axis=0)
    exp_total = jnp.sum(totals * jnp.exp(tops - row_top[None, :]), axis=0)
    prob_total = jnp.sum(masses, axis=0)
    cross_term = jnp.sum(crosses, axis=0)
    log_total = row_top + jnp.log(exp_total)
    row_div = jnp.where(live, cross_term + prob_total * log_total, 0.0)
    grad_logits = jnp.where(
        live[:, None],
        loss_scale * (prob_total[:, None] * jnp.exp(logits - log_total[:, None]) - teacher_prob),
        0.0,
    ).astype(jnp.bfloat16)
    partial_grad = lax.dot_general(
        grad_logits, weight, (((1,), (1,)), ((), ())), preferred_element_type=jnp.float32
    )
    summed = lax.psum_scatter(partial_grad, "vocab", scatter_dimension=0, tiled=True)
    hidden_grad = lax.all_gather(summed.astype(jnp.bfloat16), "vocab", axis=0, tiled=True)
    return hidden_grad, row_div


def body(hidden_rows, plan_lengths, shard_of_class, head_weight, teacher_logprobs):
    shards = lax.axis_size("dp")
    myself = lax.axis_index("dp")
    source_slots = hidden_rows.shape[0]
    slot_depth = source_slots // shards
    balanced = teacher_logprobs.shape[0]
    offsets = jnp.cumsum(plan_lengths) - plan_lengths
    classes = jnp.arange(shards, dtype=jnp.int32)
    inverse = jnp.sum(
        jnp.where(shard_of_class[None, :] == classes[:, None], classes[None, :], 0), axis=1
    )
    depth = jnp.arange(slot_depth, dtype=jnp.int32)
    first_col = (inverse[myself] - offsets) % shards
    first_slot = (offsets + first_col) // shards
    send_rows = jnp.minimum(first_slot[:, None] + depth[None, :], balanced - 1)
    outgoing = jnp.take(teacher_logprobs, send_rows.reshape(-1), axis=0).reshape(
        shards, slot_depth, teacher_logprobs.shape[1]
    )
    arriving = lax.all_to_all(outgoing, "dp", split_axis=0, concat_axis=0, tiled=True)
    own_offset = offsets[myself]
    shard_at = shard_of_class[(own_offset + classes) % shards]
    teacher_slots = jnp.take(arriving, shard_at, axis=0)
    teacher_slots = jnp.transpose(teacher_slots, (1, 0, 2)).reshape(source_slots, -1)
    live = jnp.arange(source_slots, dtype=jnp.int32) < plan_lengths[myself]
    row_grad, row_div = divergence(hidden_rows, teacher_slots, live, head_weight)
    every_div = lax.all_gather(row_div, "dp")
    packed = jnp.arange(balanced, dtype=jnp.int32) * shards + inverse[myself]
    owner = jnp.sum((offsets[None, :] <= packed[:, None]).astype(jnp.int32), axis=1) - 1
    row_kl = every_div[owner, packed - offsets[owner]]
    return row_grad, row_kl


def solution(mesh):
    return jax.shard_map(
        body,
        mesh=mesh,
        in_specs=(P("dp", None), P(), P(), P(None, "vocab"), P("dp", "vocab")),
        out_specs=(P("dp", None), P("dp")),
        check_vma=False,
    )
```

time: 299 us -> 188 us (0.63)
  waiting for transfers between devices: 118 us -> 62 us
  blocking collectives: 104 us -> 54.8 us
  between operations: 0.79 us -> 14.3 us
  starting transfers between devices: 24.4 us -> 13.2 us
  local copies, waits for them, and re-layouts: 22.9 us -> 15.1 us
    all_to_all x2 -> x1, waiting for transfers between devices: 118 us -> 4.85 us  [body(): lax.all_to_all(outgoing, 'dp', split_axis=0, concat_axis=0, tiled=True)]
    psum x2 -> x0, blocking collectives: 95.5 us -> none  [the longest x1 89.4 us: divergence(): hidden_grad = lax.psum(partial_grad, 'vocab').astype(jnp.bfloat16)]
    reduce_scatter x0 -> x1, waiting for transfers between devices: none -> 57.1 us  [divergence(): lax.psum_scatter(partial_grad, 'vocab', scatter_dimension=0, tiled=True)]
    all_gather x0 -> x2, blocking collectives: none -> 54.8 us  [the longest x1 45.3 us: body(): every_div = lax.all_gather(row_div, 'dp')]
    all_to_all x2 -> x1, starting transfers between devices: 24.4 us -> 13.1 us  [body(): lax.all_to_all(outgoing, 'dp', split_axis=0, concat_axis=0, tiled=True)]
    pmax x1 -> x0, blocking collectives: 8.47 us -> none  [divergence(): row_top = lax.pmax(own_top, 'vocab')]
    reshape x2 -> x0, local copies, waits for them, and re-layouts: 7.28 us -> none  [the longest x1 3.77 us: body(): hidden_rows.reshape(slot_depth, shards, feature_width)]
    select_n x6 -> x5, other arithmetic: 8.85 us -> 2.35 us  [the longest x1 1.32 us: body(): first_slot = (offsets + first_col) // shards]
  transfers between devices with their start and end apart: 2 -> 3, of which waited for: 2 -> 2; matrix products, arithmetic and copies ran while one was open for 2% -> 8% of each run, Pallas kernels for 0% -> 0%
where the time goes in v1:
time: 188 us; the launch traced here: 187 us
  waiting for transfers between devices  62 us (33%)
  blocking collectives  54.8 us (29%)
  local copies, waits for them, and re-layouts  15.1 us (8%)
  between operations  14.3 us (8%)
  matrix products  14.1 us (8%)
  other arithmetic  13.7 us (7%)
  starting transfers between devices  13.2 us (7%)
    reduce_scatter x1, waiting for transfers between devices, divergence(): lax.psum_scatter(partial_grad, 'vocab', scatter_dimension=0, tiled=True)  57.1 us
    all_gather x1, blocking collectives, body(): every_div = lax.all_gather(row_div, 'dp')  45.3 us
    all_to_all x1, starting transfers between devices, body(): lax.all_to_all(outgoing, 'dp', split_axis=0, concat_axis=0, tiled=True)  13.1 us
    all_gather x1, blocking collectives, divergence(): lax.all_gather(jnp.stack([own_top, own_total, own_mass, own_cross]), 'voc...  9.48 us
    dot_general x1, matrix products, divergence(): lax.dot_general(grad_logits, weight, (((1,), (1,)), ((), ())), preferred_...  7.83 us
    dot_general x1, matrix products, divergence(): logits = jnp.dot(row_block, weight, preferred_element_type=jnp.float32)  6.3 us
    all_to_all x1, waiting for transfers between devices, body(): lax.all_to_all(outgoing, 'dp', split_axis=0, concat_axis=0, tiled=True)  4.85 us
  transfers between devices with their start and end apart: 3, of which 2 were waited for; matrix products, arithmetic and copies ran while one was open for 8% of the time, Pallas kernels for 0%

profile of v1, /device:TPU:1, one launch (start us, length us, event | category | flops | bytes accessed | tf_op | source)
XLA Modules:
  0.0 187.2 jit_solution(102889818962397044)
XLA Ops:
  7.2 0.0 copy-start
  7.2 0.0 copy-start.1
  7.2 0.0 copy-start.2
  7.2 0.9 select_reduce_fusion
  8.1 0.8 copy.24
  8.9 0.1 reduce-window.9
  9.0 0.1 reduce.5
  9.1 0.6 dynamic_slice.12
  9.7 1.3 and_select_fusion
  11.0 0.1 copy.25
  11.1 0.1 copy.26
  11.2 0.1 min.22
  11.4 2.4 %gather_fusion.1 = bf16[256,768]{1,0:T(8,128)(2,1)S(1)} fusion(bf16[128,768]{1,0:T(8,128)(2,1)} %param.9, s32[1024]{0:T(1024)S(1)} %pad_clamp_fusion.2), kind=kCustom, calls=%fused_computation.1 | custom fusion | bytes 787456 | tf_op jit(solution)/shard_map/jit(_take)/gather | solution.py:53
  13.7 0.1 gather.25
  13.8 1.0 broadcast_select_fusion.1
  14.8 13.1 %all-to-all-start = ((bf16[64,4,768]{2,1,0:T(4,128)(2,1)}), bf16[64,4,768]{2,1,0:T(4,128)(2,1)S(1)}, u32[]{:S(2)}, u32[]{:S(2)}) async-start(bf16[64,4,768]{2,1,0:T(4,128)(2,1)} %broadcast_select_fusion.1), calls=%async_computation | async-start | bytes 786432 | tf_op jit(solution)/shard_map/all_to_all | solution.py:56
  28.0 0.0 reduce-scatter.2.cloned.1.call-start
  28.0 0.0 copy-done.2
  28.1 0.6 dynamic_slice.10
  28.7 0.6 dynamic_slice.11
  29.2 0.7 fusion.11
  29.9 0.0 copy-done.1
  29.9 0.8 gather_fusion
  30.7 0.6 iota_compare_fusion.1
  31.4 0.0 copy-done
  31.4 6.3 %fusion.19 = (f32[256]{0:T(256)S(1)}, f32[256,768]{1,0:T(8,128)}) fusion(bf16[256,5120]{1,0:T(8,128)(2,1)S(1)} %copy-done, bf16[5120,768]{1,0:T(8,128)(2,1)} %param.8), kind=kOutput, calls=%fused_computation.71 | convolution fusion | flops 2013462272 | bytes 11273216 | tf_op jit(solution)/shard_map/dot_general | solution.py:10
  37.7 4.8 %all-to-all-done = bf16[64,4,768]{2,1,0:T(4,128)(2,1)S(1)} async-done(((bf16[64,4,768]{2,1,0:T(4,128)(2,1)}), bf16[64,4,768]{2,1,0:T(4,128)(2,1)S(1)}, u32[]{:S(2)}, u32[]{:S(2)}) %all-to-all-start) | async-done | bytes 393248 | tf_op jit(solution)/shard_map/all_to_all | solution.py:56
  42.5 0.9 gather_fusion.2
  43.5 0.5 fusion
  43.9 1.1 convert_bitcast_fusion
  45.1 0.1 copy.27
  45.1 0.1 stack.17
  45.2 1.3 copy.28
  46.5 1.5 exponential_reduce_fusion
  48.0 9.5 %all-gather.1 = f32[4,4,256]{2,1,0:T(4,128)S(1)} all-gather(f32[1,4,256]{2,1,0:T(4,128)S(1)} %maximum_bitcast_fusion), channel_id=2, replica_groups=mesh['dp'=64,'vocab'=4] {'vocab'}, dimensions={0}, use_global_device_ids=true | all-gather | bytes 20480 | tf_op jit(solution)/shard_map/all_gather | solution.py:17
  57.6 1.4 select_convert_fusion
  59.1 7.8 %fusion.20 = f32[256,5120]{1,0:T(8,128)} fusion(bf16[256,768]{1,0:T(8,128)(2,1)S(1)} %select_convert_fusion, bf16[5120,768]{1,0:T(8,128)(2,1)} %param.8), kind=kOutput, calls=%fused_computation.72 | convolution fusion | flops 2013265920 | bytes 13500416 | tf_op jit(solution)/shard_map/dot_general | solution.py:30
  66.9 0.0 reduce-scatter.2.cloned.1.call-update
  66.9 0.0 all-gather.5.cloned.1.call-start
  67.0 57.1 %reduce-scatter.2.cloned.1.call-done = f32[64,5120]{1,0:T(8,128)} async-done(((f32[256,5120]{1,0:T(8,128)}), f32[64,5120]{1,0:T(8,128)}) %reduce-scatter.2.cloned.1.call-update) | async-done | bytes 1310736 | tf_op jit(solution)/shard_map/reduce_scatter | solution.py:33
  124.1 2.2 %convert_element_type.27 = bf16[64,5120]{1,0:T(8,128)(2,1)} convert(f32[64,5120]{1,0:T(8,128)} %reduce-scatter.2.cloned.1.call-done) | non-fusion elementwise | flops 327680 | bytes 1966080 | tf_op jit(solution)/shard_map/convert_element_type | solution.py:34
  126.3 0.0 all-gather.5.cloned.1.call-update
  126.3 0.7 multiply_add_fusion.1
  127.0 0.1 convert_reduce_fusion
  127.1 1.2 gather_fusion.3
  128.3 0.7 fusion.16
  129.0 0.6 fusion.7
  129.7 45.3 %all-gather.2 = f32[64,1,256]{2,1,0:T(1,128)S(1)} all-gather(f32[1,1,256]{2,1,0:T(1,128)S(1)} %fusion.7), channel_id=1, replica_groups=mesh['dp'=64,'vocab'=4] {'dp'}, dimensions={0}, use_global_device_ids=true | all-gather | bytes 66560 | tf_op jit(solution)/shard_map/all_gather | solution.py:63
  175.0 2.0 %gather_fusion.4 = f32[128]{0:T(128)} fusion(f32[64,256]{1,0:T(8,128)S(1)} %bitcast.74, s32[128]{0:T(128)S(1)} %fusion.16), kind=kCustom, calls=%fused_computation.4 | custom fusion | bytes 2048 | tf_op jit(solution)/shard_map/gather | solution.py:66
  177.0 0.0 all-gather.5.cloned.1.call-done
  177.0 3.4 %copy.47 = bf16[256,5120]{1,0:T(8,128)(2,1)} copy(bf16[256,5120]{1,0:T(8,128)(2,1)} %all-gather.5.cloned.1.call-done) | data formatting | bytes 5242880
  (15 shorter events, 0.2 us)
Async XLA Ops:
  7.2 24.2 %copy-start = (bf16[256,5120]{1,0:T(8,128)(2,1)S(1)}, bf16[256,5120]{1,0:T(8,128)(2,1)}, u32[]{:S(2)}) copy-start(bf16[256,5120]{1,0:T(8,128)(2,1)} %param.5) | copy-start | bytes 7864324
  7.2 22.7 %copy-start.1 = (s32[64]{0:T(128)S(1)}, s32[64]{0:T(128)}, u32[]{:S(2)}) copy-start(s32[64]{0:T(128)} %param.7) | copy-start | bytes 772
  7.2 20.9 %copy-start.2 = (s32[64]{0:T(128)S(1)}, s32[64]{0:T(128)}, u32[]{:S(2)}) copy-start(s32[64]{0:T(128)} %param.6) | copy-start | bytes 772
  14.8 27.7 %all-to-all-start = ((bf16[64,4,768]{2,1,0:T(4,128)(2,1)}), bf16[64,4,768]{2,1,0:T(4,128)(2,1)S(1)}, u32[]{:S(2)}, u32[]{:S(2)}) async-start(bf16[64,4,768]{2,1,0:T(4,128)(2,1)} %broadcast_select_fusion.1), calls=%async_computation | async-start | bytes 786432 | tf_op jit(solution)/shard_map/all_to_all | solution.py:56
  28.0 96.1 %reduce-scatter.2.cloned.1.call-start = ((), (), s32[]{:S(2)}) async-start(), calls=%async_computation.2 | async-start | bytes 6553600 | tf_op jit(solution)/shard_map/reduce_scatter | solution.py:33
  66.9 110.1 %all-gather.5.cloned.1.call-start = ((), (), s32[]{:S(2)}) async-start(), calls=%async_computation.3 | async-start | bytes 3276800 | tf_op jit(solution)/shard_map/all_gather | solution.py:34
Sparse Core Ops, SparseCore 0:
  67.0 57.0 reduce-scatter.1
  126.5 37.3 all-gather.4

commit v2 on v1

--- a/solution.py
+++ b/solution.py
@@ -60,10 +60,12 @@
     teacher_slots = jnp.transpose(teacher_slots, (1, 0, 2)).reshape(source_slots, -1)
     live = jnp.arange(source_slots, dtype=jnp.int32) < plan_lengths[myself]
     row_grad, row_div = divergence(hidden_rows, teacher_slots, live, head_weight)
-    every_div = lax.all_gather(row_div, "dp")
+    column_of = (inverse - own_offset) % shards
+    div_out = jnp.take(row_div.reshape(slot_depth, shards), column_of, axis=1).T
+    div_in = lax.all_to_all(div_out, "dp", split_axis=0, concat_axis=0, tiled=True)
     packed = jnp.arange(balanced, dtype=jnp.int32) * shards + inverse[myself]
     owner = jnp.sum((offsets[None, :] <= packed[:, None]).astype(jnp.int32), axis=1) - 1
-    row_kl = every_div[owner, packed - offsets[owner]]
+    row_kl = div_in[owner, (packed - offsets[owner]) // shards]
     return row_grad, row_kl
 
 

time: 188 us -> 175 us (0.931)
  blocking collectives: 54.8 us -> 9.48 us
  waiting for transfers between devices: 62 us -> 81.5 us
  starting transfers between devices: 13.2 us -> 24 us
    all_gather x1 -> x0, blocking collectives: 45.3 us -> none  [body(): every_div = lax.all_gather(row_div, 'dp')]
    all_gather x1, waiting for transfers between devices: 0.01 us -> 10.9 us  [divergence(): lax.all_gather(summed.astype(jnp.bfloat16), 'vocab', axis=0, tiled=True)]
    all_to_all x0 -> x1, starting transfers between devices: none -> 10.8 us  [body(): lax.all_to_all(div_out, 'dp', split_axis=0, concat_axis=0, tiled=True)]
    all_to_all x0 -> x1, waiting for transfers between devices: none -> 8.64 us  [body(): lax.all_to_all(div_out, 'dp', split_axis=0, concat_axis=0, tiled=True)]
  transfers between devices with their start and end apart: 3 -> 4, of which waited for: 2 -> 4; matrix products, arithmetic and copies ran while one was open for 8% -> 10% of each run, Pallas kernels for 0% -> 0%
where the time goes in v2:
time: 175 us; the launch traced here: 174 us
  waiting for transfers between devices  81.5 us (47%)
  starting transfers between devices  24 us (14%)
  local copies, waits for them, and re-layouts  15.7 us (9%)
  other arithmetic  15 us (9%)
  between operations  14.3 us (8%)
  matrix products  14.1 us (8%)
  blocking collectives  9.48 us (5%)
    reduce_scatter x1, waiting for transfers between devices, divergence(): lax.psum_scatter(partial_grad, 'vocab', scatter_dimension=0, tiled=True)  57.1 us
    all_to_all x1, starting transfers between devices, body(): lax.all_to_all(outgoing, 'dp', split_axis=0, concat_axis=0, tiled=True)  13.1 us
    all_gather x1, waiting for transfers between devices, divergence(): lax.all_gather(summed.astype(jnp.bfloat16), 'vocab', axis=0, tiled=True)  10.9 us
    all_to_all x1, starting transfers between devices, body(): lax.all_to_all(div_out, 'dp', split_axis=0, concat_axis=0, tiled=True)  10.8 us
    all_gather x1, blocking collectives, divergence(): lax.all_gather(jnp.stack([own_top, own_total, own_mass, own_cross]), 'voc...  9.48 us
    all_to_all x1, waiting for transfers between devices, body(): lax.all_to_all(div_out, 'dp', split_axis=0, concat_axis=0, tiled=True)  8.64 us
    dot_general x1, matrix products, divergence(): lax.dot_general(grad_logits, weight, (((1,), (1,)), ((), ())), preferred_...  7.83 us
    dot_general x1, matrix products, divergence(): logits = jnp.dot(row_block, weight, preferred_element_type=jnp.float32)  6.3 us
  transfers between devices with their start and end apart: 4, of which 4 were waited for; matrix products, arithmetic and copies ran while one was open for 10% of the time, Pallas kernels for 0%

profile of v2, /device:TPU:1, one launch (start us, length us, event | category | flops | bytes accessed | tf_op | source)
XLA Modules:
  0.0 174.1 jit_solution(5403673574187742416)
XLA Ops:
  7.2 0.0 copy-start
  7.2 0.0 copy-start.1
  7.2 0.0 copy-start.2
  7.2 0.9 select_reduce_fusion
  8.1 0.8 copy.31
  8.9 0.1 reduce-window.9
  9.0 0.1 reduce.5
  9.1 0.6 dynamic_slice.12
  9.7 1.3 and_select_fusion.3
  11.0 0.1 copy.32
  11.1 0.1 copy.33
  11.2 0.1 min.22
  11.4 2.4 %gather_fusion.1 = bf16[256,768]{1,0:T(8,128)(2,1)S(1)} fusion(bf16[128,768]{1,0:T(8,128)(2,1)} %param.9, s32[1024]{0:T(1024)S(1)} %pad_clamp_fusion.3), kind=kCustom, calls=%fused_computation.1 | custom fusion | bytes 787456 | tf_op jit(solution)/shard_map/jit(_take)/gather | solution.py:53
  13.7 0.1 gather.29
  13.8 1.0 broadcast_select_fusion.1
  14.8 13.1 %all-to-all-start = ((bf16[64,4,768]{2,1,0:T(4,128)(2,1)}), bf16[64,4,768]{2,1,0:T(4,128)(2,1)S(1)}, u32[]{:S(2)}, u32[]{:S(2)}) async-start(bf16[64,4,768]{2,1,0:T(4,128)(2,1)} %broadcast_select_fusion.1), calls=%async_computation | async-start | bytes 786432 | tf_op jit(solution)/shard_map/all_to_all | solution.py:56
  28.0 0.0 reduce-scatter.2.cloned.1.call-start
  28.0 0.0 copy-done.2
  28.1 0.6 dynamic_slice.10
  28.7 0.6 dynamic_slice.11
  29.3 0.6 fusion.13
  30.0 0.0 copy-done.1
  30.0 0.8 gather_fusion
  30.8 0.6 iota_compare_fusion.1
  31.4 0.0 copy-done
  31.4 6.3 %fusion.22 = (f32[256]{0:T(256)S(1)}, f32[256,768]{1,0:T(8,128)}) fusion(bf16[256,5120]{1,0:T(8,128)(2,1)S(1)} %copy-done, bf16[5120,768]{1,0:T(8,128)(2,1)} %param.8), kind=kOutput, calls=%fused_computation.89 | convolution fusion | flops 2013462272 | bytes 11273216 | tf_op jit(solution)/shard_map/dot_general | solution.py:10
  37.7 4.8 %all-to-all-done = bf16[64,4,768]{2,1,0:T(4,128)(2,1)S(1)} async-done(((bf16[64,4,768]{2,1,0:T(4,128)(2,1)}), bf16[64,4,768]{2,1,0:T(4,128)(2,1)S(1)}, u32[]{:S(2)}, u32[]{:S(2)}) %all-to-all-start) | async-done | bytes 393248 | tf_op jit(solution)/shard_map/all_to_all | solution.py:56
  42.5 0.9 gather_fusion.2
  43.5 0.5 fusion
  43.9 1.1 convert_bitcast_fusion
  45.1 0.1 copy.34
  45.1 0.1 stack.17
  45.2 1.3 copy.35
  46.5 1.5 exponential_reduce_fusion
  48.0 9.5 %all-gather.1 = f32[4,4,256]{2,1,0:T(4,128)S(1)} all-gather(f32[1,4,256]{2,1,0:T(4,128)S(1)} %maximum_bitcast_fusion), channel_id=2, replica_groups=mesh['dp'=64,'vocab'=4] {'vocab'}, dimensions={0}, use_global_device_ids=true | all-gather | bytes 20480 | tf_op jit(solution)/shard_map/all_gather | solution.py:17
  57.6 1.4 select_convert_fusion
  59.1 7.8 %fusion.23 = f32[256,5120]{1,0:T(8,128)} fusion(bf16[256,768]{1,0:T(8,128)(2,1)S(1)} %select_convert_fusion, bf16[5120,768]{1,0:T(8,128)(2,1)} %param.8), kind=kOutput, calls=%fused_computation.90 | convolution fusion | flops 2013265920 | bytes 13500416 | tf_op jit(solution)/shard_map/dot_general | solution.py:30
  66.9 0.0 reduce-scatter.2.cloned.1.call-update
  66.9 0.0 all-gather.4.cloned.1.call-start
  67.0 57.1 %reduce-scatter.2.cloned.1.call-done = f32[64,5120]{1,0:T(8,128)} async-done(((f32[256,5120]{1,0:T(8,128)}), f32[64,5120]{1,0:T(8,128)}) %reduce-scatter.2.cloned.1.call-update) | async-done | bytes 1310736 | tf_op jit(solution)/shard_map/reduce_scatter | solution.py:33
  124.1 2.2 %convert_element_type.27 = bf16[64,5120]{1,0:T(8,128)(2,1)} convert(f32[64,5120]{1,0:T(8,128)} %reduce-scatter.2.cloned.1.call-done) | non-fusion elementwise | flops 327680 | bytes 1966080 | tf_op jit(solution)/shard_map/convert_element_type | solution.py:34
  126.3 0.0 all-gather.4.cloned.1.call-update
  126.3 0.7 multiply_add_fusion.1
  127.0 0.1 convert_reduce_fusion
  127.1 1.2 gather_fusion.4
  128.4 0.6 compare_and_fusion
  129.0 0.1 add.262
  129.1 0.1 copy.37
  129.2 0.6 fusion.3
  129.8 0.6 gather_fusion.3
  130.4 0.7 broadcast_select_fusion.2
  131.1 10.8 %all-to-all-start.1 = ((f32[64,1,4]{2,1,0:T(1,128)}), f32[64,1,4]{2,1,0:T(1,128)S(1)}, u32[]{:S(2)}, u32[]{:S(2)}) async-start(f32[64,1,4]{2,1,0:T(1,128)} %bitcast.19), calls=%async_computation.2 | async-start | bytes 65536 | tf_op jit(solution)/shard_map/all_to_all | solution.py:65
  141.9 0.7 fusion.19
  142.5 8.6 %all-to-all-done.1 = f32[64,1,4]{2,1,0:T(1,128)S(1)} async-done(((f32[64,1,4]{2,1,0:T(1,128)}), f32[64,1,4]{2,1,0:T(1,128)S(1)}, u32[]{:S(2)}, u32[]{:S(2)}) %all-to-all-start.1) | async-done | bytes 1056 | tf_op jit(solution)/shard_map/all_to_all | solution.py:65
  151.2 1.8 %gather_fusion.5 = f32[128]{0:T(128)} fusion(f32[64,4]{1,0:T(8,128)S(1)} %bitcast.76, s32[128]{0:T(128)S(1)} %fusion.19), kind=kCustom, calls=%fused_computation.5 | custom fusion | bytes 2048 | tf_op jit(solution)/shard_map/gather | solution.py:68
  153.0 10.9 %all-gather.4.cloned.1.call-done = bf16[256,5120]{1,0:T(8,128)(2,1)} async-done(((bf16[64,5120]{1,0:T(8,128)(2,1)}), bf16[256,5120]{1,0:T(8,128)(2,1)}) %all-gather.4.cloned.1.call-update) | async-done | bytes 2621456 | tf_op jit(solution)/shard_map/all_gather | solution.py:34
  163.8 3.4 %copy.53 = bf16[256,5120]{1,0:T(8,128)(2,1)} copy(bf16[256,5120]{1,0:T(8,128)(2,1)} %all-gather.4.cloned.1.call-done) | data formatting | bytes 5242880
  (15 shorter events, 0.2 us)
Async XLA Ops:
  7.2 24.3 %copy-start = (bf16[256,5120]{1,0:T(8,128)(2,1)S(1)}, bf16[256,5120]{1,0:T(8,128)(2,1)}, u32[]{:S(2)}) copy-start(bf16[256,5120]{1,0:T(8,128)(2,1)} %param.5) | copy-start | bytes 7864324
  7.2 22.8 %copy-start.1 = (s32[64]{0:T(128)S(1)}, s32[64]{0:T(128)}, u32[]{:S(2)}) copy-start(s32[64]{0:T(128)} %param.7) | copy-start | bytes 772
  7.2 20.9 %copy-start.2 = (s32[64]{0:T(128)S(1)}, s32[64]{0:T(128)}, u32[]{:S(2)}) copy-start(s32[64]{0:T(128)} %param.6) | copy-start | bytes 772
  14.8 27.7 %all-to-all-start = ((bf16[64,4,768]{2,1,0:T(4,128)(2,1)}), bf16[64,4,768]{2,1,0:T(4,128)(2,1)S(1)}, u32[]{:S(2)}, u32[]{:S(2)}) async-start(bf16[64,4,768]{2,1,0:T(4,128)(2,1)} %broadcast_select_fusion.1), calls=%async_computation | async-start | bytes 786432 | tf_op jit(solution)/shard_map/all_to_all | solution.py:56
  28.0 96.1 %reduce-scatter.2.cloned.1.call-start = ((), (), s32[]{:S(2)}) async-start(), calls=%async_computation.3 | async-start | bytes 6553600 | tf_op jit(solution)/shard_map/reduce_scatter | solution.py:33
  66.9 96.9 %all-gather.4.cloned.1.call-start = ((), (), s32[]{:S(2)}) async-start(), calls=%async_computation.4 | async-start | bytes 3276800 | tf_op jit(solution)/shard_map/all_gather | solution.py:34
  131.1 20.1 %all-to-all-start.1 = ((f32[64,1,4]{2,1,0:T(1,128)}), f32[64,1,4]{2,1,0:T(1,128)S(1)}, u32[]{:S(2)}, u32[]{:S(2)}) async-start(f32[64,1,4]{2,1,0:T(1,128)} %bitcast.19), calls=%async_computation.2 | async-start | bytes 65536 | tf_op jit(solution)/shard_map/all_to_all | solution.py:65
Sparse Core Ops, SparseCore 0:
  67.0 57.0 reduce-scatter.1
  126.5 37.3 all-gather.3

commit v3 on v2

--- a/solution.py
+++ b/solution.py
@@ -30,9 +30,41 @@
     partial_grad = lax.dot_general(
         grad_logits, weight, (((1,), (1,)), ((), ())), preferred_element_type=jnp.float32
     )
-    summed = lax.psum_scatter(partial_grad, "vocab", scatter_dimension=0, tiled=True)
-    hidden_grad = lax.all_gather(summed.astype(jnp.bfloat16), "vocab", axis=0, tiled=True)
+    hidden_grad = ring_all_reduce(partial_grad)
     return hidden_grad, row_div
+
+
+def ring_all_reduce(partial):
+    ring = lax.axis_size("vocab")
+    me = lax.axis_index("vocab")
+    rows, width = partial.shape
+    chunk = rows // (2 * ring)
+    halves = partial.reshape(2, ring, chunk, width)
+    forward = [(i, (i + 1) % ring) for i in range(ring)]
+    backward = [(i, (i - 1) % ring) for i in range(ring)]
+
+    def own(half, index):
+        return lax.dynamic_index_in_dim(halves[half], index % ring, 0, keepdims=False)
+
+    up = own(0, me - 1)
+    down = own(1, me + 1)
+    for step in range(ring - 1):
+        up = lax.ppermute(up, "vocab", forward) + own(0, me - step - 2)
+        down = lax.ppermute(down, "vocab", backward) + own(1, me + step + 2)
+    up = up.astype(jnp.bfloat16)
+    down = down.astype(jnp.bfloat16)
+    ups, downs = [up], [down]
+    for step in range(ring - 1):
+        up = lax.ppermute(up, "vocab", forward)
+        down = lax.ppermute(down, "vocab", backward)
+        ups.append(up)
+        downs.append(down)
+    ups = jnp.stack(ups)
+    downs = jnp.stack(downs)
+    order = jnp.arange(ring, dtype=jnp.int32)
+    top = jnp.take(ups, (me - order) % ring, axis=0)
+    bottom = jnp.take(downs, (order - me) % ring, axis=0)
+    return jnp.concatenate([top, bottom], axis=0).reshape(rows, width)
 
 
 def body(hidden_rows, plan_lengths, shard_of_class, head_weight, teacher_logprobs):

time: 175 us -> 166 us (0.949)
  waiting for transfers between devices: 81.5 us -> 53.9 us
  starting transfers between devices: 24 us -> 50.5 us
  between operations: 14.3 us -> 1.14 us
  other arithmetic: 15 us -> 22.3 us
  matrix products: 14.1 us -> 11.8 us
    reduce_scatter x1 -> x0, waiting for transfers between devices: 57.1 us -> none  [divergence(): lax.psum_scatter(partial_grad, 'vocab', scatter_dimension=0, tiled=True)]
    ppermute x0 -> x12, waiting for transfers between devices: none -> 43.3 us  [the longest x3 31.9 us: ring_all_reduce(): up = lax.ppermute(up, 'vocab', forward) + own(0, me - step - 2)]
    ppermute x0 -> x12, starting transfers between devices: none -> 17.2 us  [the longest x3 8.44 us: ring_all_reduce(): down = lax.ppermute(down, 'vocab', backward)]
    all_gather x1 -> x0, waiting for transfers between devices: 10.9 us -> none  [divergence(): lax.all_gather(summed.astype(jnp.bfloat16), 'vocab', axis=0, tiled=True)]
    all_to_all x1, starting transfers between devices: 10.8 us -> 20.2 us  [body(): lax.all_to_all(div_out, 'dp', split_axis=0, concat_axis=0, tiled=True)]
    gather x0 -> x2, local copies, waits for them, and re-layouts: none -> 6.03 us  [the longest x1 3.03 us: ring_all_reduce(): top = jnp.take(ups, (me - order) % ring, axis=0)]
    another operation x2 -> x4, other arithmetic: 0.2 us -> 4.98 us  [the longest x1 2.39 us: ring_all_reduce(): ups = jnp.stack(ups)]
    select_n x0 -> x4, other arithmetic: none -> 4.22 us  [the longest x2 2.6 us: ring_all_reduce(): top = jnp.take(ups, (me - order) % ring, axis=0)]
  transfers between devices with their start and end apart: 4 -> 14, of which waited for: 4 -> 7; matrix products, arithmetic and copies ran while one was open for 10% -> 15% of each run, Pallas kernels for 0% -> 0%
where the time goes in v3:
time: 166 us
  waiting for transfers between devices  53.9 us (32%)
  starting transfers between devices  50.5 us (30%)
  other arithmetic  22.3 us (13%)
  local copies, waits for them, and re-layouts  16.8 us (10%)
  matrix products  11.8 us (7%)
  blocking collectives  9.48 us (6%)
    ppermute x3, waiting for transfers between devices, ring_all_reduce(): up = lax.ppermute(up, 'vocab', forward) + own(0, me - step - 2)  31.9 us
    all_to_all x1, starting transfers between devices, body(): lax.all_to_all(div_out, 'dp', split_axis=0, concat_axis=0, tiled=True)  20.2 us
    all_to_all x1, starting transfers between devices, body(): lax.all_to_all(outgoing, 'dp', split_axis=0, concat_axis=0, tiled=True)  13.1 us
    ppermute x3, waiting for transfers between devices, ring_all_reduce(): up = lax.ppermute(up, 'vocab', forward)  11.4 us
    all_gather x1, blocking collectives, divergence(): lax.all_gather(jnp.stack([own_top, own_total, own_mass, own_cross]), 'voc...  9.48 us
    all_to_all x1, waiting for transfers between devices, body(): lax.all_to_all(div_out, 'dp', split_axis=0, concat_axis=0, tiled=True)  9.22 us
    ppermute x3, starting transfers between devices, ring_all_reduce(): down = lax.ppermute(down, 'vocab', backward)  8.44 us
    ppermute x3, starting transfers between devices, ring_all_reduce(): down = lax.ppermute(down, 'vocab', backward) + own(1, me + step + 2)  7.47 us
  transfers between devices with their start and end apart: 14, of which 7 were waited for; matrix products, arithmetic and copies ran while one was open for 15% of the time, Pallas kernels for 0%

profile of v3, /device:TPU:1, one launch (start us, length us, event | category | flops | bytes accessed | tf_op | source)
XLA Modules:
  0.0 165.9 jit_solution(7881175184200116560)
XLA Ops:
  0.7 0.9 select_reduce_fusion
  1.6 0.8 copy.31
  2.4 0.1 reduce-window.9
  2.5 0.1 reduce.5
  2.6 0.6 dynamic_slice.37
  3.2 1.3 and_select_fusion.5
  4.5 0.1 copy.33
  4.6 0.1 min.22
  4.7 1.2 gather_fusion.1
  6.0 0.1 gather.32
  6.1 0.1 copy.32
  6.2 1.0 broadcast_select_fusion.3
  7.2 13.1 %all-to-all-start = ((bf16[64,4,768]{2,1,0:T(4,128)(2,1)}), bf16[64,4,768]{2,1,0:T(4,128)(2,1)S(1)}, u32[]{:S(2)}, u32[]{:S(2)}) async-start(bf16[64,4,768]{2,1,0:T(4,128)(2,1)} %broadcast_select_fusion.3), calls=%async_computation | async-start | bytes 786432 | tf_op jit(solution)/shard_map/all_to_all | solution.py:88
  20.3 0.6 dynamic_slice.36
  20.9 0.7 fusion.17
  21.6 0.8 gather_fusion
  22.4 0.7 dynamic_slice.35
  23.1 0.7 compare_and_fusion.2
  23.8 0.7 multiply_add_fusion.1
  24.6 1.2 gather_fusion.4
  25.8 0.7 fusion.23
  26.5 0.6 iota_compare_fusion.1
  27.2 6.3 %fusion.27 = (f32[256]{0:T(256)S(1)}, f32[256,768]{1,0:T(8,128)}) fusion(bf16[256,5120]{1,0:T(8,128)(2,1)S(1)} %copy-done, bf16[5120,768]{1,0:T(8,128)(2,1)} %param.10), kind=kOutput, calls=%fused_computation.121 | convolution fusion | flops 2013462272 | bytes 11273216 | tf_op jit(solution)/shard_map/dot_general | solution.py:10
  33.5 1.3 all-to-all-done
  34.9 0.9 gather_fusion.2
  35.8 0.2 convert_bitcast_fusion
  36.1 0.5 fusion
  36.5 0.2 copy.35
  36.8 1.6 exponential_reduce_fusion
  38.5 9.5 %all-gather.1 = f32[4,4,256]{2,1,0:T(4,128)S(1)} all-gather(f32[1,4,256]{2,1,0:T(4,128)S(1)} %maximum_bitcast_fusion), channel_id=2, replica_groups=mesh['dp'=64,'vocab'=4] {'vocab'}, dimensions={0}, use_global_device_ids=true | all-gather | bytes 20480 | tf_op jit(solution)/shard_map/all_gather | solution.py:17
  48.0 0.3 select_convert_fusion
  48.4 5.5 %fusion.28 = f32[256,5120]{1,0:T(8,128)S(1)} fusion(bf16[256,768]{1,0:T(8,128)(2,1)S(1)} %select_convert_fusion, bf16[5120,768]{1,0:T(8,128)(2,1)} %param.10), kind=kOutput, calls=%fused_computation.122 | convolution fusion | flops 2013265920 | bytes 13500416 | tf_op jit(solution)/shard_map/dot_general | solution.py:30
  53.9 0.5 fusion.25
  54.5 1.0 collective-permute-start
  55.5 1.8 %collective-permute-start.6 = (f32[32,5120]{1,0:T(8,128)S(1)}, f32[32,5120]{1,0:T(8,128)S(1)}, u32[]{:S(2)}, u32[]{:S(2)}) collective-permute-start(f32[32,5120]{1,0:T(8,128)S(1)} %dynamic-slice_bitcast_fusion), channel_id=1, source_target_pairs={{0,3},{1,0},{2,1},{3,2},{4,7},{5,4},{6,5},{7,6},{8,11},{9,8},{10,9... | collective-permute-start | bytes 1966088 | tf_op jit(solution)/shard_map/ppermute | solution.py:53
  57.4 11.4 %collective-permute-done = f32[32,5120]{1,0:T(8,128)S(1)} collective-permute-done((f32[32,5120]{1,0:T(8,128)S(1)}, f32[32,5120]{1,0:T(8,128)S(1)}, u32[]{:S(2)}, u32[]{:S(2)}) %collective-permute-start) | collective-permute-done | bytes 655392 | tf_op jit(solution)/shard_map/ppermute | solution.py:52
  68.8 0.1 bitcast_add_fusion.5
  69.0 0.1 bitcast_add_fusion.2
  69.1 2.9 %collective-permute-start.7 = (f32[32,5120]{1,0:T(8,128)S(1)}, f32[32,5120]{1,0:T(8,128)S(1)}, u32[]{:S(2)}, u32[]{:S(2)}) collective-permute-start(f32[32,5120]{1,0:T(8,128)S(1)} %bitcast_add_fusion.2), channel_id=1, source_target_pairs={{0,3},{1,0},{2,1},{3,2},{4,7},{5,4},{6,5},{7,6},{8,11},{9,8},{10,9... | collective-permute-start | bytes 1966088 | tf_op jit(solution)/shard_map/ppermute | solution.py:53
  72.0 10.3 %collective-permute-done.1 = f32[32,5120]{1,0:T(8,128)S(1)} collective-permute-done((f32[32,5120]{1,0:T(8,128)S(1)}, f32[32,5120]{1,0:T(8,128)S(1)}, u32[]{:S(2)}, u32[]{:S(2)}) %collective-permute-start.1) | collective-permute-done | bytes 655392 | tf_op jit(solution)/shard_map/ppermute | solution.py:52
  82.3 0.1 bitcast_add_fusion.4
  82.5 0.1 bitcast_add_fusion.1
  82.6 2.7 %collective-permute-start.8 = (f32[32,5120]{1,0:T(8,128)S(1)}, f32[32,5120]{1,0:T(8,128)S(1)}, u32[]{:S(2)}, u32[]{:S(2)}) collective-permute-start(f32[32,5120]{1,0:T(8,128)S(1)} %bitcast_add_fusion.1), channel_id=1, source_target_pairs={{0,3},{1,0},{2,1},{3,2},{4,7},{5,4},{6,5},{7,6},{8,11},{9,8},{10,9... | collective-permute-start | bytes 1966088 | tf_op jit(solution)/shard_map/ppermute | solution.py:53
  85.3 10.2 %collective-permute-done.2 = f32[32,5120]{1,0:T(8,128)S(1)} collective-permute-done((f32[32,5120]{1,0:T(8,128)S(1)}, f32[32,5120]{1,0:T(8,128)S(1)}, u32[]{:S(2)}, u32[]{:S(2)}) %collective-permute-start.2) | collective-permute-done | bytes 655392 | tf_op jit(solution)/shard_map/ppermute | solution.py:52
  95.8 2.7 %collective-permute-start.9 = (bf16[32,5120]{1,0:T(8,128)(2,1)S(1)}, bf16[32,5120]{1,0:T(8,128)(2,1)}, u32[]{:S(2)}, u32[]{:S(2)}) collective-permute-start(bf16[32,5120]{1,0:T(8,128)(2,1)S(1)} %fusion.3), channel_id=1, source_target_pairs={{0,3},{1,0},{2,1},{3,2},{4,7},{5,4},{6,5},{7,6},{8,11},{9,8},{10,9... | collective-permute-start | bytes 983048 | tf_op jit(solution)/shard_map/ppermute | solution.py:59
  98.5 5.8 %collective-permute-done.3 = bf16[32,5120]{1,0:T(8,128)(2,1)} collective-permute-done((bf16[32,5120]{1,0:T(8,128)(2,1)S(1)}, bf16[32,5120]{1,0:T(8,128)(2,1)}, u32[]{:S(2)}, u32[]{:S(2)}) %collective-permute-start.3) | collective-permute-done | bytes 327712 | tf_op jit(solution)/shard_map/ppermute | solution.py:58
  104.4 0.1 copy.37
  104.5 0.6 fusion.5
  105.1 0.6 gather_fusion.3
  105.7 2.7 %collective-permute-start.10 = (bf16[32,5120]{1,0:T(8,128)(2,1)}, bf16[32,5120]{1,0:T(8,128)(2,1)}, u32[]{:S(2)}, u32[]{:S(2)}) collective-permute-start(bf16[32,5120]{1,0:T(8,128)(2,1)} %collective-permute-done.9), channel_id=1, source_target_pairs={{0,3},{1,0},{2,1},{3,2},{4,7},{5,4},{6,5},{7,6},{8,11},{9,8},{10,9... | collective-permute-start | bytes 983048 | tf_op jit(solution)/shard_map/ppermute | solution.py:59
  108.5 5.6 %collective-permute-done.4 = bf16[32,5120]{1,0:T(8,128)(2,1)} collective-permute-done((bf16[32,5120]{1,0:T(8,128)(2,1)}, bf16[32,5120]{1,0:T(8,128)(2,1)}, u32[]{:S(2)}, u32[]{:S(2)}) %collective-permute-start.4) | collective-permute-done | bytes 327712 | tf_op jit(solution)/shard_map/ppermute | solution.py:58
  114.1 0.7 broadcast_select_fusion.4
  114.8 20.2 %all-to-all-start.1 = ((f32[64,1,4]{2,1,0:T(1,128)}), f32[64,1,4]{2,1,0:T(1,128)S(1)}, u32[]{:S(2)}, u32[]{:S(2)}) async-start(f32[64,1,4]{2,1,0:T(1,128)} %bitcast.38), calls=%async_computation.1 | async-start | bytes 65536 | tf_op jit(solution)/shard_map/all_to_all | solution.py:97
  135.1 9.2 %all-to-all-done.1 = f32[64,1,4]{2,1,0:T(1,128)S(1)} async-done(((f32[64,1,4]{2,1,0:T(1,128)}), f32[64,1,4]{2,1,0:T(1,128)S(1)}, u32[]{:S(2)}, u32[]{:S(2)}) %all-to-all-start.1) | async-done | bytes 1056 | tf_op jit(solution)/shard_map/all_to_all | solution.py:97
  144.3 1.8 %gather_fusion.5 = f32[128]{0:T(128)} fusion(f32[64,4]{1,0:T(8,128)S(1)} %bitcast.115, s32[128]{0:T(128)S(1)} %fusion.23), kind=kCustom, calls=%fused_computation.7 | custom fusion | bytes 2048 | tf_op jit(solution)/shard_map/gather | solution.py:100
  146.1 3.0 %collective-permute-start.11 = (bf16[32,5120]{1,0:T(8,128)(2,1)}, bf16[32,5120]{1,0:T(8,128)(2,1)}, u32[]{:S(2)}, u32[]{:S(2)}) collective-permute-start(bf16[32,5120]{1,0:T(8,128)(2,1)} %collective-permute-done.10), channel_id=1, source_target_pairs={{0,3},{1,0},{2,1},{3,2},{4,7},{5,4},{6,5},{7,6},{8,11},{9,8},{10,9... | collective-permute-start | bytes 983048 | tf_op jit(solution)/shard_map/ppermute | solution.py:59
  149.1 2.4 %pad_maximum_fusion.1 = bf16[4,32,5120]{2,1,0:T(8,128)(2,1)} fusion(bf16[1,32,5120]{2,1,0:T(8,128)(2,1)} %bitcast.24, bf16[1,32,5120]{2,1,0:T(8,128)(2,1)} %bitcast.23, bf16[1,32,5120]{2,1,0:T(8,128)(2,1)} %bitcast.22, bf16[1,32,5120]{2,1,0:T(8,128)(2,1)S(1)} %bitcast.118), kind=kLoop, calls=%fused_computation.9 | loop fusion | flops 1966080 | bytes 2621440 | tf_op jit(solution)/shard_map/stack | solution.py:62
  151.4 3.0 %gather_fusion.6 = bf16[4,32,5120]{2,1,0:T(8,128)(2,1)} fusion(bf16[4,32,5120]{2,1,0:T(8,128)(2,1)} %pad_maximum_fusion.1, s32[1024]{0:T(1024)S(1)} %pad_clamp_fusion.3), kind=kCustom, calls=%fused_computation.clone | custom fusion | bytes 2621456 | tf_op jit(solution)/shard_map/jit(_take)/gather | solution.py:65
  154.5 2.6 %broadcast_select_fusion.1 = bf16[4,32,5120]{2,1,0:T(8,128)(2,1)} fusion(bf16[4,32,5120]{2,1,0:T(8,128)(2,1)} %gather_fusion.6, pred[4]{0:T(512)(128)(4,1)S(1)} %get-tuple-element.22), kind=kLoop, calls=%fused_computation.12 | loop fusion | flops 655360 | bytes 2621444 | tf_op jit(solution)/shard_map/jit(_take)/select_n | solution.py:65
  157.1 2.4 %pad_maximum_fusion.2 = bf16[4,32,5120]{2,1,0:T(8,128)(2,1)} fusion(bf16[1,32,5120]{2,1,0:T(8,128)(2,1)} %bitcast.33, bf16[1,32,5120]{2,1,0:T(8,128)(2,1)} %bitcast.32, bf16[1,32,5120]{2,1,0:T(8,128)(2,1)} %bitcast.31, bf16[1,32,5120]{2,1,0:T(8,128)(2,1)S(1)} %bitcast.117), kind=kLoop, calls=%fused_computation.10 | loop fusion | flops 1966080 | bytes 2621440 | tf_op jit(solution)/shard_map/stack | solution.py:63
  159.4 3.0 %gather_fusion.7 = bf16[4,32,5120]{2,1,0:T(8,128)(2,1)} fusion(bf16[4,32,5120]{2,1,0:T(8,128)(2,1)} %pad_maximum_fusion.2, s32[1024]{0:T(1024)S(1)} %pad_clamp_fusion.2), kind=kCustom, calls=%fused_computation.1.clone | custom fusion | bytes 2621456 | tf_op jit(solution)/shard_map/jit(_take)/gather | solution.py:66
  162.5 1.6 broadcast_select_fusion
  164.1 0.1 copy-done.3
  164.2 1.7 %pad_maximum_fusion = bf16[8,32,5120]{2,1,0:T(8,128)(2,1)} fusion(bf16[4,32,5120]{2,1,0:T(8,128)(2,1)S(1)} %broadcast_select_fusion, bf16[4,32,5120]{2,1,0:T(8,128)(2,1)S(1)} %copy-done.3), kind=kLoop, calls=%fused_computation.8 | loop fusion | flops 1310720 | bytes 5242880 | tf_op jit(solution)/shard_map/concatenate | solution.py:67
  (51 shorter events, 1.1 us)
Async XLA Ops:
  0.6 26.6 %copy-start = (bf16[256,5120]{1,0:T(8,128)(2,1)S(1)}, bf16[256,5120]{1,0:T(8,128)(2,1)}, u32[]{:S(2)}) copy-start(bf16[256,5120]{1,0:T(8,128)(2,1)} %param.7) | copy-start | bytes 7864324
  0.6 4.1 %copy-start.2 = (bf16[128,768]{1,0:T(8,128)(2,1)S(1)}, bf16[128,768]{1,0:T(8,128)(2,1)}, u32[]{:S(2)}) copy-start(bf16[128,768]{1,0:T(8,128)(2,1)} %param.11) | copy-start | bytes 589828
  5.9 15.7 %copy-start.1 = (s32[64]{0:T(128)S(1)}, s32[64]{0:T(128)}, u32[]{:S(2)}) copy-start(s32[64]{0:T(128)} %param.9) | copy-start | bytes 772
  5.9 16.5 %copy-start.5 = (s32[64]{0:T(128)S(1)}, s32[64]{0:T(128)}, u32[]{:S(2)}) copy-start(s32[64]{0:T(128)} %param.8) | copy-start | bytes 772
  7.2 27.7 %all-to-all-start = ((bf16[64,4,768]{2,1,0:T(4,128)(2,1)}), bf16[64,4,768]{2,1,0:T(4,128)(2,1)S(1)}, u32[]{:S(2)}, u32[]{:S(2)}) async-start(bf16[64,4,768]{2,1,0:T(4,128)(2,1)} %broadcast_select_fusion.3), calls=%async_computation | async-start | bytes 786432 | tf_op jit(solution)/shard_map/all_to_all | solution.py:88
  36.8 11.2 %copy-start.4 = (f32[256,768]{1,0:T(8,128)S(1)}, f32[256,768]{1,0:T(8,128)}, u32[]{:S(2)}) copy-start(f32[256,768]{1,0:T(8,128)} %get-tuple-element.20) | copy-start | bytes 2359300
  54.5 14.3 %collective-permute-start = (f32[32,5120]{1,0:T(8,128)S(1)}, f32[32,5120]{1,0:T(8,128)S(1)}, u32[]{:S(2)}, u32[]{:S(2)}) collective-permute-start(f32[32,5120]{1,0:T(8,128)S(1)} %dynamic-slice_bitcast_fusion.1), channel_id=1, source_target_pairs={{0,1},{1,2},{2,3},{3,0},{4,5},{5,6},{6,7},{7,4},{8,9},{9,10},{10,1... | collective-permute-start | bytes 1966088 | tf_op jit(solution)/shard_map/ppermute | solution.py:52
  55.5 13.4 %collective-permute-start.6 = (f32[32,5120]{1,0:T(8,128)S(1)}, f32[32,5120]{1,0:T(8,128)S(1)}, u32[]{:S(2)}, u32[]{:S(2)}) collective-permute-start(f32[32,5120]{1,0:T(8,128)S(1)} %dynamic-slice_bitcast_fusion), channel_id=1, source_target_pairs={{0,3},{1,0},{2,1},{3,2},{4,7},{5,4},{6,5},{7,6},{8,11},{9,8},{10,9... | collective-permute-start | bytes 1966088 | tf_op jit(solution)/shard_map/ppermute | solution.py:53
  68.9 13.4 %collective-permute-start.1 = (f32[32,5120]{1,0:T(8,128)S(1)}, f32[32,5120]{1,0:T(8,128)S(1)}, u32[]{:S(2)}, u32[]{:S(2)}) collective-permute-start(f32[32,5120]{1,0:T(8,128)S(1)} %bitcast_add_fusion.5), channel_id=1, source_target_pairs={{0,1},{1,2},{2,3},{3,0},{4,5},{5,6},{6,7},{7,4},{8,9},{9,10},{10,1... | collective-permute-start | bytes 1966088 | tf_op jit(solution)/shard_map/ppermute | solution.py:52
  69.1 13.4 %collective-permute-start.7 = (f32[32,5120]{1,0:T(8,128)S(1)}, f32[32,5120]{1,0:T(8,128)S(1)}, u32[]{:S(2)}, u32[]{:S(2)}) collective-permute-start(f32[32,5120]{1,0:T(8,128)S(1)} %bitcast_add_fusion.2), channel_id=1, source_target_pairs={{0,3},{1,0},{2,1},{3,2},{4,7},{5,4},{6,5},{7,6},{8,11},{9,8},{10,9... | collective-permute-start | bytes 1966088 | tf_op jit(solution)/shard_map/ppermute | solution.py:53
  82.4 13.1 %collective-permute-start.2 = (f32[32,5120]{1,0:T(8,128)S(1)}, f32[32,5120]{1,0:T(8,128)S(1)}, u32[]{:S(2)}, u32[]{:S(2)}) collective-permute-start(f32[32,5120]{1,0:T(8,128)S(1)} %bitcast_add_fusion.4), channel_id=1, source_target_pairs={{0,1},{1,2},{2,3},{3,0},{4,5},{5,6},{6,7},{7,4},{8,9},{9,10},{10,1... | collective-permute-start | bytes 1966088 | tf_op jit(solution)/shard_map/ppermute | solution.py:52
  82.6 13.1 %collective-permute-start.8 = (f32[32,5120]{1,0:T(8,128)S(1)}, f32[32,5120]{1,0:T(8,128)S(1)}, u32[]{:S(2)}, u32[]{:S(2)}) collective-permute-start(f32[32,5120]{1,0:T(8,128)S(1)} %bitcast_add_fusion.1), channel_id=1, source_target_pairs={{0,3},{1,0},{2,1},{3,2},{4,7},{5,4},{6,5},{7,6},{8,11},{9,8},{10,9... | collective-permute-start | bytes 1966088 | tf_op jit(solution)/shard_map/ppermute | solution.py:53
  95.6 8.7 %collective-permute-start.3 = (bf16[32,5120]{1,0:T(8,128)(2,1)S(1)}, bf16[32,5120]{1,0:T(8,128)(2,1)}, u32[]{:S(2)}, u32[]{:S(2)}) collective-permute-start(bf16[32,5120]{1,0:T(8,128)(2,1)S(1)} %fusion.4), channel_id=1, source_target_pairs={{0,1},{1,2},{2,3},{3,0},{4,5},{5,6},{6,7},{7,4},{8,9},{9,10},{10,1... | collective-permute-start | bytes 983048 | tf_op jit(solution)/shard_map/ppermute | solution.py:58
  95.8 9.9 %collective-permute-start.9 = (bf16[32,5120]{1,0:T(8,128)(2,1)S(1)}, bf16[32,5120]{1,0:T(8,128)(2,1)}, u32[]{:S(2)}, u32[]{:S(2)}) collective-permute-start(bf16[32,5120]{1,0:T(8,128)(2,1)S(1)} %fusion.3), channel_id=1, source_target_pairs={{0,3},{1,0},{2,1},{3,2},{4,7},{5,4},{6,5},{7,6},{8,11},{9,8},{10,9... | collective-permute-start | bytes 983048 | tf_op jit(solution)/shard_map/ppermute | solution.py:59
  104.3 9.8 %collective-permute-start.4 = (bf16[32,5120]{1,0:T(8,128)(2,1)}, bf16[32,5120]{1,0:T(8,128)(2,1)}, u32[]{:S(2)}, u32[]{:S(2)}) collective-permute-start(bf16[32,5120]{1,0:T(8,128)(2,1)} %collective-permute-done.3), channel_id=1, source_target_pairs={{0,1},{1,2},{2,3},{3,0},{4,5},{5,6},{6,7},{7,4},{8,9},{9,10},{10,1... | collective-permute-start | bytes 983048 | tf_op jit(solution)/shard_map/ppermute | solution.py:58
  105.7 40.4 %collective-permute-start.10 = (bf16[32,5120]{1,0:T(8,128)(2,1)}, bf16[32,5120]{1,0:T(8,128)(2,1)}, u32[]{:S(2)}, u32[]{:S(2)}) collective-permute-start(bf16[32,5120]{1,0:T(8,128)(2,1)} %collective-permute-done.9), channel_id=1, source_target_pairs={{0,3},{1,0},{2,1},{3,2},{4,7},{5,4},{6,5},{7,6},{8,11},{9,8},{10,9... | collective-permute-start | bytes 983048 | tf_op jit(solution)/shard_map/ppermute | solution.py:59
  114.1 34.9 %collective-permute-start.5 = (bf16[32,5120]{1,0:T(8,128)(2,1)}, bf16[32,5120]{1,0:T(8,128)(2,1)}, u32[]{:S(2)}, u32[]{:S(2)}) collective-permute-start(bf16[32,5120]{1,0:T(8,128)(2,1)} %collective-permute-done.4), channel_id=1, source_target_pairs={{0,1},{1,2},{2,3},{3,0},{4,5},{5,6},{6,7},{7,4},{8,9},{9,10},{10,1... | collective-permute-start | bytes 983048 | tf_op jit(solution)/shard_map/ppermute | solution.py:58
  114.8 29.5 %all-to-all-start.1 = ((f32[64,1,4]{2,1,0:T(1,128)}), f32[64,1,4]{2,1,0:T(1,128)S(1)}, u32[]{:S(2)}, u32[]{:S(2)}) async-start(f32[64,1,4]{2,1,0:T(1,128)} %bitcast.38), calls=%async_computation.1 | async-start | bytes 65536 | tf_op jit(solution)/shard_map/all_to_all | solution.py:97
  146.1 11.0 %collective-permute-start.11 = (bf16[32,5120]{1,0:T(8,128)(2,1)}, bf16[32,5120]{1,0:T(8,128)(2,1)}, u32[]{:S(2)}, u32[]{:S(2)}) collective-permute-start(bf16[32,5120]{1,0:T(8,128)(2,1)} %collective-permute-done.10), channel_id=1, source_target_pairs={{0,3},{1,0},{2,1},{3,2},{4,7},{5,4},{6,5},{7,6},{8,11},{9,8},{10,9... | collective-permute-start | bytes 983048 | tf_op jit(solution)/shard_map/ppermute | solution.py:59
  162.5 1.7 %copy-start.3 = (bf16[4,32,5120]{2,1,0:T(8,128)(2,1)S(1)}, bf16[4,32,5120]{2,1,0:T(8,128)(2,1)}, u32[]{:S(2)}) copy-start(bf16[4,32,5120]{2,1,0:T(8,128)(2,1)} %broadcast_select_fusion.1) | copy-start | bytes 3932164

commit v4 on v3

--- a/solution.py
+++ b/solution.py
@@ -59,12 +59,11 @@
         down = lax.ppermute(down, "vocab", backward)
         ups.append(up)
         downs.append(down)
-    ups = jnp.stack(ups)
-    downs = jnp.stack(downs)
-    order = jnp.arange(ring, dtype=jnp.int32)
-    top = jnp.take(ups, (me - order) % ring, axis=0)
-    bottom = jnp.take(downs, (order - me) % ring, axis=0)
-    return jnp.concatenate([top, bottom], axis=0).reshape(rows, width)
+    placed = jnp.zeros((2 * ring, chunk, width), jnp.bfloat16)
+    for k in range(ring):
+        placed = lax.dynamic_update_index_in_dim(placed, ups[k], (me - k) % ring, 0)
+        placed = lax.dynamic_update_index_in_dim(placed, downs[k], ring + (me + k) % ring, 0)
+    return placed.reshape(rows, width)
 
 
 def body(hidden_rows, plan_lengths, shard_of_class, head_weight, teacher_logprobs):
@@ -92,12 +91,19 @@
     teacher_slots = jnp.transpose(teacher_slots, (1, 0, 2)).reshape(source_slots, -1)
     live = jnp.arange(source_slots, dtype=jnp.int32) < plan_lengths[myself]
     row_grad, row_div = divergence(hidden_rows, teacher_slots, live, head_weight)
+    slot_class = (own_offset + jnp.arange(source_slots, dtype=jnp.int32)) % shards
+    slot_target = shard_of_class[slot_class] * balanced + (own_offset + jnp.arange(source_slots, dtype=jnp.int32)) // shards
+    slot_target = jnp.where(live, slot_target, shards * balanced)
+    positions = jnp.arange(shards * balanced, dtype=jnp.int32)
     column_of = (inverse - own_offset) % shards
-    div_out = jnp.take(row_div.reshape(slot_depth, shards), column_of, axis=1).T
-    div_in = lax.all_to_all(div_out, "dp", split_axis=0, concat_axis=0, tiled=True)
-    packed = jnp.arange(balanced, dtype=jnp.int32) * shards + inverse[myself]
-    owner = jnp.sum((offsets[None, :] <= packed[:, None]).astype(jnp.int32), axis=1) - 1
-    row_kl = div_in[owner, (packed - offsets[owner]) // shards]
+    target_of = jnp.take(slot_target.reshape(slot_depth, shards), column_of, axis=1)
+    div_of = jnp.take(row_div.reshape(slot_depth, shards), column_of, axis=1)
+    spread = jnp.zeros((shards, balanced), jnp.float32)
+    for r in range(slot_depth):
+        hit = target_of[r][:, None] == positions.reshape(shards, balanced)
+        spread = spread + jnp.where(hit, div_of[r][:, None], 0.0)
+    wide = jnp.broadcast_to(spread[:, :, None], (shards, balanced, 16))
+    row_kl = lax.psum_scatter(wide, "dp", scatter_dimension=0, tiled=True)[0, :, 0]
     return row_grad, row_kl
 
 

time: 166 us -> 246 us (1.48)
  the two profiles are of different devices: /device:TPU:1 before, /device:TPU:6 now
where the time goes in v4:
time: 246 us; the launch traced here: 245 us
  waiting for transfers between devices  134 us (54%)
  starting transfers between devices  30.6 us (12%)
  local copies, waits for them, and re-layouts  25.4 us (10%)
  other arithmetic  16.9 us (7%)
  between operations  14.5 us (6%)
  blocking collectives  12 us (5%)
  matrix products  11.8 us (5%)
    reduce_scatter x1, waiting for transfers between devices, body(): lax.psum_scatter(wide, 'dp', scatter_dimension=0, tiled=True)[0, :, 0]  95.1 us
    ppermute x3, waiting for transfers between devices, ring_all_reduce(): up = lax.ppermute(up, 'vocab', forward) + own(0, me - step - 2)  26.7 us
    all_to_all x1, starting transfers between devices, body(): lax.all_to_all(outgoing, 'dp', split_axis=0, concat_axis=0, tiled=True)  12.1 us
    all_gather x1, blocking collectives, divergence(): lax.all_gather(jnp.stack([own_top, own_total, own_mass, own_cross]), 'voc...  12 us
    ppermute x3, starting transfers between devices, ring_all_reduce(): up = lax.ppermute(up, 'vocab', forward) + own(0, me - step - 2)  10.8 us
    ppermute x3, waiting for transfers between devices, ring_all_reduce(): up = lax.ppermute(up, 'vocab', forward)  8.5 us
    dot_general x1, matrix products, divergence(): logits = jnp.dot(row_block, weight, preferred_element_type=jnp.float32)  6.3 us
    ppermute x3, starting transfers between devices, ring_all_reduce(): up = lax.ppermute(up, 'vocab', forward)  5.74 us
  transfers between devices with their start and end apart: 14, of which 10 were waited for; matrix products, arithmetic and copies ran while one was open for 12% of the time, Pallas kernels for 0%

profile of v4, /device:TPU:6, one launch (start us, length us, event | category | flops | bytes accessed | tf_op | source)
XLA Modules:
  0.0 244.8 jit_solution(4490720420309734749)
XLA Ops:
  7.2 0.9 select_reduce_fusion
  8.1 0.8 copy.32
  9.1 0.6 dynamic_slice.36
  9.7 1.3 and_select_fusion.3
  11.0 0.6 dynamic_slice.35
  11.8 0.7 compare_select_fusion
  12.5 2.4 gather_fusion.1
  15.1 1.0 broadcast_select_fusion.1
  16.1 12.1 %all-to-all-start = ((bf16[64,4,768]{2,1,0:T(4,128)(2,1)}), bf16[64,4,768]{2,1,0:T(4,128)(2,1)S(1)}, u32[]{:S(2)}, u32[]{:S(2)}) async-start(bf16[64,4,768]{2,1,0:T(4,128)(2,1)} %broadcast_select_fusion.1), calls=%async_computation | async-start | bytes 786432 | tf_op jit(solution)/shard_map/all_to_all | solution.py:87
  28.3 0.7 fusion.27
  28.9 0.8 gather_fusion
  29.7 0.6 dynamic_slice.34
  30.3 0.7 compare_and_fusion
  31.0 1.9 gather_fusion.3
  33.1 1.2 fusion.7
  34.3 0.6 gather_fusion.4
  35.0 0.2 slice_reduce_fusion.7
  35.2 0.6 iota_compare_fusion.1
  36.0 6.3 %fusion.34 = (f32[256]{0:T(256)S(1)}, f32[256,768]{1,0:T(8,128)}) fusion(bf16[256,5120]{1,0:T(8,128)(2,1)S(1)} %copy-done, bf16[5120,768]{1,0:T(8,128)(2,1)} %param.8), kind=kOutput, calls=%fused_computation.128 | convolution fusion | flops 2013462272 | bytes 11273216 | tf_op jit(solution)/shard_map/dot_general | solution.py:10
  42.3 0.4 all-to-all-done
  42.7 0.9 gather_fusion.2
  43.6 0.2 convert_bitcast_fusion
  43.9 0.5 fusion
  44.6 1.5 exponential_reduce_fusion
  46.2 12.0 %all-gather.1 = f32[4,4,256]{2,1,0:T(4,128)S(1)} all-gather(f32[1,4,256]{2,1,0:T(4,128)S(1)} %maximum_bitcast_fusion), channel_id=2, replica_groups=mesh['dp'=64,'vocab'=4] {'vocab'}, dimensions={0}, use_global_device_ids=true | all-gather | bytes 20480 | tf_op jit(solution)/shard_map/all_gather | solution.py:17
  58.3 1.4 select_convert_fusion
  59.7 5.5 %fusion.35 = f32[256,5120]{1,0:T(8,128)S(1)} fusion(bf16[256,768]{1,0:T(8,128)(2,1)S(1)} %select_convert_fusion, bf16[5120,768]{1,0:T(8,128)(2,1)} %param.8), kind=kOutput, calls=%fused_computation.129 | convolution fusion | flops 2013265920 | bytes 13500416 | tf_op jit(solution)/shard_map/dot_general | solution.py:30
  65.2 0.5 fusion.32
  65.8 1.5 copy-done.2
  67.3 1.1 dynamic-slice_bitcast_fusion
  68.3 0.9 dynamic-slice_bitcast_fusion.1
  69.2 3.2 %collective-permute-start = (f32[32,5120]{1,0:T(8,128)}, f32[32,5120]{1,0:T(8,128)}, u32[]{:S(2)}, u32[]{:S(2)}) collective-permute-start(f32[32,5120]{1,0:T(8,128)} %dynamic-slice_bitcast_fusion.1), channel_id=1, source_target_pairs={{0,1},{1,2},{2,3},{3,0},{4,5},{5,6},{6,7},{7,4},{8,9},{9,10},{10,1... | collective-permute-start | bytes 1966088 | tf_op jit(solution)/shard_map/ppermute | solution.py:52
  72.6 0.6 fusion.16
  73.2 0.6 gather_fusion.5
  74.3 0.8 broadcast_in_dim.182
  75.1 8.7 %collective-permute-done = f32[32,5120]{1,0:T(8,128)} collective-permute-done((f32[32,5120]{1,0:T(8,128)}, f32[32,5120]{1,0:T(8,128)}, u32[]{:S(2)}, u32[]{:S(2)}) %collective-permute-start) | collective-permute-done | bytes 655392 | tf_op jit(solution)/shard_map/ppermute | solution.py:52
  83.9 1.4 bitcast_add_fusion.5
  85.2 3.8 %collective-permute-start.1 = (f32[32,5120]{1,0:T(8,128)S(1)}, f32[32,5120]{1,0:T(8,128)S(1)}, u32[]{:S(2)}, u32[]{:S(2)}) collective-permute-start(f32[32,5120]{1,0:T(8,128)S(1)} %bitcast_add_fusion.5), channel_id=1, source_target_pairs={{0,1},{1,2},{2,3},{3,0},{4,5},{5,6},{6,7},{7,4},{8,9},{9,10},{10,1... | collective-permute-start | bytes 1966088 | tf_op jit(solution)/shard_map/ppermute | solution.py:52
  89.0 1.2 bitcast_add_fusion.2
  90.3 9.0 %collective-permute-done.1 = f32[32,5120]{1,0:T(8,128)S(1)} collective-permute-done((f32[32,5120]{1,0:T(8,128)S(1)}, f32[32,5120]{1,0:T(8,128)S(1)}, u32[]{:S(2)}, u32[]{:S(2)}) %collective-permute-start.1) | collective-permute-done | bytes 655392 | tf_op jit(solution)/shard_map/ppermute | solution.py:52
  99.2 1.2 bitcast_add_fusion.4
  100.4 3.8 %collective-permute-start.2 = (f32[32,5120]{1,0:T(8,128)S(1)}, f32[32,5120]{1,0:T(8,128)S(1)}, u32[]{:S(2)}, u32[]{:S(2)}) collective-permute-start(f32[32,5120]{1,0:T(8,128)S(1)} %bitcast_add_fusion.4), channel_id=1, source_target_pairs={{0,1},{1,2},{2,3},{3,0},{4,5},{5,6},{6,7},{7,4},{8,9},{9,10},{10,1... | collective-permute-start | bytes 1966088 | tf_op jit(solution)/shard_map/ppermute | solution.py:52
  104.2 0.5 collective-permute-done.4
  104.9 8.9 %collective-permute-done.2 = f32[32,5120]{1,0:T(8,128)S(1)} collective-permute-done((f32[32,5120]{1,0:T(8,128)S(1)}, f32[32,5120]{1,0:T(8,128)S(1)}, u32[]{:S(2)}, u32[]{:S(2)}) %collective-permute-start.2) | collective-permute-done | bytes 655392 | tf_op jit(solution)/shard_map/ppermute | solution.py:52
  113.8 0.3 broadcast_in_dim.152
  114.1 1.2 bitcast_dynamic-update-slice_fusion.7
  115.3 3.8 %collective-permute-start.6 = (bf16[32,5120]{1,0:T(8,128)(2,1)S(1)}, bf16[32,5120]{1,0:T(8,128)(2,1)}, u32[]{:S(2)}, u32[]{:S(2)}) collective-permute-start(bf16[32,5120]{1,0:T(8,128)(2,1)S(1)} %get-tuple-element.20), channel_id=1, source_target_pairs={{0,1},{1,2},{2,3},{3,0},{4,5},{5,6},{6,7},{7,4},{8,9},{9,10},{10,1... | collective-permute-start | bytes 983048 | tf_op jit(solution)/shard_map/ppermute | solution.py:58
  119.2 1.5 copy-done.5
  120.6 95.1 %reduce-scatter.2.cloned.1.call-done = f32[1,128,16]{1,2,0:T(8,128)} async-done(((f32[64,128,16]{1,2,0:T(8,128)}), f32[1,128,16]{1,2,0:T(8,128)}) %reduce-scatter.2.cloned.1.call-update) | async-done | bytes 8208 | tf_op jit(solution)/shard_map/reduce_scatter | solution.py:106
  215.7 1.2 slice_bitcast_fusion
  216.9 0.6 collective-permute-start.8
  217.5 1.4 collective-permute-start.9
  218.9 1.7 bitcast_dynamic-update-slice_fusion.5
  220.6 1.7 bitcast_dynamic-update-slice_fusion.4
  222.3 4.9 %collective-permute-done.8 = bf16[32,5120]{1,0:T(8,128)(2,1)S(1)} collective-permute-done((bf16[32,5120]{1,0:T(8,128)(2,1)}, bf16[32,5120]{1,0:T(8,128)(2,1)S(1)}, u32[]{:S(2)}, u32[]{:S(2)}) %collective-permute-start.8) | collective-permute-done | bytes 327712 | tf_op jit(solution)/shard_map/ppermute | solution.py:58
  227.3 1.4 collective-permute-start.10
  228.7 0.3 collective-permute-done.9
  228.9 0.4 collective-permute-start.11
  229.3 0.7 bitcast_dynamic-update-slice_fusion.3
  230.1 0.7 bitcast_dynamic-update-slice_fusion.2
  230.8 3.6 %collective-permute-done.10 = bf16[32,5120]{1,0:T(8,128)(2,1)S(1)} collective-permute-done((bf16[32,5120]{1,0:T(8,128)(2,1)S(1)}, bf16[32,5120]{1,0:T(8,128)(2,1)S(1)}, u32[]{:S(2)}, u32[]{:S(2)}) %collective-permute-start.10) | collective-permute-done | bytes 327712 | tf_op jit(solution)/shard_map/ppermute | solution.py:58
  234.4 0.7 bitcast_dynamic-update-slice_fusion.1
  235.1 2.1 collective-permute-done.11
  237.2 0.7 bitcast_dynamic-update-slice_fusion
  (55 shorter events, 2.4 us)
Async XLA Ops:
  7.2 28.8 %copy-start = (bf16[256,5120]{1,0:T(8,128)(2,1)S(1)}, bf16[256,5120]{1,0:T(8,128)(2,1)}, u32[]{:S(2)}) copy-start(bf16[256,5120]{1,0:T(8,128)(2,1)} %param.5) | copy-start | bytes 7864324
  12.5 16.5 %copy-start.1 = (s32[64]{0:T(128)S(1)}, s32[64]{0:T(128)}, u32[]{:S(2)}) copy-start(s32[64]{0:T(128)} %param.7) | copy-start | bytes 772
  12.5 17.3 %copy-start.6 = (s32[64]{0:T(128)S(1)}, s32[64]{0:T(128)}, u32[]{:S(2)}) copy-start(s32[64]{0:T(128)} %param.6) | copy-start | bytes 772
  16.1 26.6 %all-to-all-start = ((bf16[64,4,768]{2,1,0:T(4,128)(2,1)}), bf16[64,4,768]{2,1,0:T(4,128)(2,1)S(1)}, u32[]{:S(2)}, u32[]{:S(2)}) async-start(bf16[64,4,768]{2,1,0:T(4,128)(2,1)} %broadcast_select_fusion.1), calls=%async_computation | async-start | bytes 786432 | tf_op jit(solution)/shard_map/all_to_all | solution.py:87
  28.2 187.5 %reduce-scatter.2.cloned.1.call-start = ((), (), s32[]{:S(2)}) async-start(), calls=%async_computation.2 | async-start | bytes 532480 | tf_op jit(solution)/shard_map/reduce_scatter | solution.py:106
  65.8 1.5 copy-start.2
  65.8 2.6 %copy-start.4 = (f32[128,5120]{1,0:T(8,128)}, f32[128,5120]{1,0:T(8,128)S(1)}, u32[]{:S(2)}) copy-start(f32[128,5120]{1,0:T(8,128)S(1)} %get-tuple-element.24) | copy-start | bytes 7864324
  68.3 20.7 %collective-permute-start.3 = (f32[32,5120]{1,0:T(8,128)}, f32[32,5120]{1,0:T(8,128)S(1)}, u32[]{:S(2)}, u32[]{:S(2)}) collective-permute-start(f32[32,5120]{1,0:T(8,128)} %dynamic-slice_bitcast_fusion), channel_id=1, source_target_pairs={{0,3},{1,0},{2,1},{3,2},{4,7},{5,4},{6,5},{7,6},{8,11},{9,8},{10,9... | collective-permute-start | bytes 1966088 | tf_op jit(solution)/shard_map/ppermute | solution.py:53
  69.2 14.7 %collective-permute-start = (f32[32,5120]{1,0:T(8,128)}, f32[32,5120]{1,0:T(8,128)}, u32[]{:S(2)}, u32[]{:S(2)}) collective-permute-start(f32[32,5120]{1,0:T(8,128)} %dynamic-slice_bitcast_fusion.1), channel_id=1, source_target_pairs={{0,1},{1,2},{2,3},{3,0},{4,5},{5,6},{6,7},{7,4},{8,9},{9,10},{10,1... | collective-permute-start | bytes 1966088 | tf_op jit(solution)/shard_map/ppermute | solution.py:52
  75.1 29.6 %copy-start.3 = (f32[128,5120]{1,0:T(8,128)S(1)}, f32[128,5120]{1,0:T(8,128)}, u32[]{:S(2)}) copy-start(f32[128,5120]{1,0:T(8,128)} %copy-done.2) | copy-start | bytes 7864324
  85.2 14.0 %collective-permute-start.1 = (f32[32,5120]{1,0:T(8,128)S(1)}, f32[32,5120]{1,0:T(8,128)S(1)}, u32[]{:S(2)}, u32[]{:S(2)}) collective-permute-start(f32[32,5120]{1,0:T(8,128)S(1)} %bitcast_add_fusion.5), channel_id=1, source_target_pairs={{0,1},{1,2},{2,3},{3,0},{4,5},{5,6},{6,7},{7,4},{8,9},{9,10},{10,1... | collective-permute-start | bytes 1966088 | tf_op jit(solution)/shard_map/ppermute | solution.py:52
  90.2 14.5 %collective-permute-start.4 = (f32[32,5120]{1,0:T(8,128)S(1)}, f32[32,5120]{1,0:T(8,128)S(1)}, u32[]{:S(2)}, u32[]{:S(2)}) collective-permute-start(f32[32,5120]{1,0:T(8,128)S(1)} %bitcast_add_fusion.2), channel_id=1, source_target_pairs={{0,3},{1,0},{2,1},{3,2},{4,7},{5,4},{6,5},{7,6},{8,11},{9,8},{10,9... | collective-permute-start | bytes 1966088 | tf_op jit(solution)/shard_map/ppermute | solution.py:53
  100.4 13.4 %collective-permute-start.2 = (f32[32,5120]{1,0:T(8,128)S(1)}, f32[32,5120]{1,0:T(8,128)S(1)}, u32[]{:S(2)}, u32[]{:S(2)}) collective-permute-start(f32[32,5120]{1,0:T(8,128)S(1)} %bitcast_add_fusion.4), channel_id=1, source_target_pairs={{0,1},{1,2},{2,3},{3,0},{4,5},{5,6},{6,7},{7,4},{8,9},{9,10},{10,1... | collective-permute-start | bytes 1966088 | tf_op jit(solution)/shard_map/ppermute | solution.py:52
  104.8 14.3 %collective-permute-start.5 = (f32[32,5120]{1,0:T(8,128)S(1)}, f32[32,5120]{1,0:T(8,128)S(1)}, u32[]{:S(2)}, u32[]{:S(2)}) collective-permute-start(f32[32,5120]{1,0:T(8,128)S(1)} %bitcast_add_fusion.1), channel_id=1, source_target_pairs={{0,3},{1,0},{2,1},{3,2},{4,7},{5,4},{6,5},{7,6},{8,11},{9,8},{10,9... | collective-permute-start | bytes 1966088 | tf_op jit(solution)/shard_map/ppermute | solution.py:53
  115.3 101.6 %collective-permute-start.6 = (bf16[32,5120]{1,0:T(8,128)(2,1)S(1)}, bf16[32,5120]{1,0:T(8,128)(2,1)}, u32[]{:S(2)}, u32[]{:S(2)}) collective-permute-start(bf16[32,5120]{1,0:T(8,128)(2,1)S(1)} %get-tuple-element.20), channel_id=1, source_target_pairs={{0,1},{1,2},{2,3},{3,0},{4,5},{5,6},{6,7},{7,4},{8,9},{9,10},{10,1... | collective-permute-start | bytes 983048 | tf_op jit(solution)/shard_map/ppermute | solution.py:58
  119.1 1.5 copy-start.5
  120.6 96.8 %collective-permute-start.7 = (bf16[32,5120]{1,0:T(8,128)(2,1)S(1)}, bf16[32,5120]{1,0:T(8,128)(2,1)}, u32[]{:S(2)}, u32[]{:S(2)}) collective-permute-start(bf16[32,5120]{1,0:T(8,128)(2,1)S(1)} %get-tuple-element.18), channel_id=1, source_target_pairs={{0,3},{1,0},{2,1},{3,2},{4,7},{5,4},{6,5},{7,6},{8,11},{9,8},{10,9... | collective-permute-start | bytes 983048 | tf_op jit(solution)/shard_map/ppermute | solution.py:59
  216.9 10.4 %collective-permute-start.8 = (bf16[32,5120]{1,0:T(8,128)(2,1)}, bf16[32,5120]{1,0:T(8,128)(2,1)S(1)}, u32[]{:S(2)}, u32[]{:S(2)}) collective-permute-start(bf16[32,5120]{1,0:T(8,128)(2,1)} %collective-permute-done.6), channel_id=1, source_target_pairs={{0,1},{1,2},{2,3},{3,0},{4,5},{5,6},{6,7},{7,4},{8,9},{9,10},{10,1... | collective-permute-start | bytes 983048 | tf_op jit(solution)/shard_map/ppermute | solution.py:58
  217.5 11.5 %collective-permute-start.9 = (bf16[32,5120]{1,0:T(8,128)(2,1)}, bf16[32,5120]{1,0:T(8,128)(2,1)S(1)}, u32[]{:S(2)}, u32[]{:S(2)}) collective-permute-start(bf16[32,5120]{1,0:T(8,128)(2,1)} %collective-permute-done.7), channel_id=1, source_target_pairs={{0,3},{1,0},{2,1},{3,2},{4,7},{5,4},{6,5},{7,6},{8,11},{9,8},{10,9... | collective-permute-start | bytes 983048 | tf_op jit(solution)/shard_map/ppermute | solution.py:59
  227.3 7.1 %collective-permute-start.10 = (bf16[32,5120]{1,0:T(8,128)(2,1)S(1)}, bf16[32,5120]{1,0:T(8,128)(2,1)S(1)}, u32[]{:S(2)}, u32[]{:S(2)}) collective-permute-start(bf16[32,5120]{1,0:T(8,128)(2,1)S(1)} %collective-permute-done.8), channel_id=1, source_target_pairs={{0,1},{1,2},{2,3},{3,0},{4,5},{5,6},{6,7},{7,4},{8,9},{9,10},{10,1... | collective-permute-start | bytes 983048 | tf_op jit(solution)/shard_map/ppermute | solution.py:58
  228.9 8.3 %collective-permute-start.11 = (bf16[32,5120]{1,0:T(8,128)(2,1)S(1)}, bf16[32,5120]{1,0:T(8,128)(2,1)S(1)}, u32[]{:S(2)}, u32[]{:S(2)}) collective-permute-start(bf16[32,5120]{1,0:T(8,128)(2,1)S(1)} %collective-permute-done.9), channel_id=1, source_target_pairs={{0,3},{1,0},{2,1},{3,2},{4,7},{5,4},{6,5},{7,6},{8,11},{9,8},{10,9... | collective-permute-start | bytes 983048 | tf_op jit(solution)/shard_map/ppermute | solution.py:59
Sparse Core Ops, SparseCore 0:
  75.2 140.4 reduce-scatter.1

commit v5 on v3

--- a/solution.py
+++ b/solution.py
@@ -49,22 +49,23 @@
     up = own(0, me - 1)
     down = own(1, me + 1)
     for step in range(ring - 1):
-        up = lax.ppermute(up, "vocab", forward) + own(0, me - step - 2)
-        down = lax.ppermute(down, "vocab", backward) + own(1, me + step + 2)
+        up = lax.ppermute(up, "vocab", forward)
+        down = lax.ppermute(down, "vocab", backward)
+        up = up + own(0, me - step - 2)
+        down = down + own(1, me + step + 2)
     up = up.astype(jnp.bfloat16)
     down = down.astype(jnp.bfloat16)
     ups, downs = [up], [down]
-    for step in range(ring - 1):
+    for _ in range(ring - 1):
         up = lax.ppermute(up, "vocab", forward)
         down = lax.ppermute(down, "vocab", backward)
         ups.append(up)
         downs.append(down)
-    ups = jnp.stack(ups)
-    downs = jnp.stack(downs)
-    order = jnp.arange(ring, dtype=jnp.int32)
-    top = jnp.take(ups, (me - order) % ring, axis=0)
-    bottom = jnp.take(downs, (order - me) % ring, axis=0)
-    return jnp.concatenate([top, bottom], axis=0).reshape(rows, width)
+    placed = jnp.zeros((2 * ring, chunk, width), jnp.bfloat16)
+    for k in range(ring):
+        placed = lax.dynamic_update_index_in_dim(placed, ups[k], (me - k) % ring, 0)
+        placed = lax.dynamic_update_index_in_dim(placed, downs[k], ring + (me + k) % ring, 0)
+    return placed.reshape(rows, width)
 
 
 def body(hidden_rows, plan_lengths, shard_of_class, head_weight, teacher_logprobs):

time: 166 us -> 154 us (0.928)
  starting transfers between devices: 50.5 us -> 44.3 us
  waiting for transfers between devices: 53.9 us -> 47.8 us
  other arithmetic: 22.3 us -> 16.9 us
  local copies, waits for them, and re-layouts: 16.8 us -> 21.7 us
    ppermute x6 -> x0, waiting for transfers between devices: 31.9 us -> none  [the longest x3 31.9 us: ring_all_reduce(): up = lax.ppermute(up, 'vocab', forward) + own(0, me - step - 2)]
    ppermute x3 -> x6, waiting for transfers between devices: 11.4 us -> 37 us  [ring_all_reduce(): up = lax.ppermute(up, 'vocab', forward)]
    ppermute x6 -> x0, starting transfers between devices: 8.63 us -> none  [the longest x3 7.47 us: ring_all_reduce(): down = lax.ppermute(down, 'vocab', backward) + own(1, me + step + 2)]
    ppermute x3 -> x6, starting transfers between devices: 8.44 us -> 15.5 us  [ring_all_reduce(): down = lax.ppermute(down, 'vocab', backward)]
    dynamic_update_slice x0 -> x6, local copies, waits for them, and re-layouts: none -> 6.41 us  [the longest x3 3.21 us: ring_all_reduce(): lax.dynamic_update_index_in_dim(placed, downs[k], ring + (me + k) % ring, 0)]
    gather x2 -> x0, local copies, waits for them, and re-layouts: 6.03 us -> none  [the longest x1 3.03 us: ring_all_reduce(): top = jnp.take(ups, (me - order) % ring, axis=0)]
    all_to_all x1, starting transfers between devices: 20.2 us -> 14.2 us  [body(): lax.all_to_all(div_out, 'dp', split_axis=0, concat_axis=0, tiled=True)]
    another operation x4 -> x2, other arithmetic: 4.98 us -> 0.2 us  [the longest x1 2.39 us: ring_all_reduce(): ups = jnp.stack(ups)]
  transfers between devices with their start and end apart: 14 -> 14, of which waited for: 7 -> 7; matrix products, arithmetic and copies ran while one was open for 15% -> 19% of each run, Pallas kernels for 0% -> 0%
where the time goes in v5:
time: 154 us; the launch traced here: 153 us
  waiting for transfers between devices  47.8 us (31%)
  starting transfers between devices  44.3 us (29%)
  local copies, waits for them, and re-layouts  21.7 us (14%)
  other arithmetic  16.9 us (11%)
  matrix products  11.8 us (8%)
  blocking collectives  9.48 us (6%)
    ppermute x6, waiting for transfers between devices, ring_all_reduce(): up = lax.ppermute(up, 'vocab', forward)  37 us
    ppermute x6, starting transfers between devices, ring_all_reduce(): down = lax.ppermute(down, 'vocab', backward)  15.5 us
    all_to_all x1, starting transfers between devices, body(): lax.all_to_all(div_out, 'dp', split_axis=0, concat_axis=0, tiled=True)  14.2 us
    all_to_all x1, starting transfers between devices, body(): lax.all_to_all(outgoing, 'dp', split_axis=0, concat_axis=0, tiled=True)  13.1 us
    all_gather x1, blocking collectives, divergence(): lax.all_gather(jnp.stack([own_top, own_total, own_mass, own_cross]), 'voc...  9.48 us
    all_to_all x1, waiting for transfers between devices, body(): lax.all_to_all(div_out, 'dp', split_axis=0, concat_axis=0, tiled=True)  8.61 us
    dot_general x1, matrix products, divergence(): logits = jnp.dot(row_block, weight, preferred_element_type=jnp.float32)  6.31 us
    dot_general x1, matrix products, divergence(): lax.dot_general(grad_logits, weight, (((1,), (1,)), ((), ())), preferred_...  5.51 us
  transfers between devices with their start and end apart: 14, of which 7 were waited for; matrix products, arithmetic and copies ran while one was open for 19% of the time, Pallas kernels for 0%

profile of v5, /device:TPU:1, one launch (start us, length us, event | category | flops | bytes accessed | tf_op | source)
XLA Modules:
  0.0 153.2 jit_solution(10004945254367200588)
XLA Ops:
  0.6 0.9 select_reduce_fusion
  1.6 0.8 copy.31
  2.4 0.1 reduce.5
  2.5 0.6 dynamic_slice.37
  3.1 1.3 and_select_fusion.3
  4.6 0.1 min.22
  4.7 2.4 %gather_fusion.1 = bf16[256,768]{1,0:T(8,128)(2,1)S(1)} fusion(bf16[128,768]{1,0:T(8,128)(2,1)} %param.9, s32[1024]{0:T(1024)S(1)} %pad_clamp_fusion.3), kind=kCustom, calls=%fused_computation.1 | custom fusion | bytes 787456 | tf_op jit(solution)/shard_map/jit(_take)/gather | solution.py:86
  7.2 0.1 copy.32
  7.3 1.0 broadcast_select_fusion.1
  8.3 13.1 %all-to-all-start = ((bf16[64,4,768]{2,1,0:T(4,128)(2,1)}), bf16[64,4,768]{2,1,0:T(4,128)(2,1)S(1)}, u32[]{:S(2)}, u32[]{:S(2)}) async-start(bf16[64,4,768]{2,1,0:T(4,128)(2,1)} %broadcast_select_fusion.1), calls=%async_computation | async-start | bytes 786432 | tf_op jit(solution)/shard_map/all_to_all | solution.py:89
  21.5 0.6 dynamic_slice.36
  22.1 0.7 fusion.15
  22.7 0.8 gather_fusion
  23.5 0.6 dynamic_slice.35
  24.1 0.7 compare_and_fusion
  24.8 0.7 multiply_add_fusion.1
  25.6 0.6 iota_compare_fusion.1
  26.3 1.2 gather_fusion.4
  27.6 6.3 %fusion.27 = (f32[256]{0:T(256)S(1)}, f32[256,768]{1,0:T(8,128)}) fusion(bf16[256,5120]{1,0:T(8,128)(2,1)S(1)} %copy-done, bf16[5120,768]{1,0:T(8,128)(2,1)} %param.8), kind=kOutput, calls=%fused_computation.108 | convolution fusion | flops 2013462272 | bytes 11273216 | tf_op jit(solution)/shard_map/dot_general | solution.py:10
  33.9 2.1 %all-to-all-done = bf16[64,4,768]{2,1,0:T(4,128)(2,1)S(1)} async-done(((bf16[64,4,768]{2,1,0:T(4,128)(2,1)}), bf16[64,4,768]{2,1,0:T(4,128)(2,1)S(1)}, u32[]{:S(2)}, u32[]{:S(2)}) %all-to-all-start) | async-done | bytes 393248 | tf_op jit(solution)/shard_map/all_to_all | solution.py:89
  36.0 0.9 gather_fusion.2
  36.9 0.2 convert_bitcast_fusion
  37.2 0.5 fusion
  37.6 0.2 copy.35
  38.0 1.5 exponential_reduce_fusion
  39.5 9.5 %all-gather.1 = f32[4,4,256]{2,1,0:T(4,128)S(1)} all-gather(f32[1,4,256]{2,1,0:T(4,128)S(1)} %maximum_bitcast_fusion), channel_id=2, replica_groups=mesh['dp'=64,'vocab'=4] {'vocab'}, dimensions={0}, use_global_device_ids=true | all-gather | bytes 20480 | tf_op jit(solution)/shard_map/all_gather | solution.py:17
  49.1 1.4 select_convert_fusion
  50.5 5.5 %fusion.28 = f32[256,5120]{1,0:T(8,128)S(1)} fusion(bf16[256,768]{1,0:T(8,128)(2,1)S(1)} %select_convert_fusion, bf16[5120,768]{1,0:T(8,128)(2,1)} %param.8), kind=kOutput, calls=%fused_computation.109 | convolution fusion | flops 2013265920 | bytes 13500416 | tf_op jit(solution)/shard_map/dot_general | solution.py:30
  56.0 0.5 fusion.25
  56.6 1.0 dynamic-slice_bitcast_fusion.1
  57.6 0.9 collective-permute-start
  58.5 0.9 dynamic-slice_bitcast_fusion
  59.4 2.1 %collective-permute-start.3 = (f32[32,5120]{1,0:T(8,128)}, f32[32,5120]{1,0:T(8,128)S(1)}, u32[]{:S(2)}, u32[]{:S(2)}) collective-permute-start(f32[32,5120]{1,0:T(8,128)} %dynamic-slice_bitcast_fusion), channel_id=1, source_target_pairs={{0,3},{1,0},{2,1},{3,2},{4,7},{5,4},{6,5},{7,6},{8,11},{9,8},{10,9... | collective-permute-start | bytes 1966088 | tf_op jit(solution)/shard_map/ppermute | solution.py:53
  61.6 0.1 copy.37
  61.7 0.6 fusion.5
  62.2 0.6 gather_fusion.3
  62.8 9.3 %collective-permute-done = f32[32,5120]{1,0:T(8,128)} collective-permute-done((f32[32,5120]{1,0:T(8,128)}, f32[32,5120]{1,0:T(8,128)}, u32[]{:S(2)}, u32[]{:S(2)}) %collective-permute-start) | collective-permute-done | bytes 655392 | tf_op jit(solution)/shard_map/ppermute | solution.py:52
  72.1 1.4 bitcast_add_fusion.5
  73.5 0.3 collective-permute-start.1
  73.7 1.2 bitcast_add_fusion.2
  74.9 2.7 %collective-permute-start.4 = (f32[32,5120]{1,0:T(8,128)S(1)}, f32[32,5120]{1,0:T(8,128)S(1)}, u32[]{:S(2)}, u32[]{:S(2)}) collective-permute-start(f32[32,5120]{1,0:T(8,128)S(1)} %bitcast_add_fusion.2), channel_id=1, source_target_pairs={{0,3},{1,0},{2,1},{3,2},{4,7},{5,4},{6,5},{7,6},{8,11},{9,8},{10,9... | collective-permute-start | bytes 1966088 | tf_op jit(solution)/shard_map/ppermute | solution.py:53
  77.7 9.4 %collective-permute-done.1 = f32[32,5120]{1,0:T(8,128)S(1)} collective-permute-done((f32[32,5120]{1,0:T(8,128)S(1)}, f32[32,5120]{1,0:T(8,128)S(1)}, u32[]{:S(2)}, u32[]{:S(2)}) %collective-permute-start.1) | collective-permute-done | bytes 655392 | tf_op jit(solution)/shard_map/ppermute | solution.py:52
  87.1 1.2 bitcast_add_fusion.4
  88.5 2.7 %collective-permute-start.5 = (f32[32,5120]{1,0:T(8,128)S(1)}, f32[32,5120]{1,0:T(8,128)S(1)}, u32[]{:S(2)}, u32[]{:S(2)}) collective-permute-start(f32[32,5120]{1,0:T(8,128)S(1)} %bitcast_add_fusion.1), channel_id=1, source_target_pairs={{0,3},{1,0},{2,1},{3,2},{4,7},{5,4},{6,5},{7,6},{8,11},{9,8},{10,9... | collective-permute-start | bytes 1966088 | tf_op jit(solution)/shard_map/ppermute | solution.py:53
  91.2 9.7 %collective-permute-done.2 = f32[32,5120]{1,0:T(8,128)S(1)} collective-permute-done((f32[32,5120]{1,0:T(8,128)S(1)}, f32[32,5120]{1,0:T(8,128)S(1)}, u32[]{:S(2)}, u32[]{:S(2)}) %collective-permute-start.2) | collective-permute-done | bytes 655392 | tf_op jit(solution)/shard_map/ppermute | solution.py:52
  100.9 0.3 broadcast_in_dim.100
  101.2 1.2 bitcast_dynamic-update-slice_fusion.7
  102.5 1.5 copy-done.5
  104.0 2.6 %collective-permute-start.7 = (bf16[32,5120]{1,0:T(8,128)(2,1)S(1)}, bf16[32,5120]{1,0:T(8,128)(2,1)}, u32[]{:S(2)}, u32[]{:S(2)}) collective-permute-start(bf16[32,5120]{1,0:T(8,128)(2,1)S(1)} %get-tuple-element.10), channel_id=1, source_target_pairs={{0,3},{1,0},{2,1},{3,2},{4,7},{5,4},{6,5},{7,6},{8,11},{9,8},{10,9... | collective-permute-start | bytes 983048 | tf_op jit(solution)/shard_map/ppermute | solution.py:61
  106.6 0.7 broadcast_select_fusion.2
  107.3 14.2 %all-to-all-start.1 = ((f32[64,1,4]{2,1,0:T(1,128)}), f32[64,1,4]{2,1,0:T(1,128)S(1)}, u32[]{:S(2)}, u32[]{:S(2)}) async-start(f32[64,1,4]{2,1,0:T(1,128)} %bitcast.38), calls=%async_computation.1 | async-start | bytes 65536 | tf_op jit(solution)/shard_map/all_to_all | solution.py:98
  121.6 0.7 fusion.21
  122.3 8.6 %all-to-all-done.1 = f32[64,1,4]{2,1,0:T(1,128)S(1)} async-done(((f32[64,1,4]{2,1,0:T(1,128)}), f32[64,1,4]{2,1,0:T(1,128)S(1)}, u32[]{:S(2)}, u32[]{:S(2)}) %all-to-all-start.1) | async-done | bytes 1056 | tf_op jit(solution)/shard_map/all_to_all | solution.py:98
  130.9 1.8 %gather_fusion.5 = f32[128]{0:T(128)} fusion(f32[64,4]{1,0:T(8,128)S(1)} %bitcast.125, s32[128]{0:T(128)S(1)} %fusion.21), kind=kCustom, calls=%fused_computation.5 | custom fusion | bytes 2048 | tf_op jit(solution)/shard_map/gather | solution.py:101
  132.7 2.7 %collective-permute-start.9 = (bf16[32,5120]{1,0:T(8,128)(2,1)}, bf16[32,5120]{1,0:T(8,128)(2,1)S(1)}, u32[]{:S(2)}, u32[]{:S(2)}) collective-permute-start(bf16[32,5120]{1,0:T(8,128)(2,1)} %collective-permute-done.7), channel_id=1, source_target_pairs={{0,3},{1,0},{2,1},{3,2},{4,7},{5,4},{6,5},{7,6},{8,11},{9,8},{10,9... | collective-permute-start | bytes 983048 | tf_op jit(solution)/shard_map/ppermute | solution.py:61
  135.4 1.7 %bitcast_dynamic-update-slice_fusion.5 = bf16[8,32,5120]{2,1,0:T(8,128)(2,1)} fusion(bf16[8,32,5120]{2,1,0:T(8,128)(2,1)} %copy-done.5, s32[]{:T(128)S(6)} %select_n.300, bf16[32,5120]{1,0:T(8,128)(2,1)} %collective-permute-done.6), kind=kLoop, calls=%fused_computation.32 | loop fusion | bytes 655364 | tf_op jit(solution)/shard_map/jit(dynamic_update_index_in_dim)/dynamic_update_slice | solution.py:66
  137.1 1.7 %bitcast_dynamic-update-slice_fusion.4 = bf16[8,32,5120]{2,1,0:T(8,128)(2,1)} fusion(bf16[8,32,5120]{2,1,0:T(8,128)(2,1)} %bitcast_dynamic-update-slice_fusion.5, s32[]{:T(128)S(6)} %select_n.301, bf16[32,5120]{1,0:T(8,128)(2,1)} %collective-permute-done.7), kind=kLoop, calls=%fused_computation.31 | loop fusion | bytes 655364 | tf_op jit(solution)/shard_map/jit(dynamic_update_index_in_dim)/dynamic_update_slice | solution.py:67
  138.8 3.9 %collective-permute-done.8 = bf16[32,5120]{1,0:T(8,128)(2,1)S(1)} collective-permute-done((bf16[32,5120]{1,0:T(8,128)(2,1)}, bf16[32,5120]{1,0:T(8,128)(2,1)S(1)}, u32[]{:S(2)}, u32[]{:S(2)}) %collective-permute-start.8) | collective-permute-done | bytes 327712 | tf_op jit(solution)/shard_map/ppermute | solution.py:60
  142.7 2.7 %collective-permute-start.11 = (bf16[32,5120]{1,0:T(8,128)(2,1)S(1)}, bf16[32,5120]{1,0:T(8,128)(2,1)S(1)}, u32[]{:S(2)}, u32[]{:S(2)}) collective-permute-start(bf16[32,5120]{1,0:T(8,128)(2,1)S(1)} %collective-permute-done.9), channel_id=1, source_target_pairs={{0,3},{1,0},{2,1},{3,2},{4,7},{5,4},{6,5},{7,6},{8,11},{9,8},{10,9... | collective-permute-start | bytes 983048 | tf_op jit(solution)/shard_map/ppermute | solution.py:61
  145.4 0.7 bitcast_dynamic-update-slice_fusion.3
  146.1 0.7 bitcast_dynamic-update-slice_fusion.2
  146.9 4.8 %collective-permute-done.10 = bf16[32,5120]{1,0:T(8,128)(2,1)S(1)} collective-permute-done((bf16[32,5120]{1,0:T(8,128)(2,1)S(1)}, bf16[32,5120]{1,0:T(8,128)(2,1)S(1)}, u32[]{:S(2)}, u32[]{:S(2)}) %collective-permute-start.10) | collective-permute-done | bytes 327712 | tf_op jit(solution)/shard_map/ppermute | solution.py:60
  151.7 0.7 bitcast_dynamic-update-slice_fusion.1
  152.4 0.7 bitcast_dynamic-update-slice_fusion
  (48 shorter events, 1.2 us)
Async XLA Ops:
  0.6 27.0 %copy-start = (bf16[256,5120]{1,0:T(8,128)(2,1)S(1)}, bf16[256,5120]{1,0:T(8,128)(2,1)}, u32[]{:S(2)}) copy-start(bf16[256,5120]{1,0:T(8,128)(2,1)} %param.5) | copy-start | bytes 7864324
  4.7 18.0 %copy-start.1 = (s32[64]{0:T(128)S(1)}, s32[64]{0:T(128)}, u32[]{:S(2)}) copy-start(s32[64]{0:T(128)} %param.7) | copy-start | bytes 772
  4.7 18.8 %copy-start.6 = (s32[64]{0:T(128)S(1)}, s32[64]{0:T(128)}, u32[]{:S(2)}) copy-start(s32[64]{0:T(128)} %param.6) | copy-start | bytes 772
  8.3 27.7 %all-to-all-start = ((bf16[64,4,768]{2,1,0:T(4,128)(2,1)}), bf16[64,4,768]{2,1,0:T(4,128)(2,1)S(1)}, u32[]{:S(2)}, u32[]{:S(2)}) async-start(bf16[64,4,768]{2,1,0:T(4,128)(2,1)} %broadcast_select_fusion.1), calls=%async_computation | async-start | bytes 786432 | tf_op jit(solution)/shard_map/all_to_all | solution.py:89
  56.6 1.9 %copy-start.2 = (f32[128,5120]{1,0:T(8,128)}, f32[128,5120]{1,0:T(8,128)S(1)}, u32[]{:S(2)}) copy-start(f32[128,5120]{1,0:T(8,128)S(1)} %get-tuple-element.15) | copy-start | bytes 7864324
  56.6 2.8 %copy-start.4 = (f32[128,5120]{1,0:T(8,128)}, f32[128,5120]{1,0:T(8,128)S(1)}, u32[]{:S(2)}) copy-start(f32[128,5120]{1,0:T(8,128)S(1)} %get-tuple-element.16) | copy-start | bytes 7864324
  57.6 14.5 %collective-permute-start = (f32[32,5120]{1,0:T(8,128)}, f32[32,5120]{1,0:T(8,128)}, u32[]{:S(2)}, u32[]{:S(2)}) collective-permute-start(f32[32,5120]{1,0:T(8,128)} %dynamic-slice_bitcast_fusion.1), channel_id=1, source_target_pairs={{0,1},{1,2},{2,3},{3,0},{4,5},{5,6},{6,7},{7,4},{8,9},{9,10},{10,1... | collective-permute-start | bytes 1966088 | tf_op jit(solution)/shard_map/ppermute | solution.py:52
  59.4 14.4 %collective-permute-start.3 = (f32[32,5120]{1,0:T(8,128)}, f32[32,5120]{1,0:T(8,128)S(1)}, u32[]{:S(2)}, u32[]{:S(2)}) collective-permute-start(f32[32,5120]{1,0:T(8,128)} %dynamic-slice_bitcast_fusion), channel_id=1, source_target_pairs={{0,3},{1,0},{2,1},{3,2},{4,7},{5,4},{6,5},{7,6},{8,11},{9,8},{10,9... | collective-permute-start | bytes 1966088 | tf_op jit(solution)/shard_map/ppermute | solution.py:53
  62.8 25.5 %copy-start.3 = (f32[128,5120]{1,0:T(8,128)S(1)}, f32[128,5120]{1,0:T(8,128)}, u32[]{:S(2)}) copy-start(f32[128,5120]{1,0:T(8,128)} %copy-done.2) | copy-start | bytes 7864324
  73.5 13.6 %collective-permute-start.1 = (f32[32,5120]{1,0:T(8,128)S(1)}, f32[32,5120]{1,0:T(8,128)S(1)}, u32[]{:S(2)}, u32[]{:S(2)}) collective-permute-start(f32[32,5120]{1,0:T(8,128)S(1)} %bitcast_add_fusion.5), channel_id=1, source_target_pairs={{0,1},{1,2},{2,3},{3,0},{4,5},{5,6},{6,7},{7,4},{8,9},{9,10},{10,1... | collective-permute-start | bytes 1966088 | tf_op jit(solution)/shard_map/ppermute | solution.py:52
  74.9 13.4 %collective-permute-start.4 = (f32[32,5120]{1,0:T(8,128)S(1)}, f32[32,5120]{1,0:T(8,128)S(1)}, u32[]{:S(2)}, u32[]{:S(2)}) collective-permute-start(f32[32,5120]{1,0:T(8,128)S(1)} %bitcast_add_fusion.2), channel_id=1, source_target_pairs={{0,3},{1,0},{2,1},{3,2},{4,7},{5,4},{6,5},{7,6},{8,11},{9,8},{10,9... | collective-permute-start | bytes 1966088 | tf_op jit(solution)/shard_map/ppermute | solution.py:53
  88.3 12.6 %collective-permute-start.2 = (f32[32,5120]{1,0:T(8,128)S(1)}, f32[32,5120]{1,0:T(8,128)S(1)}, u32[]{:S(2)}, u32[]{:S(2)}) collective-permute-start(f32[32,5120]{1,0:T(8,128)S(1)} %bitcast_add_fusion.4), channel_id=1, source_target_pairs={{0,1},{1,2},{2,3},{3,0},{4,5},{5,6},{6,7},{7,4},{8,9},{9,10},{10,1... | collective-permute-start | bytes 1966088 | tf_op jit(solution)/shard_map/ppermute | solution.py:52
  88.5 13.9 %collective-permute-start.5 = (f32[32,5120]{1,0:T(8,128)S(1)}, f32[32,5120]{1,0:T(8,128)S(1)}, u32[]{:S(2)}, u32[]{:S(2)}) collective-permute-start(f32[32,5120]{1,0:T(8,128)S(1)} %bitcast_add_fusion.1), channel_id=1, source_target_pairs={{0,3},{1,0},{2,1},{3,2},{4,7},{5,4},{6,5},{7,6},{8,11},{9,8},{10,9... | collective-permute-start | bytes 1966088 | tf_op jit(solution)/shard_map/ppermute | solution.py:53
  102.3 30.4 %collective-permute-start.6 = (bf16[32,5120]{1,0:T(8,128)(2,1)S(1)}, bf16[32,5120]{1,0:T(8,128)(2,1)}, u32[]{:S(2)}, u32[]{:S(2)}) collective-permute-start(bf16[32,5120]{1,0:T(8,128)(2,1)S(1)} %get-tuple-element.12), channel_id=1, source_target_pairs={{0,1},{1,2},{2,3},{3,0},{4,5},{5,6},{6,7},{7,4},{8,9},{9,10},{10,1... | collective-permute-start | bytes 983048 | tf_op jit(solution)/shard_map/ppermute | solution.py:60
  102.5 1.5 copy-start.5
  104.0 28.7 %collective-permute-start.7 = (bf16[32,5120]{1,0:T(8,128)(2,1)S(1)}, bf16[32,5120]{1,0:T(8,128)(2,1)}, u32[]{:S(2)}, u32[]{:S(2)}) collective-permute-start(bf16[32,5120]{1,0:T(8,128)(2,1)S(1)} %get-tuple-element.10), channel_id=1, source_target_pairs={{0,3},{1,0},{2,1},{3,2},{4,7},{5,4},{6,5},{7,6},{8,11},{9,8},{10,9... | collective-permute-start | bytes 983048 | tf_op jit(solution)/shard_map/ppermute | solution.py:61
  107.3 23.6 %all-to-all-start.1 = ((f32[64,1,4]{2,1,0:T(1,128)}), f32[64,1,4]{2,1,0:T(1,128)S(1)}, u32[]{:S(2)}, u32[]{:S(2)}) async-start(f32[64,1,4]{2,1,0:T(1,128)} %bitcast.38), calls=%async_computation.1 | async-start | bytes 65536 | tf_op jit(solution)/shard_map/all_to_all | solution.py:98
  132.7 10.0 %collective-permute-start.8 = (bf16[32,5120]{1,0:T(8,128)(2,1)}, bf16[32,5120]{1,0:T(8,128)(2,1)S(1)}, u32[]{:S(2)}, u32[]{:S(2)}) collective-permute-start(bf16[32,5120]{1,0:T(8,128)(2,1)} %collective-permute-done.6), channel_id=1, source_target_pairs={{0,1},{1,2},{2,3},{3,0},{4,5},{5,6},{6,7},{7,4},{8,9},{9,10},{10,1... | collective-permute-start | bytes 983048 | tf_op jit(solution)/shard_map/ppermute | solution.py:60
  132.7 10.0 %collective-permute-start.9 = (bf16[32,5120]{1,0:T(8,128)(2,1)}, bf16[32,5120]{1,0:T(8,128)(2,1)S(1)}, u32[]{:S(2)}, u32[]{:S(2)}) collective-permute-start(bf16[32,5120]{1,0:T(8,128)(2,1)} %collective-permute-done.7), channel_id=1, source_target_pairs={{0,3},{1,0},{2,1},{3,2},{4,7},{5,4},{6,5},{7,6},{8,11},{9,8},{10,9... | collective-permute-start | bytes 983048 | tf_op jit(solution)/shard_map/ppermute | solution.py:61
  142.7 9.0 %collective-permute-start.10 = (bf16[32,5120]{1,0:T(8,128)(2,1)S(1)}, bf16[32,5120]{1,0:T(8,128)(2,1)S(1)}, u32[]{:S(2)}, u32[]{:S(2)}) collective-permute-start(bf16[32,5120]{1,0:T(8,128)(2,1)S(1)} %collective-permute-done.8), channel_id=1, source_target_pairs={{0,1},{1,2},{2,3},{3,0},{4,5},{5,6},{6,7},{7,4},{8,9},{9,10},{10,1... | collective-permute-start | bytes 983048 | tf_op jit(solution)/shard_map/ppermute | solution.py:60
  142.7 9.7 %collective-permute-start.11 = (bf16[32,5120]{1,0:T(8,128)(2,1)S(1)}, bf16[32,5120]{1,0:T(8,128)(2,1)S(1)}, u32[]{:S(2)}, u32[]{:S(2)}) collective-permute-start(bf16[32,5120]{1,0:T(8,128)(2,1)S(1)} %collective-permute-done.9), channel_id=1, source_target_pairs={{0,3},{1,0},{2,1},{3,2},{4,7},{5,4},{6,5},{7,6},{8,11},{9,8},{10,9... | collective-permute-start | bytes 983048 | tf_op jit(solution)/shard_map/ppermute | solution.py:61

commit v6 on v5

--- a/solution.py
+++ b/solution.py
@@ -14,7 +14,9 @@
     own_total = jnp.sum(jnp.exp(logits - own_top[:, None]), axis=1)
     own_mass = jnp.sum(teacher_prob, axis=1)
     own_cross = jnp.sum(teacher_prob * (log_teacher - logits), axis=1)
-    stats = lax.all_gather(jnp.stack([own_top, own_total, own_mass, own_cross]), "vocab")
+    mine = lax.axis_index("vocab") == jnp.arange(lax.axis_size("vocab"), dtype=jnp.int32)
+    local = jnp.stack([own_top, own_total, own_mass, own_cross])
+    stats = lax.psum(jnp.where(mine[:, None, None], local[None], 0.0), "vocab")
     tops, totals, masses, crosses = stats[:, 0], stats[:, 1], stats[:, 2], stats[:, 3]
     row_top = jnp.max(tops, axis=0)
     exp_total = jnp.sum(totals * jnp.exp(tops - row_top[None, :]), axis=0)
@@ -83,18 +85,18 @@
     first_col = (inverse[myself] - offsets) % shards
     first_slot = (offsets + first_col) // shards
     send_rows = jnp.minimum(first_slot[:, None] + depth[None, :], balanced - 1)
-    outgoing = jnp.take(teacher_logprobs, send_rows.reshape(-1), axis=0).reshape(
+    outgoing = jnp.take(teacher_logprobs, send_rows.reshape(-1), axis=0, mode="clip").reshape(
         shards, slot_depth, teacher_logprobs.shape[1]
     )
     arriving = lax.all_to_all(outgoing, "dp", split_axis=0, concat_axis=0, tiled=True)
     own_offset = offsets[myself]
     shard_at = shard_of_class[(own_offset + classes) % shards]
-    teacher_slots = jnp.take(arriving, shard_at, axis=0)
+    teacher_slots = jnp.take(arriving, shard_at, axis=0, mode="clip")
     teacher_slots = jnp.transpose(teacher_slots, (1, 0, 2)).reshape(source_slots, -1)
     live = jnp.arange(source_slots, dtype=jnp.int32) < plan_lengths[myself]
     row_grad, row_div = divergence(hidden_rows, teacher_slots, live, head_weight)
     column_of = (inverse - own_offset) % shards
-    div_out = jnp.take(row_div.reshape(slot_depth, shards), column_of, axis=1).T
+    div_out = jnp.take(row_div.reshape(slot_depth, shards), column_of, axis=1, mode="clip").T
     div_in = lax.all_to_all(div_out, "dp", split_axis=0, concat_axis=0, tiled=True)
     packed = jnp.arange(balanced, dtype=jnp.int32) * shards + inverse[myself]
     owner = jnp.sum((offsets[None, :] <= packed[:, None]).astype(jnp.int32), axis=1) - 1

time: 154 us -> 157 us (1.019)
  blocking collectives: 9.48 us -> 13.1 us
  other arithmetic: 16.9 us -> 14.3 us
  local copies, waits for them, and re-layouts: 21.7 us -> 23.7 us
    psum x0 -> x1, blocking collectives: none -> 13.1 us  [divergence(): stats = lax.psum(jnp.where(mine[:, None, None], local[None], 0.0), 'vocab')]
    all_gather x1 -> x0, blocking collectives: 9.48 us -> none  [divergence(): lax.all_gather(jnp.stack([own_top, own_total, own_mass, own_cross]), 'voc...]
    select_n x5 -> x2, other arithmetic: 2.36 us -> 0.73 us  [the longest x1 0.66 us: body(): column_of = (inverse - own_offset) % shards]
    gather x4 -> x3, local copies, waits for them, and re-layouts: 3.97 us -> 4.45 us  [the longest x1 2.35 us: body(): jnp.take(teacher_logprobs, send_rows.reshape(-1), axis=0, mode='clip')]
  transfers between devices with their start and end apart: 14 -> 14, of which waited for: 7 -> 7; matrix products, arithmetic and copies ran while one was open for 19% -> 18% of each run, Pallas kernels for 0% -> 0%
where the time goes in v6:
time: 157 us; the launch traced here: 156 us
  waiting for transfers between devices  47.5 us (30%)
  starting transfers between devices  44.1 us (28%)
  local copies, waits for them, and re-layouts  23.7 us (15%)
  other arithmetic  14.3 us (9%)
  blocking collectives  13.1 us (8%)
  matrix products  11.8 us (8%)
    ppermute x6, waiting for transfers between devices, ring_all_reduce(): up = lax.ppermute(up, 'vocab', forward)  36 us
    ppermute x6, starting transfers between devices, ring_all_reduce(): down = lax.ppermute(down, 'vocab', backward)  15.4 us
    all_to_all x1, starting transfers between devices, body(): lax.all_to_all(div_out, 'dp', split_axis=0, concat_axis=0, tiled=True)  15.3 us
    all_to_all x1, starting transfers between devices, body(): lax.all_to_all(outgoing, 'dp', split_axis=0, concat_axis=0, tiled=True)  13.1 us
    psum x1, blocking collectives, divergence(): stats = lax.psum(jnp.where(mine[:, None, None], local[None], 0.0), 'vocab')  13.1 us
    all_to_all x1, waiting for transfers between devices, body(): lax.all_to_all(div_out, 'dp', split_axis=0, concat_axis=0, tiled=True)  8.61 us
    dot_general x1, matrix products, divergence(): logits = jnp.dot(row_block, weight, preferred_element_type=jnp.float32)  6.3 us
    dot_general x1, matrix products, divergence(): lax.dot_general(grad_logits, weight, (((1,), (1,)), ((), ())), preferred_...  5.52 us
  transfers between devices with their start and end apart: 14, of which 7 were waited for; matrix products, arithmetic and copies ran while one was open for 18% of the time, Pallas kernels for 0%

profile of v6, /device:TPU:1, one launch (start us, length us, event | category | flops | bytes accessed | tf_op | source)
XLA Modules:
  0.0 155.7 jit_solution(5877472637724044494)
XLA Ops:
  0.6 0.9 select_reduce_fusion
  1.6 0.8 copy.24
  2.3 0.1 reduce-window.9
  2.4 0.1 reduce.5
  2.5 0.6 dynamic_slice.36
  3.1 1.3 and_select_fusion.3
  4.5 0.1 reshape.299
  4.7 2.4 %gather_fusion = bf16[256,768]{1,0:T(8,128)(2,1)S(1)} fusion(bf16[128,768]{1,0:T(8,128)(2,1)} %param.9, s32[1024]{0:T(1024)S(1)} %pad_clamp_fusion.4), kind=kCustom, calls=%fused_computation | custom fusion | bytes 787456 | tf_op jit(solution)/shard_map/jit(_take)/gather | solution.py:88
  7.0 0.8 reshape.294
  7.8 13.1 %all-to-all-start = ((bf16[64,4,768]{2,1,0:T(4,128)(2,1)}), bf16[64,4,768]{2,1,0:T(4,128)(2,1)S(1)}, u32[]{:S(2)}, u32[]{:S(2)}) async-start(bf16[64,4,768]{2,1,0:T(4,128)(2,1)} %reshape.294), calls=%async_computation | async-start | bytes 786432 | tf_op jit(solution)/shard_map/all_to_all | solution.py:91
  21.0 0.6 dynamic_slice.35
  21.6 0.6 multiply_add_fusion.1
  22.2 0.6 dynamic_slice.37
  22.8 0.7 fusion.10
  23.5 0.8 gather_fusion.1
  24.3 0.1 convert_reduce_fusion
  24.4 0.6 iota_compare_fusion.1
  25.1 1.2 gather_fusion.4
  26.4 6.3 %fusion.23 = (f32[256]{0:T(256)S(1)}, f32[256,768]{1,0:T(8,128)}) fusion(bf16[256,5120]{1,0:T(8,128)(2,1)S(1)} %copy-done, bf16[5120,768]{1,0:T(8,128)(2,1)} %param.8), kind=kOutput, calls=%fused_computation.92 | convolution fusion | flops 2013462272 | bytes 11273216 | tf_op jit(solution)/shard_map/dot_general | solution.py:10
  32.7 2.8 %all-to-all-done = bf16[64,4,768]{2,1,0:T(4,128)(2,1)S(1)} async-done(((bf16[64,4,768]{2,1,0:T(4,128)(2,1)}), bf16[64,4,768]{2,1,0:T(4,128)(2,1)S(1)}, u32[]{:S(2)}, u32[]{:S(2)}) %all-to-all-start) | async-done | bytes 393248 | tf_op jit(solution)/shard_map/all_to_all | solution.py:91
  35.5 0.9 gather_fusion.2
  36.5 0.3 fusion
  36.9 0.2 copy.26
  37.1 0.1 stack.17
  37.2 1.5 exponential_reduce_fusion
  38.8 13.1 %psum.7 = f32[4,4,256]{2,0,1:T(4,128)S(1)} all-reduce(f32[4,4,256]{2,0,1:T(4,128)S(1)} %broadcast_select_fusion), channel_id=1, replica_groups=mesh['dp'=64,'vocab'=4] {'vocab'}, use_global_device_ids=true, to_apply=%region_6.7 | all-reduce | flops 4096 | bytes 32768 | tf_op jit(solution)/shard_map/psum | solution.py:19
  52.0 1.4 select_convert_fusion
  53.4 5.5 %fusion.24 = f32[256,5120]{1,0:T(8,128)S(1)} fusion(bf16[256,768]{1,0:T(8,128)(2,1)S(1)} %select_convert_fusion, bf16[5120,768]{1,0:T(8,128)(2,1)} %param.8), kind=kOutput, calls=%fused_computation.93 | convolution fusion | flops 2013265920 | bytes 13500416 | tf_op jit(solution)/shard_map/dot_general | solution.py:32
  59.0 0.5 fusion.22
  59.5 1.0 dynamic-slice_bitcast_fusion.1
  60.5 0.7 copy-done.2
  61.2 1.1 dynamic-slice_bitcast_fusion
  62.3 1.8 %collective-permute-start.3 = (f32[32,5120]{1,0:T(8,128)}, f32[32,5120]{1,0:T(8,128)S(1)}, u32[]{:S(2)}, u32[]{:S(2)}) collective-permute-start(f32[32,5120]{1,0:T(8,128)} %dynamic-slice_bitcast_fusion), channel_id=1, source_target_pairs={{0,3},{1,0},{2,1},{3,2},{4,7},{5,4},{6,5},{7,6},{8,11},{9,8},{10,9... | collective-permute-start | bytes 1966088 | tf_op jit(solution)/shard_map/ppermute | solution.py:55
  64.2 0.1 copy.27
  64.3 9.9 %collective-permute-done = f32[32,5120]{1,0:T(8,128)} collective-permute-done((f32[32,5120]{1,0:T(8,128)}, f32[32,5120]{1,0:T(8,128)}, u32[]{:S(2)}, u32[]{:S(2)}) %collective-permute-start) | collective-permute-done | bytes 655392 | tf_op jit(solution)/shard_map/ppermute | solution.py:54
  74.2 1.4 bitcast_add_fusion.5
  75.5 0.1 collective-permute-start.1
  75.6 1.2 bitcast_add_fusion.2
  76.8 2.9 %collective-permute-start.4 = (f32[32,5120]{1,0:T(8,128)S(1)}, f32[32,5120]{1,0:T(8,128)S(1)}, u32[]{:S(2)}, u32[]{:S(2)}) collective-permute-start(f32[32,5120]{1,0:T(8,128)S(1)} %bitcast_add_fusion.2), channel_id=1, source_target_pairs={{0,3},{1,0},{2,1},{3,2},{4,7},{5,4},{6,5},{7,6},{8,11},{9,8},{10,9... | collective-permute-start | bytes 1966088 | tf_op jit(solution)/shard_map/ppermute | solution.py:55
  79.7 8.4 %collective-permute-done.1 = f32[32,5120]{1,0:T(8,128)S(1)} collective-permute-done((f32[32,5120]{1,0:T(8,128)S(1)}, f32[32,5120]{1,0:T(8,128)S(1)}, u32[]{:S(2)}, u32[]{:S(2)}) %collective-permute-start.1) | collective-permute-done | bytes 655392 | tf_op jit(solution)/shard_map/ppermute | solution.py:54
  88.1 1.2 bitcast_add_fusion.4
  89.5 2.7 %collective-permute-start.5 = (f32[32,5120]{1,0:T(8,128)S(1)}, f32[32,5120]{1,0:T(8,128)S(1)}, u32[]{:S(2)}, u32[]{:S(2)}) collective-permute-start(f32[32,5120]{1,0:T(8,128)S(1)} %bitcast_add_fusion.1), channel_id=1, source_target_pairs={{0,3},{1,0},{2,1},{3,2},{4,7},{5,4},{6,5},{7,6},{8,11},{9,8},{10,9... | collective-permute-start | bytes 1966088 | tf_op jit(solution)/shard_map/ppermute | solution.py:55
  92.2 9.1 %collective-permute-done.2 = f32[32,5120]{1,0:T(8,128)S(1)} collective-permute-done((f32[32,5120]{1,0:T(8,128)S(1)}, f32[32,5120]{1,0:T(8,128)S(1)}, u32[]{:S(2)}, u32[]{:S(2)}) %collective-permute-start.2) | collective-permute-done | bytes 655392 | tf_op jit(solution)/shard_map/ppermute | solution.py:54
  101.3 0.3 broadcast_in_dim.102
  101.6 1.2 bitcast_dynamic-update-slice_fusion.7
  102.7 0.1 collective-permute-start.6
  102.9 1.5 copy-done.5
  104.4 2.6 %collective-permute-start.7 = (bf16[32,5120]{1,0:T(8,128)(2,1)S(1)}, bf16[32,5120]{1,0:T(8,128)(2,1)}, u32[]{:S(2)}, u32[]{:S(2)}) collective-permute-start(bf16[32,5120]{1,0:T(8,128)(2,1)S(1)} %get-tuple-element.10), channel_id=1, source_target_pairs={{0,3},{1,0},{2,1},{3,2},{4,7},{5,4},{6,5},{7,6},{8,11},{9,8},{10,9... | collective-permute-start | bytes 983048 | tf_op jit(solution)/shard_map/ppermute | solution.py:63
  107.1 0.6 fusion.5
  107.6 1.2 gather_fusion.3
  108.8 15.3 %all-to-all-start.1 = ((f32[64,1,4]{2,1,0:T(1,128)}), f32[64,1,4]{2,1,0:T(1,128)S(1)}, u32[]{:S(2)}, u32[]{:S(2)}) async-start(f32[64,1,4]{2,1,0:T(1,128)} %bitcast.35), calls=%async_computation.1 | async-start | bytes 65536 | tf_op jit(solution)/shard_map/all_to_all | solution.py:100
  124.1 0.7 fusion.18
  124.8 8.6 %all-to-all-done.1 = f32[64,1,4]{2,1,0:T(1,128)S(1)} async-done(((f32[64,1,4]{2,1,0:T(1,128)}), f32[64,1,4]{2,1,0:T(1,128)S(1)}, u32[]{:S(2)}, u32[]{:S(2)}) %all-to-all-start.1) | async-done | bytes 1056 | tf_op jit(solution)/shard_map/all_to_all | solution.py:100
  133.4 1.8 %gather_fusion.5 = f32[128]{0:T(128)} fusion(f32[64,4]{1,0:T(8,128)S(1)} %bitcast.118, s32[128]{0:T(128)S(1)} %fusion.18), kind=kCustom, calls=%fused_computation.5 | custom fusion | bytes 2048 | tf_op jit(solution)/shard_map/gather | solution.py:103
  135.2 2.7 %collective-permute-start.9 = (bf16[32,5120]{1,0:T(8,128)(2,1)}, bf16[32,5120]{1,0:T(8,128)(2,1)S(1)}, u32[]{:S(2)}, u32[]{:S(2)}) collective-permute-start(bf16[32,5120]{1,0:T(8,128)(2,1)} %collective-permute-done.7), channel_id=1, source_target_pairs={{0,3},{1,0},{2,1},{3,2},{4,7},{5,4},{6,5},{7,6},{8,11},{9,8},{10,9... | collective-permute-start | bytes 983048 | tf_op jit(solution)/shard_map/ppermute | solution.py:63
  137.9 1.7 %bitcast_dynamic-update-slice_fusion.5 = bf16[8,32,5120]{2,1,0:T(8,128)(2,1)} fusion(bf16[8,32,5120]{2,1,0:T(8,128)(2,1)} %copy-done.5, s32[]{:T(128)S(6)} %select_n.229, bf16[32,5120]{1,0:T(8,128)(2,1)} %collective-permute-done.6), kind=kLoop, calls=%fused_computation.30 | loop fusion | bytes 655364 | tf_op jit(solution)/shard_map/jit(dynamic_update_index_in_dim)/dynamic_update_slice | solution.py:68
  139.6 1.7 %bitcast_dynamic-update-slice_fusion.4 = bf16[8,32,5120]{2,1,0:T(8,128)(2,1)} fusion(bf16[8,32,5120]{2,1,0:T(8,128)(2,1)} %bitcast_dynamic-update-slice_fusion.5, s32[]{:T(128)S(6)} %select_n.230, bf16[32,5120]{1,0:T(8,128)(2,1)} %collective-permute-done.7), kind=kLoop, calls=%fused_computation.29 | loop fusion | bytes 655364 | tf_op jit(solution)/shard_map/jit(dynamic_update_index_in_dim)/dynamic_update_slice | solution.py:69
  141.3 3.9 %collective-permute-done.8 = bf16[32,5120]{1,0:T(8,128)(2,1)S(1)} collective-permute-done((bf16[32,5120]{1,0:T(8,128)(2,1)}, bf16[32,5120]{1,0:T(8,128)(2,1)S(1)}, u32[]{:S(2)}, u32[]{:S(2)}) %collective-permute-start.8) | collective-permute-done | bytes 327712 | tf_op jit(solution)/shard_map/ppermute | solution.py:62
  145.2 2.7 %collective-permute-start.11 = (bf16[32,5120]{1,0:T(8,128)(2,1)S(1)}, bf16[32,5120]{1,0:T(8,128)(2,1)S(1)}, u32[]{:S(2)}, u32[]{:S(2)}) collective-permute-start(bf16[32,5120]{1,0:T(8,128)(2,1)S(1)} %collective-permute-done.9), channel_id=1, source_target_pairs={{0,3},{1,0},{2,1},{3,2},{4,7},{5,4},{6,5},{7,6},{8,11},{9,8},{10,9... | collective-permute-start | bytes 983048 | tf_op jit(solution)/shard_map/ppermute | solution.py:63
  147.9 0.7 bitcast_dynamic-update-slice_fusion.3
  148.6 0.7 bitcast_dynamic-update-slice_fusion.2
  149.4 4.8 %collective-permute-done.10 = bf16[32,5120]{1,0:T(8,128)(2,1)S(1)} collective-permute-done((bf16[32,5120]{1,0:T(8,128)(2,1)S(1)}, bf16[32,5120]{1,0:T(8,128)(2,1)S(1)}, u32[]{:S(2)}, u32[]{:S(2)}) %collective-permute-start.10) | collective-permute-done | bytes 327712 | tf_op jit(solution)/shard_map/ppermute | solution.py:62
  154.2 0.7 bitcast_dynamic-update-slice_fusion.1
  154.9 0.7 bitcast_dynamic-update-slice_fusion
  (41 shorter events, 0.8 us)
Async XLA Ops:
  0.6 25.8 %copy-start = (bf16[256,5120]{1,0:T(8,128)(2,1)S(1)}, bf16[256,5120]{1,0:T(8,128)(2,1)}, u32[]{:S(2)}) copy-start(bf16[256,5120]{1,0:T(8,128)(2,1)} %param.5) | copy-start | bytes 7864324
  2.4 18.6 %copy-start.6 = (s32[64]{0:T(128)S(1)}, s32[64]{0:T(128)}, u32[]{:S(2)}) copy-start(s32[64]{0:T(128)} %param.6) | copy-start | bytes 772
  2.4 21.1 %copy-start.1 = (s32[64]{0:T(128)S(1)}, s32[64]{0:T(128)}, u32[]{:S(2)}) copy-start(s32[64]{0:T(128)} %param.7) | copy-start | bytes 772
  7.8 27.7 %all-to-all-start = ((bf16[64,4,768]{2,1,0:T(4,128)(2,1)}), bf16[64,4,768]{2,1,0:T(4,128)(2,1)S(1)}, u32[]{:S(2)}, u32[]{:S(2)}) async-start(bf16[64,4,768]{2,1,0:T(4,128)(2,1)} %reshape.294), calls=%async_computation | async-start | bytes 786432 | tf_op jit(solution)/shard_map/all_to_all | solution.py:91
  59.5 1.7 %copy-start.2 = (f32[128,5120]{1,0:T(8,128)}, f32[128,5120]{1,0:T(8,128)S(1)}, u32[]{:S(2)}) copy-start(f32[128,5120]{1,0:T(8,128)S(1)} %get-tuple-element.15) | copy-start | bytes 7864324
  59.5 2.8 %copy-start.4 = (f32[128,5120]{1,0:T(8,128)}, f32[128,5120]{1,0:T(8,128)S(1)}, u32[]{:S(2)}) copy-start(f32[128,5120]{1,0:T(8,128)S(1)} %get-tuple-element.16) | copy-start | bytes 7864324
  60.5 13.7 %collective-permute-start = (f32[32,5120]{1,0:T(8,128)}, f32[32,5120]{1,0:T(8,128)}, u32[]{:S(2)}, u32[]{:S(2)}) collective-permute-start(f32[32,5120]{1,0:T(8,128)} %dynamic-slice_bitcast_fusion.1), channel_id=1, source_target_pairs={{0,1},{1,2},{2,3},{3,0},{4,5},{5,6},{6,7},{7,4},{8,9},{9,10},{10,1... | collective-permute-start | bytes 1966088 | tf_op jit(solution)/shard_map/ppermute | solution.py:54
  62.3 13.3 %collective-permute-start.3 = (f32[32,5120]{1,0:T(8,128)}, f32[32,5120]{1,0:T(8,128)S(1)}, u32[]{:S(2)}, u32[]{:S(2)}) collective-permute-start(f32[32,5120]{1,0:T(8,128)} %dynamic-slice_bitcast_fusion), channel_id=1, source_target_pairs={{0,3},{1,0},{2,1},{3,2},{4,7},{5,4},{6,5},{7,6},{8,11},{9,8},{10,9... | collective-permute-start | bytes 1966088 | tf_op jit(solution)/shard_map/ppermute | solution.py:55
  64.2 25.1 %copy-start.3 = (f32[128,5120]{1,0:T(8,128)S(1)}, f32[128,5120]{1,0:T(8,128)}, u32[]{:S(2)}) copy-start(f32[128,5120]{1,0:T(8,128)} %copy-done.2) | copy-start | bytes 7864324
  75.5 12.6 %collective-permute-start.1 = (f32[32,5120]{1,0:T(8,128)S(1)}, f32[32,5120]{1,0:T(8,128)S(1)}, u32[]{:S(2)}, u32[]{:S(2)}) collective-permute-start(f32[32,5120]{1,0:T(8,128)S(1)} %bitcast_add_fusion.5), channel_id=1, source_target_pairs={{0,1},{1,2},{2,3},{3,0},{4,5},{5,6},{6,7},{7,4},{8,9},{9,10},{10,1... | collective-permute-start | bytes 1966088 | tf_op jit(solution)/shard_map/ppermute | solution.py:54
  76.8 12.5 %collective-permute-start.4 = (f32[32,5120]{1,0:T(8,128)S(1)}, f32[32,5120]{1,0:T(8,128)S(1)}, u32[]{:S(2)}, u32[]{:S(2)}) collective-permute-start(f32[32,5120]{1,0:T(8,128)S(1)} %bitcast_add_fusion.2), channel_id=1, source_target_pairs={{0,3},{1,0},{2,1},{3,2},{4,7},{5,4},{6,5},{7,6},{8,11},{9,8},{10,9... | collective-permute-start | bytes 1966088 | tf_op jit(solution)/shard_map/ppermute | solution.py:55
  89.3 12.0 %collective-permute-start.2 = (f32[32,5120]{1,0:T(8,128)S(1)}, f32[32,5120]{1,0:T(8,128)S(1)}, u32[]{:S(2)}, u32[]{:S(2)}) collective-permute-start(f32[32,5120]{1,0:T(8,128)S(1)} %bitcast_add_fusion.4), channel_id=1, source_target_pairs={{0,1},{1,2},{2,3},{3,0},{4,5},{5,6},{6,7},{7,4},{8,9},{9,10},{10,1... | collective-permute-start | bytes 1966088 | tf_op jit(solution)/shard_map/ppermute | solution.py:54
  89.5 13.4 %collective-permute-start.5 = (f32[32,5120]{1,0:T(8,128)S(1)}, f32[32,5120]{1,0:T(8,128)S(1)}, u32[]{:S(2)}, u32[]{:S(2)}) collective-permute-start(f32[32,5120]{1,0:T(8,128)S(1)} %bitcast_add_fusion.1), channel_id=1, source_target_pairs={{0,3},{1,0},{2,1},{3,2},{4,7},{5,4},{6,5},{7,6},{8,11},{9,8},{10,9... | collective-permute-start | bytes 1966088 | tf_op jit(solution)/shard_map/ppermute | solution.py:55
  102.7 32.5 %collective-permute-start.6 = (bf16[32,5120]{1,0:T(8,128)(2,1)S(1)}, bf16[32,5120]{1,0:T(8,128)(2,1)}, u32[]{:S(2)}, u32[]{:S(2)}) collective-permute-start(bf16[32,5120]{1,0:T(8,128)(2,1)S(1)} %get-tuple-element.12), channel_id=1, source_target_pairs={{0,1},{1,2},{2,3},{3,0},{4,5},{5,6},{6,7},{7,4},{8,9},{9,10},{10,1... | collective-permute-start | bytes 983048 | tf_op jit(solution)/shard_map/ppermute | solution.py:62
  102.9 1.5 copy-start.5
  104.4 30.8 %collective-permute-start.7 = (bf16[32,5120]{1,0:T(8,128)(2,1)S(1)}, bf16[32,5120]{1,0:T(8,128)(2,1)}, u32[]{:S(2)}, u32[]{:S(2)}) collective-permute-start(bf16[32,5120]{1,0:T(8,128)(2,1)S(1)} %get-tuple-element.10), channel_id=1, source_target_pairs={{0,3},{1,0},{2,1},{3,2},{4,7},{5,4},{6,5},{7,6},{8,11},{9,8},{10,9... | collective-permute-start | bytes 983048 | tf_op jit(solution)/shard_map/ppermute | solution.py:63
  108.8 24.6 %all-to-all-start.1 = ((f32[64,1,4]{2,1,0:T(1,128)}), f32[64,1,4]{2,1,0:T(1,128)S(1)}, u32[]{:S(2)}, u32[]{:S(2)}) async-start(f32[64,1,4]{2,1,0:T(1,128)} %bitcast.35), calls=%async_computation.1 | async-start | bytes 65536 | tf_op jit(solution)/shard_map/all_to_all | solution.py:100
  135.2 10.0 %collective-permute-start.8 = (bf16[32,5120]{1,0:T(8,128)(2,1)}, bf16[32,5120]{1,0:T(8,128)(2,1)S(1)}, u32[]{:S(2)}, u32[]{:S(2)}) collective-permute-start(bf16[32,5120]{1,0:T(8,128)(2,1)} %collective-permute-done.6), channel_id=1, source_target_pairs={{0,1},{1,2},{2,3},{3,0},{4,5},{5,6},{6,7},{7,4},{8,9},{9,10},{10,1... | collective-permute-start | bytes 983048 | tf_op jit(solution)/shard_map/ppermute | solution.py:62
  135.2 10.0 %collective-permute-start.9 = (bf16[32,5120]{1,0:T(8,128)(2,1)}, bf16[32,5120]{1,0:T(8,128)(2,1)S(1)}, u32[]{:S(2)}, u32[]{:S(2)}) collective-permute-start(bf16[32,5120]{1,0:T(8,128)(2,1)} %collective-permute-done.7), channel_id=1, source_target_pairs={{0,3},{1,0},{2,1},{3,2},{4,7},{5,4},{6,5},{7,6},{8,11},{9,8},{10,9... | collective-permute-start | bytes 983048 | tf_op jit(solution)/shard_map/ppermute | solution.py:63
  145.2 9.0 %collective-permute-start.10 = (bf16[32,5120]{1,0:T(8,128)(2,1)S(1)}, bf16[32,5120]{1,0:T(8,128)(2,1)S(1)}, u32[]{:S(2)}, u32[]{:S(2)}) collective-permute-start(bf16[32,5120]{1,0:T(8,128)(2,1)S(1)} %collective-permute-done.8), channel_id=1, source_target_pairs={{0,1},{1,2},{2,3},{3,0},{4,5},{5,6},{6,7},{7,4},{8,9},{9,10},{10,1... | collective-permute-start | bytes 983048 | tf_op jit(solution)/shard_map/ppermute | solution.py:62
  145.2 9.7 %collective-permute-start.11 = (bf16[32,5120]{1,0:T(8,128)(2,1)S(1)}, bf16[32,5120]{1,0:T(8,128)(2,1)S(1)}, u32[]{:S(2)}, u32[]{:S(2)}) collective-permute-start(bf16[32,5120]{1,0:T(8,128)(2,1)S(1)} %collective-permute-done.9), channel_id=1, source_target_pairs={{0,3},{1,0},{2,1},{3,2},{4,7},{5,4},{6,5},{7,6},{8,11},{9,8},{10,9... | collective-permute-start | bytes 983048 | tf_op jit(solution)/shard_map/ppermute | solution.py:63

commit v7 on v6

--- a/solution.py
+++ b/solution.py
@@ -14,9 +14,7 @@
     own_total = jnp.sum(jnp.exp(logits - own_top[:, None]), axis=1)
     own_mass = jnp.sum(teacher_prob, axis=1)
     own_cross = jnp.sum(teacher_prob * (log_teacher - logits), axis=1)
-    mine = lax.axis_index("vocab") == jnp.arange(lax.axis_size("vocab"), dtype=jnp.int32)
-    local = jnp.stack([own_top, own_total, own_mass, own_cross])
-    stats = lax.psum(jnp.where(mine[:, None, None], local[None], 0.0), "vocab")
+    stats = lax.all_gather(jnp.stack([own_top, own_total, own_mass, own_cross]), "vocab")
     tops, totals, masses, crosses = stats[:, 0], stats[:, 1], stats[:, 2], stats[:, 3]
     row_top = jnp.max(tops, axis=0)
     exp_total = jnp.sum(totals * jnp.exp(tops - row_top[None, :]), axis=0)
@@ -85,9 +83,7 @@
     first_col = (inverse[myself] - offsets) % shards
     first_slot = (offsets + first_col) // shards
     send_rows = jnp.minimum(first_slot[:, None] + depth[None, :], balanced - 1)
-    outgoing = jnp.take(teacher_logprobs, send_rows.reshape(-1), axis=0, mode="clip").reshape(
-        shards, slot_depth, teacher_logprobs.shape[1]
-    )
+    outgoing = jnp.take(teacher_logprobs, send_rows, axis=0, mode="clip")
     arriving = lax.all_to_all(outgoing, "dp", split_axis=0, concat_axis=0, tiled=True)
     own_offset = offsets[myself]
     shard_at = shard_of_class[(own_offset + classes) % shards]

time: 157 us -> 154 us (0.981)
  blocking collectives: 13.1 us -> 9.48 us
  waiting for transfers between devices: 47.5 us -> 49.5 us
    psum x1 -> x0, blocking collectives: 13.1 us -> none  [divergence(): stats = lax.psum(jnp.where(mine[:, None, None], local[None], 0.0), 'vocab')]
    all_gather x0 -> x1, blocking collectives: none -> 9.48 us  [divergence(): lax.all_gather(jnp.stack([own_top, own_total, own_mass, own_cross]), 'voc...]
    ppermute x6, waiting for transfers between devices: 36 us -> 38 us  [ring_all_reduce(): up = lax.ppermute(up, 'vocab', forward)]
    all_to_all x1, starting transfers between devices: 15.3 us -> 13.5 us  [body(): lax.all_to_all(div_out, 'dp', split_axis=0, concat_axis=0, tiled=True)]
    gather x1 -> x2, local copies, waits for them, and re-layouts: 2.35 us -> 3.18 us  [body(): outgoing = jnp.take(teacher_logprobs, send_rows, axis=0, mode='clip')]
where the time goes in v7:
time: 154 us; the launch traced here: 153 us
  waiting for transfers between devices  49.5 us (32%)
  starting transfers between devices  43.6 us (28%)
  local copies, waits for them, and re-layouts  22.8 us (15%)
  other arithmetic  14.3 us (9%)
  matrix products  11.8 us (8%)
  blocking collectives  9.48 us (6%)
    ppermute x6, waiting for transfers between devices, ring_all_reduce(): up = lax.ppermute(up, 'vocab', forward)  38 us
    ppermute x6, starting transfers between devices, ring_all_reduce(): down = lax.ppermute(down, 'vocab', backward)  15.7 us
    all_to_all x1, starting transfers between devices, body(): lax.all_to_all(div_out, 'dp', split_axis=0, concat_axis=0, tiled=True)  13.5 us
    all_to_all x1, starting transfers between devices, body(): lax.all_to_all(outgoing, 'dp', split_axis=0, concat_axis=0, tiled=True)  13.1 us
    all_gather x1, blocking collectives, divergence(): lax.all_gather(jnp.stack([own_top, own_total, own_mass, own_cross]), 'voc...  9.48 us
    all_to_all x1, waiting for transfers between devices, body(): lax.all_to_all(div_out, 'dp', split_axis=0, concat_axis=0, tiled=True)  8.61 us
    dot_general x1, matrix products, divergence(): logits = jnp.dot(row_block, weight, preferred_element_type=jnp.float32)  6.3 us
    dot_general x1, matrix products, divergence(): lax.dot_general(grad_logits, weight, (((1,), (1,)), ((), ())), preferred_...  5.51 us
  transfers between devices with their start and end apart: 14, of which 7 were waited for; matrix products, arithmetic and copies ran while one was open for 18% of the time, Pallas kernels for 0%

profile of v7, /device:TPU:1, one launch (start us, length us, event | category | flops | bytes accessed | tf_op | source)
XLA Modules:
  0.0 152.6 jit_solution(10255895930569797648)
XLA Ops:
  0.6 0.9 select_reduce_fusion
  1.6 0.8 copy.24
  2.3 0.1 reduce-window.9
  2.4 0.1 reduce.5
  2.5 0.6 dynamic_slice.36
  3.1 1.3 and_select_fusion.3
  4.5 0.1 reshape.294
  4.7 2.4 %gather_fusion = bf16[256,768]{1,0:T(8,128)(2,1)S(1)} fusion(bf16[128,768]{1,0:T(8,128)(2,1)} %param.9, s32[1024]{0:T(1024)S(1)} %pad_clamp_fusion.4), kind=kCustom, calls=%fused_computation | custom fusion | bytes 787456 | tf_op jit(solution)/shard_map/jit(_take)/gather | solution.py:86
  7.0 0.8 reshape.293
  7.9 13.1 %all-to-all-start = ((bf16[64,4,768]{2,1,0:T(4,128)(2,1)}), bf16[64,4,768]{2,1,0:T(4,128)(2,1)S(1)}, u32[]{:S(2)}, u32[]{:S(2)}) async-start(bf16[64,4,768]{2,1,0:T(4,128)(2,1)} %reshape.293), calls=%async_computation | async-start | bytes 786432 | tf_op jit(solution)/shard_map/all_to_all | solution.py:87
  21.0 0.6 dynamic_slice.35
  21.6 0.6 multiply_add_fusion.1
  22.3 0.6 dynamic_slice.37
  22.8 0.7 fusion.11
  23.5 0.8 gather_fusion.1
  24.3 0.1 convert_reduce_fusion
  24.4 0.6 iota_compare_fusion.1
  25.1 1.2 gather_fusion.4
  26.4 6.3 %fusion.25 = (f32[256]{0:T(256)S(1)}, f32[256,768]{1,0:T(8,128)}) fusion(bf16[256,5120]{1,0:T(8,128)(2,1)S(1)} %copy-done, bf16[5120,768]{1,0:T(8,128)(2,1)} %param.8), kind=kOutput, calls=%fused_computation.91 | convolution fusion | flops 2013462272 | bytes 11273216 | tf_op jit(solution)/shard_map/dot_general | solution.py:10
  32.7 2.8 %all-to-all-done = bf16[64,4,768]{2,1,0:T(4,128)(2,1)S(1)} async-done(((bf16[64,4,768]{2,1,0:T(4,128)(2,1)}), bf16[64,4,768]{2,1,0:T(4,128)(2,1)S(1)}, u32[]{:S(2)}, u32[]{:S(2)}) %all-to-all-start) | async-done | bytes 393248 | tf_op jit(solution)/shard_map/all_to_all | solution.py:87
  35.6 0.9 gather_fusion.2
  36.5 0.3 fusion
  36.9 0.2 copy.26
  37.1 0.1 stack.17
  37.2 1.5 %exponential_reduce_fusion = (f32[256]{0:T(256)S(1)}, f32[256]{0:T(256)S(1)}) fusion(f32[256,768]{1,0:T(8,128)} %get-tuple-element.23, f32[256]{0:T(256)S(1)} %get-tuple-element.22, f32[4,64,768]{2,1,0:T(8,128)S(1)} %copy.26), kind=kLoop, calls=%fused_computation.14 | loop fusion | flops 982528 | bytes 1575936 | tf_op jit(solution)/shard_map/reduce_sum | solution.py:14
  38.7 9.5 %all-gather.1 = f32[4,4,256]{2,1,0:T(4,128)S(1)} all-gather(f32[1,4,256]{2,1,0:T(4,128)S(1)} %maximum_bitcast_fusion), channel_id=2, replica_groups=mesh['dp'=64,'vocab'=4] {'vocab'}, dimensions={0}, use_global_device_ids=true | all-gather | bytes 20480 | tf_op jit(solution)/shard_map/all_gather | solution.py:17
  48.3 1.4 select_convert_fusion
  49.7 5.5 %fusion.26 = f32[256,5120]{1,0:T(8,128)S(1)} fusion(bf16[256,768]{1,0:T(8,128)(2,1)S(1)} %select_convert_fusion, bf16[5120,768]{1,0:T(8,128)(2,1)} %param.8), kind=kOutput, calls=%fused_computation.92 | convolution fusion | flops 2013265920 | bytes 13500416 | tf_op jit(solution)/shard_map/dot_general | solution.py:30
  55.3 0.5 fusion.23
  55.8 1.0 dynamic-slice_bitcast_fusion.1
  56.8 0.9 collective-permute-start
  57.7 0.9 dynamic-slice_bitcast_fusion
  58.6 2.1 %collective-permute-start.3 = (f32[32,5120]{1,0:T(8,128)}, f32[32,5120]{1,0:T(8,128)S(1)}, u32[]{:S(2)}, u32[]{:S(2)}) collective-permute-start(f32[32,5120]{1,0:T(8,128)} %dynamic-slice_bitcast_fusion), channel_id=1, source_target_pairs={{0,3},{1,0},{2,1},{3,2},{4,7},{5,4},{6,5},{7,6},{8,11},{9,8},{10,9... | collective-permute-start | bytes 1966088 | tf_op jit(solution)/shard_map/ppermute | solution.py:53
  60.8 0.1 copy.28
  60.9 10.4 %collective-permute-done = f32[32,5120]{1,0:T(8,128)} collective-permute-done((f32[32,5120]{1,0:T(8,128)}, f32[32,5120]{1,0:T(8,128)}, u32[]{:S(2)}, u32[]{:S(2)}) %collective-permute-start) | collective-permute-done | bytes 655392 | tf_op jit(solution)/shard_map/ppermute | solution.py:52
  71.3 1.4 bitcast_add_fusion.5
  72.7 0.1 collective-permute-start.1
  72.8 1.2 bitcast_add_fusion.2
  74.0 2.9 %collective-permute-start.4 = (f32[32,5120]{1,0:T(8,128)S(1)}, f32[32,5120]{1,0:T(8,128)S(1)}, u32[]{:S(2)}, u32[]{:S(2)}) collective-permute-start(f32[32,5120]{1,0:T(8,128)S(1)} %bitcast_add_fusion.2), channel_id=1, source_target_pairs={{0,3},{1,0},{2,1},{3,2},{4,7},{5,4},{6,5},{7,6},{8,11},{9,8},{10,9... | collective-permute-start | bytes 1966088 | tf_op jit(solution)/shard_map/ppermute | solution.py:53
  76.9 9.2 %collective-permute-done.1 = f32[32,5120]{1,0:T(8,128)S(1)} collective-permute-done((f32[32,5120]{1,0:T(8,128)S(1)}, f32[32,5120]{1,0:T(8,128)S(1)}, u32[]{:S(2)}, u32[]{:S(2)}) %collective-permute-start.1) | collective-permute-done | bytes 655392 | tf_op jit(solution)/shard_map/ppermute | solution.py:52
  86.1 1.2 bitcast_add_fusion.4
  87.5 2.7 %collective-permute-start.5 = (f32[32,5120]{1,0:T(8,128)S(1)}, f32[32,5120]{1,0:T(8,128)S(1)}, u32[]{:S(2)}, u32[]{:S(2)}) collective-permute-start(f32[32,5120]{1,0:T(8,128)S(1)} %bitcast_add_fusion.1), channel_id=1, source_target_pairs={{0,3},{1,0},{2,1},{3,2},{4,7},{5,4},{6,5},{7,6},{8,11},{9,8},{10,9... | collective-permute-start | bytes 1966088 | tf_op jit(solution)/shard_map/ppermute | solution.py:53
  90.2 9.7 %collective-permute-done.2 = f32[32,5120]{1,0:T(8,128)S(1)} collective-permute-done((f32[32,5120]{1,0:T(8,128)S(1)}, f32[32,5120]{1,0:T(8,128)S(1)}, u32[]{:S(2)}, u32[]{:S(2)}) %collective-permute-start.2) | collective-permute-done | bytes 655392 | tf_op jit(solution)/shard_map/ppermute | solution.py:52
  99.9 0.3 broadcast_in_dim.80
  100.2 1.2 bitcast_dynamic-update-slice_fusion.7
  101.4 0.1 collective-permute-start.6
  101.6 1.5 copy-done.5
  103.0 2.6 %collective-permute-start.7 = (bf16[32,5120]{1,0:T(8,128)(2,1)S(1)}, bf16[32,5120]{1,0:T(8,128)(2,1)}, u32[]{:S(2)}, u32[]{:S(2)}) collective-permute-start(bf16[32,5120]{1,0:T(8,128)(2,1)S(1)} %get-tuple-element.10), channel_id=1, source_target_pairs={{0,3},{1,0},{2,1},{3,2},{4,7},{5,4},{6,5},{7,6},{8,11},{9,8},{10,9... | collective-permute-start | bytes 983048 | tf_op jit(solution)/shard_map/ppermute | solution.py:61
  105.7 0.6 fusion.5
  106.3 1.2 gather_fusion.3
  107.4 13.5 %all-to-all-start.1 = ((f32[64,1,4]{2,1,0:T(1,128)}), f32[64,1,4]{2,1,0:T(1,128)S(1)}, u32[]{:S(2)}, u32[]{:S(2)}) async-start(f32[64,1,4]{2,1,0:T(1,128)} %bitcast.35), calls=%async_computation.1 | async-start | bytes 65536 | tf_op jit(solution)/shard_map/all_to_all | solution.py:96
  121.0 0.7 fusion.19
  121.7 8.6 %all-to-all-done.1 = f32[64,1,4]{2,1,0:T(1,128)S(1)} async-done(((f32[64,1,4]{2,1,0:T(1,128)}), f32[64,1,4]{2,1,0:T(1,128)S(1)}, u32[]{:S(2)}, u32[]{:S(2)}) %all-to-all-start.1) | async-done | bytes 1056 | tf_op jit(solution)/shard_map/all_to_all | solution.py:96
  130.3 1.8 %gather_fusion.5 = f32[128]{0:T(128)} fusion(f32[64,4]{1,0:T(8,128)S(1)} %bitcast.122, s32[128]{0:T(128)S(1)} %fusion.19), kind=kCustom, calls=%fused_computation.5 | custom fusion | bytes 2048 | tf_op jit(solution)/shard_map/gather | solution.py:99
  132.1 2.7 %collective-permute-start.9 = (bf16[32,5120]{1,0:T(8,128)(2,1)}, bf16[32,5120]{1,0:T(8,128)(2,1)S(1)}, u32[]{:S(2)}, u32[]{:S(2)}) collective-permute-start(bf16[32,5120]{1,0:T(8,128)(2,1)} %collective-permute-done.7), channel_id=1, source_target_pairs={{0,3},{1,0},{2,1},{3,2},{4,7},{5,4},{6,5},{7,6},{8,11},{9,8},{10,9... | collective-permute-start | bytes 983048 | tf_op jit(solution)/shard_map/ppermute | solution.py:61
  134.8 1.7 %bitcast_dynamic-update-slice_fusion.5 = bf16[8,32,5120]{2,1,0:T(8,128)(2,1)} fusion(bf16[8,32,5120]{2,1,0:T(8,128)(2,1)} %copy-done.5, s32[]{:T(128)S(6)} %select_n.224, bf16[32,5120]{1,0:T(8,128)(2,1)} %collective-permute-done.6), kind=kLoop, calls=%fused_computation.30 | loop fusion | bytes 655364 | tf_op jit(solution)/shard_map/jit(dynamic_update_index_in_dim)/dynamic_update_slice | solution.py:66
  136.5 1.7 %bitcast_dynamic-update-slice_fusion.4 = bf16[8,32,5120]{2,1,0:T(8,128)(2,1)} fusion(bf16[8,32,5120]{2,1,0:T(8,128)(2,1)} %bitcast_dynamic-update-slice_fusion.5, s32[]{:T(128)S(6)} %select_n.225, bf16[32,5120]{1,0:T(8,128)(2,1)} %collective-permute-done.7), kind=kLoop, calls=%fused_computation.29 | loop fusion | bytes 655364 | tf_op jit(solution)/shard_map/jit(dynamic_update_index_in_dim)/dynamic_update_slice | solution.py:67
  138.2 3.9 %collective-permute-done.8 = bf16[32,5120]{1,0:T(8,128)(2,1)S(1)} collective-permute-done((bf16[32,5120]{1,0:T(8,128)(2,1)}, bf16[32,5120]{1,0:T(8,128)(2,1)S(1)}, u32[]{:S(2)}, u32[]{:S(2)}) %collective-permute-start.8) | collective-permute-done | bytes 327712 | tf_op jit(solution)/shard_map/ppermute | solution.py:60
  142.1 2.7 %collective-permute-start.11 = (bf16[32,5120]{1,0:T(8,128)(2,1)S(1)}, bf16[32,5120]{1,0:T(8,128)(2,1)S(1)}, u32[]{:S(2)}, u32[]{:S(2)}) collective-permute-start(bf16[32,5120]{1,0:T(8,128)(2,1)S(1)} %collective-permute-done.9), channel_id=1, source_target_pairs={{0,3},{1,0},{2,1},{3,2},{4,7},{5,4},{6,5},{7,6},{8,11},{9,8},{10,9... | collective-permute-start | bytes 983048 | tf_op jit(solution)/shard_map/ppermute | solution.py:61
  144.8 0.7 bitcast_dynamic-update-slice_fusion.3
  145.5 0.7 bitcast_dynamic-update-slice_fusion.2
  146.3 4.8 %collective-permute-done.10 = bf16[32,5120]{1,0:T(8,128)(2,1)S(1)} collective-permute-done((bf16[32,5120]{1,0:T(8,128)(2,1)S(1)}, bf16[32,5120]{1,0:T(8,128)(2,1)S(1)}, u32[]{:S(2)}, u32[]{:S(2)}) %collective-permute-start.10) | collective-permute-done | bytes 327712 | tf_op jit(solution)/shard_map/ppermute | solution.py:60
  151.1 0.7 bitcast_dynamic-update-slice_fusion.1
  151.8 0.7 bitcast_dynamic-update-slice_fusion
  (39 shorter events, 0.7 us)
Async XLA Ops:
  0.6 25.8 %copy-start = (bf16[256,5120]{1,0:T(8,128)(2,1)S(1)}, bf16[256,5120]{1,0:T(8,128)(2,1)}, u32[]{:S(2)}) copy-start(bf16[256,5120]{1,0:T(8,128)(2,1)} %param.5) | copy-start | bytes 7864324
  2.5 18.5 %copy-start.6 = (s32[64]{0:T(128)S(1)}, s32[64]{0:T(128)}, u32[]{:S(2)}) copy-start(s32[64]{0:T(128)} %param.6) | copy-start | bytes 772
  3.1 20.4 %copy-start.1 = (s32[64]{0:T(128)S(1)}, s32[64]{0:T(128)}, u32[]{:S(2)}) copy-start(s32[64]{0:T(128)} %param.7) | copy-start | bytes 772
  7.9 27.7 %all-to-all-start = ((bf16[64,4,768]{2,1,0:T(4,128)(2,1)}), bf16[64,4,768]{2,1,0:T(4,128)(2,1)S(1)}, u32[]{:S(2)}, u32[]{:S(2)}) async-start(bf16[64,4,768]{2,1,0:T(4,128)(2,1)} %reshape.293), calls=%async_computation | async-start | bytes 786432 | tf_op jit(solution)/shard_map/all_to_all | solution.py:87
  55.8 1.9 %copy-start.2 = (f32[128,5120]{1,0:T(8,128)}, f32[128,5120]{1,0:T(8,128)S(1)}, u32[]{:S(2)}) copy-start(f32[128,5120]{1,0:T(8,128)S(1)} %get-tuple-element.15) | copy-start | bytes 7864324
  55.8 2.8 %copy-start.4 = (f32[128,5120]{1,0:T(8,128)}, f32[128,5120]{1,0:T(8,128)S(1)}, u32[]{:S(2)}) copy-start(f32[128,5120]{1,0:T(8,128)S(1)} %get-tuple-element.16) | copy-start | bytes 7864324
  56.8 14.5 %collective-permute-start = (f32[32,5120]{1,0:T(8,128)}, f32[32,5120]{1,0:T(8,128)}, u32[]{:S(2)}, u32[]{:S(2)}) collective-permute-start(f32[32,5120]{1,0:T(8,128)} %dynamic-slice_bitcast_fusion.1), channel_id=1, source_target_pairs={{0,1},{1,2},{2,3},{3,0},{4,5},{5,6},{6,7},{7,4},{8,9},{9,10},{10,1... | collective-permute-start | bytes 1966088 | tf_op jit(solution)/shard_map/ppermute | solution.py:52
  58.6 14.2 %collective-permute-start.3 = (f32[32,5120]{1,0:T(8,128)}, f32[32,5120]{1,0:T(8,128)S(1)}, u32[]{:S(2)}, u32[]{:S(2)}) collective-permute-start(f32[32,5120]{1,0:T(8,128)} %dynamic-slice_bitcast_fusion), channel_id=1, source_target_pairs={{0,3},{1,0},{2,1},{3,2},{4,7},{5,4},{6,5},{7,6},{8,11},{9,8},{10,9... | collective-permute-start | bytes 1966088 | tf_op jit(solution)/shard_map/ppermute | solution.py:53
  60.9 26.5 %copy-start.3 = (f32[128,5120]{1,0:T(8,128)S(1)}, f32[128,5120]{1,0:T(8,128)}, u32[]{:S(2)}) copy-start(f32[128,5120]{1,0:T(8,128)} %copy-done.2) | copy-start | bytes 7864324
  72.7 13.4 %collective-permute-start.1 = (f32[32,5120]{1,0:T(8,128)S(1)}, f32[32,5120]{1,0:T(8,128)S(1)}, u32[]{:S(2)}, u32[]{:S(2)}) collective-permute-start(f32[32,5120]{1,0:T(8,128)S(1)} %bitcast_add_fusion.5), channel_id=1, source_target_pairs={{0,1},{1,2},{2,3},{3,0},{4,5},{5,6},{6,7},{7,4},{8,9},{9,10},{10,1... | collective-permute-start | bytes 1966088 | tf_op jit(solution)/shard_map/ppermute | solution.py:52
  74.0 13.4 %collective-permute-start.4 = (f32[32,5120]{1,0:T(8,128)S(1)}, f32[32,5120]{1,0:T(8,128)S(1)}, u32[]{:S(2)}, u32[]{:S(2)}) collective-permute-start(f32[32,5120]{1,0:T(8,128)S(1)} %bitcast_add_fusion.2), channel_id=1, source_target_pairs={{0,3},{1,0},{2,1},{3,2},{4,7},{5,4},{6,5},{7,6},{8,11},{9,8},{10,9... | collective-permute-start | bytes 1966088 | tf_op jit(solution)/shard_map/ppermute | solution.py:53
  87.3 12.6 %collective-permute-start.2 = (f32[32,5120]{1,0:T(8,128)S(1)}, f32[32,5120]{1,0:T(8,128)S(1)}, u32[]{:S(2)}, u32[]{:S(2)}) collective-permute-start(f32[32,5120]{1,0:T(8,128)S(1)} %bitcast_add_fusion.4), channel_id=1, source_target_pairs={{0,1},{1,2},{2,3},{3,0},{4,5},{5,6},{6,7},{7,4},{8,9},{9,10},{10,1... | collective-permute-start | bytes 1966088 | tf_op jit(solution)/shard_map/ppermute | solution.py:52
  87.5 13.9 %collective-permute-start.5 = (f32[32,5120]{1,0:T(8,128)S(1)}, f32[32,5120]{1,0:T(8,128)S(1)}, u32[]{:S(2)}, u32[]{:S(2)}) collective-permute-start(f32[32,5120]{1,0:T(8,128)S(1)} %bitcast_add_fusion.1), channel_id=1, source_target_pairs={{0,3},{1,0},{2,1},{3,2},{4,7},{5,4},{6,5},{7,6},{8,11},{9,8},{10,9... | collective-permute-start | bytes 1966088 | tf_op jit(solution)/shard_map/ppermute | solution.py:53
  101.4 30.7 %collective-permute-start.6 = (bf16[32,5120]{1,0:T(8,128)(2,1)S(1)}, bf16[32,5120]{1,0:T(8,128)(2,1)}, u32[]{:S(2)}, u32[]{:S(2)}) collective-permute-start(bf16[32,5120]{1,0:T(8,128)(2,1)S(1)} %get-tuple-element.12), channel_id=1, source_target_pairs={{0,1},{1,2},{2,3},{3,0},{4,5},{5,6},{6,7},{7,4},{8,9},{9,10},{10,1... | collective-permute-start | bytes 983048 | tf_op jit(solution)/shard_map/ppermute | solution.py:60
  101.5 1.5 copy-start.5
  103.0 29.1 %collective-permute-start.7 = (bf16[32,5120]{1,0:T(8,128)(2,1)S(1)}, bf16[32,5120]{1,0:T(8,128)(2,1)}, u32[]{:S(2)}, u32[]{:S(2)}) collective-permute-start(bf16[32,5120]{1,0:T(8,128)(2,1)S(1)} %get-tuple-element.10), channel_id=1, source_target_pairs={{0,3},{1,0},{2,1},{3,2},{4,7},{5,4},{6,5},{7,6},{8,11},{9,8},{10,9... | collective-permute-start | bytes 983048 | tf_op jit(solution)/shard_map/ppermute | solution.py:61
  107.4 22.9 %all-to-all-start.1 = ((f32[64,1,4]{2,1,0:T(1,128)}), f32[64,1,4]{2,1,0:T(1,128)S(1)}, u32[]{:S(2)}, u32[]{:S(2)}) async-start(f32[64,1,4]{2,1,0:T(1,128)} %bitcast.35), calls=%async_computation.1 | async-start | bytes 65536 | tf_op jit(solution)/shard_map/all_to_all | solution.py:96
  132.1 10.0 %collective-permute-start.8 = (bf16[32,5120]{1,0:T(8,128)(2,1)}, bf16[32,5120]{1,0:T(8,128)(2,1)S(1)}, u32[]{:S(2)}, u32[]{:S(2)}) collective-permute-start(bf16[32,5120]{1,0:T(8,128)(2,1)} %collective-permute-done.6), channel_id=1, source_target_pairs={{0,1},{1,2},{2,3},{3,0},{4,5},{5,6},{6,7},{7,4},{8,9},{9,10},{10,1... | collective-permute-start | bytes 983048 | tf_op jit(solution)/shard_map/ppermute | solution.py:60
  132.1 10.0 %collective-permute-start.9 = (bf16[32,5120]{1,0:T(8,128)(2,1)}, bf16[32,5120]{1,0:T(8,128)(2,1)S(1)}, u32[]{:S(2)}, u32[]{:S(2)}) collective-permute-start(bf16[32,5120]{1,0:T(8,128)(2,1)} %collective-permute-done.7), channel_id=1, source_target_pairs={{0,3},{1,0},{2,1},{3,2},{4,7},{5,4},{6,5},{7,6},{8,11},{9,8},{10,9... | collective-permute-start | bytes 983048 | tf_op jit(solution)/shard_map/ppermute | solution.py:61
  142.1 9.0 %collective-permute-start.10 = (bf16[32,5120]{1,0:T(8,128)(2,1)S(1)}, bf16[32,5120]{1,0:T(8,128)(2,1)S(1)}, u32[]{:S(2)}, u32[]{:S(2)}) collective-permute-start(bf16[32,5120]{1,0:T(8,128)(2,1)S(1)} %collective-permute-done.8), channel_id=1, source_target_pairs={{0,1},{1,2},{2,3},{3,0},{4,5},{5,6},{6,7},{7,4},{8,9},{9,10},{10,1... | collective-permute-start | bytes 983048 | tf_op jit(solution)/shard_map/ppermute | solution.py:60
  142.1 9.7 %collective-permute-start.11 = (bf16[32,5120]{1,0:T(8,128)(2,1)S(1)}, bf16[32,5120]{1,0:T(8,128)(2,1)S(1)}, u32[]{:S(2)}, u32[]{:S(2)}) collective-permute-start(bf16[32,5120]{1,0:T(8,128)(2,1)S(1)} %collective-permute-done.9), channel_id=1, source_target_pairs={{0,3},{1,0},{2,1},{3,2},{4,7},{5,4},{6,5},{7,6},{8,11},{9,8},{10,9... | collective-permute-start | bytes 983048 | tf_op jit(solution)/shard_map/ppermute | solution.py:61

commit v8 on v7

--- a/solution.py
+++ b/solution.py
@@ -14,7 +14,7 @@
     own_total = jnp.sum(jnp.exp(logits - own_top[:, None]), axis=1)
     own_mass = jnp.sum(teacher_prob, axis=1)
     own_cross = jnp.sum(teacher_prob * (log_teacher - logits), axis=1)
-    stats = lax.all_gather(jnp.stack([own_top, own_total, own_mass, own_cross]), "vocab")
+    stats = exchange_stats(jnp.stack([own_top, own_total, own_mass, own_cross]))
     tops, totals, masses, crosses = stats[:, 0], stats[:, 1], stats[:, 2], stats[:, 3]
     row_top = jnp.max(tops, axis=0)
     exp_total = jnp.sum(totals * jnp.exp(tops - row_top[None, :]), axis=0)
@@ -32,6 +32,18 @@
     )
     hidden_grad = ring_all_reduce(partial_grad)
     return hidden_grad, row_div
+
+
+def exchange_stats(local):
+    ring = lax.axis_size("vocab")
+    me = lax.axis_index("vocab")
+    stats = jnp.broadcast_to(local[None], (ring,) + local.shape)
+    slot = jnp.arange(ring, dtype=jnp.int32)[:, None, None]
+    for off in range(1, ring):
+        pairs = [(i, (i - off) % ring) for i in range(ring)]
+        got = lax.ppermute(local, "vocab", pairs)
+        stats = jnp.where(slot == (me + off) % ring, got[None], stats)
+    return stats
 
 
 def ring_all_reduce(partial):

time: 154 us -> 153 us (level)
  blocking collectives: 9.48 us -> 0 us
  waiting for transfers between devices: 49.5 us -> 55.6 us
    all_gather x1 -> x0, blocking collectives: 9.48 us -> none  [divergence(): lax.all_gather(jnp.stack([own_top, own_total, own_mass, own_cross]), 'voc...]
    ppermute x0 -> x3, starting transfers between devices: none -> 4.89 us  [exchange_stats(): got = lax.ppermute(local, 'vocab', pairs)]
    ppermute x6, waiting for transfers between devices: 38 us -> 42.7 us  [ring_all_reduce(): up = lax.ppermute(up, 'vocab', forward)]
    all_to_all x1, starting transfers between devices: 13.5 us -> 11 us  [body(): lax.all_to_all(div_out, 'dp', split_axis=0, concat_axis=0, tiled=True)]
  transfers between devices with their start and end apart: 14 -> 17, of which waited for: 7 -> 8; matrix products, arithmetic and copies ran while one was open for 18% -> 19% of each run, Pallas kernels for 0% -> 0%
where the time goes in v8:
time: 153 us; the launch traced here: 152 us
  waiting for transfers between devices  55.6 us (36%)
  starting transfers between devices  44.8 us (29%)
  local copies, waits for them, and re-layouts  23.7 us (15%)
  other arithmetic  14.5 us (9%)
  matrix products  11.8 us (8%)
    ppermute x6, waiting for transfers between devices, ring_all_reduce(): up = lax.ppermute(up, 'vocab', forward)  42.7 us
    ppermute x6, starting transfers between devices, ring_all_reduce(): down = lax.ppermute(down, 'vocab', backward)  15.5 us
    all_to_all x1, starting transfers between devices, body(): lax.all_to_all(outgoing, 'dp', split_axis=0, concat_axis=0, tiled=True)  13.1 us
    all_to_all x1, starting transfers between devices, body(): lax.all_to_all(div_out, 'dp', split_axis=0, concat_axis=0, tiled=True)  11 us
    all_to_all x1, waiting for transfers between devices, body(): lax.all_to_all(div_out, 'dp', split_axis=0, concat_axis=0, tiled=True)  8.61 us
    dot_general x1, matrix products, divergence(): logits = jnp.dot(row_block, weight, preferred_element_type=jnp.float32)  6.3 us
    dot_general x1, matrix products, divergence(): lax.dot_general(grad_logits, weight, (((1,), (1,)), ((), ())), preferred_...  5.51 us
    ppermute x3, starting transfers between devices, exchange_stats(): got = lax.ppermute(local, 'vocab', pairs)  4.89 us
  transfers between devices with their start and end apart: 17, of which 8 were waited for; matrix products, arithmetic and copies ran while one was open for 19% of the time, Pallas kernels for 0%

profile of v8, /device:TPU:1, one launch (start us, length us, event | category | flops | bytes accessed | tf_op | source)
XLA Modules:
  0.0 151.6 jit_solution(6313387272065167272)
XLA Ops:
  0.6 0.9 select_reduce_fusion
  1.6 0.8 copy.24
  2.3 0.1 reduce-window.9
  2.4 0.1 reduce.5
  2.5 0.6 dynamic_slice.36
  3.1 1.3 and_select_fusion.3
  4.5 0.1 reshape.313
  4.7 2.4 %gather_fusion = bf16[256,768]{1,0:T(8,128)(2,1)S(1)} fusion(bf16[128,768]{1,0:T(8,128)(2,1)} %param.9, s32[1024]{0:T(1024)S(1)} %pad_clamp_fusion.4), kind=kCustom, calls=%fused_computation | custom fusion | bytes 787456 | tf_op jit(solution)/shard_map/jit(_take)/gather | solution.py:98
  7.0 0.8 reshape.312
  7.8 13.1 %all-to-all-start = ((bf16[64,4,768]{2,1,0:T(4,128)(2,1)}), bf16[64,4,768]{2,1,0:T(4,128)(2,1)S(1)}, u32[]{:S(2)}, u32[]{:S(2)}) async-start(bf16[64,4,768]{2,1,0:T(4,128)(2,1)} %reshape.312), calls=%async_computation | async-start | bytes 786432 | tf_op jit(solution)/shard_map/all_to_all | solution.py:99
  21.0 0.7 dynamic_slice.35
  21.7 0.6 multiply_add_fusion.1
  22.4 0.6 dynamic_slice.37
  22.9 0.7 fusion.10
  23.6 0.8 gather_fusion.1
  24.4 0.1 convert_reduce_fusion
  24.6 0.7 iota_compare_fusion.1
  25.3 6.3 %fusion.23 = (f32[256]{0:T(256)S(1)}, f32[256,768]{1,0:T(8,128)}) fusion(bf16[256,5120]{1,0:T(8,128)(2,1)S(1)} %copy-done, bf16[5120,768]{1,0:T(8,128)(2,1)} %param.8), kind=kOutput, calls=%fused_computation.94 | convolution fusion | flops 2013462272 | bytes 11273216 | tf_op jit(solution)/shard_map/dot_general | solution.py:10
  31.6 3.9 %all-to-all-done = bf16[64,4,768]{2,1,0:T(4,128)(2,1)S(1)} async-done(((bf16[64,4,768]{2,1,0:T(4,128)(2,1)}), bf16[64,4,768]{2,1,0:T(4,128)(2,1)S(1)}, u32[]{:S(2)}, u32[]{:S(2)}) %all-to-all-start) | async-done | bytes 393248 | tf_op jit(solution)/shard_map/all_to_all | solution.py:99
  35.5 0.9 gather_fusion.2
  36.5 0.3 fusion
  36.9 0.2 copy.26
  37.2 1.5 %exponential_reduce_fusion = (f32[256]{0:T(256)S(1)}, f32[256]{0:T(256)S(1)}) fusion(f32[256,768]{1,0:T(8,128)} %get-tuple-element.18, f32[256]{0:T(256)S(1)} %get-tuple-element.17, f32[4,64,768]{2,1,0:T(8,128)S(1)} %copy.26), kind=kLoop, calls=%fused_computation.14 | loop fusion | flops 982528 | bytes 1575936 | tf_op jit(solution)/shard_map/reduce_sum | solution.py:14
  38.7 1.3 collective-permute-start
  40.0 2.5 %collective-permute-start.1 = (f32[4,256]{1,0:T(4,128)S(1)}, f32[4,256]{1,0:T(4,128)S(1)}, u32[]{:S(2)}, u32[]{:S(2)}) collective-permute-start(f32[4,256]{1,0:T(4,128)S(1)} %pad_maximum_fusion), channel_id=1, source_target_pairs={{0,2},{1,3},{2,0},{3,1},{4,6},{5,7},{6,4},{7,5},{8,10},{9,11},{10,... | collective-permute-start | bytes 12296 | tf_op jit(solution)/shard_map/ppermute | solution.py:44
  42.5 1.2 collective-permute-start.2
  43.6 1.2 gather_fusion.4
  44.9 0.3 collective-permute-done.2
  45.4 1.4 select_convert_fusion
  46.8 5.5 %fusion.24 = f32[256,5120]{1,0:T(8,128)S(1)} fusion(bf16[256,768]{1,0:T(8,128)(2,1)S(1)} %select_convert_fusion, bf16[5120,768]{1,0:T(8,128)(2,1)} %param.8), kind=kOutput, calls=%fused_computation.95 | convolution fusion | flops 2013265920 | bytes 13500416 | tf_op jit(solution)/shard_map/dot_general | solution.py:30
  52.3 0.5 fusion.22
  52.9 1.0 dynamic-slice_bitcast_fusion.1
  53.9 0.7 copy-done.2
  54.6 1.0 dynamic-slice_bitcast_fusion
  55.6 2.1 %collective-permute-start.6 = (f32[32,5120]{1,0:T(8,128)}, f32[32,5120]{1,0:T(8,128)S(1)}, u32[]{:S(2)}, u32[]{:S(2)}) collective-permute-start(f32[32,5120]{1,0:T(8,128)} %dynamic-slice_bitcast_fusion), channel_id=1, source_target_pairs={{0,3},{1,0},{2,1},{3,2},{4,7},{5,4},{6,5},{7,6},{8,11},{9,8},{10,9... | collective-permute-start | bytes 1966088 | tf_op jit(solution)/shard_map/ppermute | solution.py:65
  57.8 0.1 copy.27
  57.9 12.0 %collective-permute-done.3 = f32[32,5120]{1,0:T(8,128)} collective-permute-done((f32[32,5120]{1,0:T(8,128)}, f32[32,5120]{1,0:T(8,128)}, u32[]{:S(2)}, u32[]{:S(2)}) %collective-permute-start.3) | collective-permute-done | bytes 655392 | tf_op jit(solution)/shard_map/ppermute | solution.py:64
  69.9 1.4 bitcast_add_fusion.5
  71.3 1.2 bitcast_add_fusion.2
  72.5 2.7 %collective-permute-start.7 = (f32[32,5120]{1,0:T(8,128)S(1)}, f32[32,5120]{1,0:T(8,128)S(1)}, u32[]{:S(2)}, u32[]{:S(2)}) collective-permute-start(f32[32,5120]{1,0:T(8,128)S(1)} %bitcast_add_fusion.2), channel_id=1, source_target_pairs={{0,3},{1,0},{2,1},{3,2},{4,7},{5,4},{6,5},{7,6},{8,11},{9,8},{10,9... | collective-permute-start | bytes 1966088 | tf_op jit(solution)/shard_map/ppermute | solution.py:65
  75.2 10.9 %collective-permute-done.4 = f32[32,5120]{1,0:T(8,128)S(1)} collective-permute-done((f32[32,5120]{1,0:T(8,128)S(1)}, f32[32,5120]{1,0:T(8,128)S(1)}, u32[]{:S(2)}, u32[]{:S(2)}) %collective-permute-start.4) | collective-permute-done | bytes 655392 | tf_op jit(solution)/shard_map/ppermute | solution.py:64
  86.1 1.2 bitcast_add_fusion.4
  87.5 2.7 %collective-permute-start.8 = (f32[32,5120]{1,0:T(8,128)S(1)}, f32[32,5120]{1,0:T(8,128)S(1)}, u32[]{:S(2)}, u32[]{:S(2)}) collective-permute-start(f32[32,5120]{1,0:T(8,128)S(1)} %bitcast_add_fusion.1), channel_id=1, source_target_pairs={{0,3},{1,0},{2,1},{3,2},{4,7},{5,4},{6,5},{7,6},{8,11},{9,8},{10,9... | collective-permute-start | bytes 1966088 | tf_op jit(solution)/shard_map/ppermute | solution.py:65
  90.2 11.1 %collective-permute-done.5 = f32[32,5120]{1,0:T(8,128)S(1)} collective-permute-done((f32[32,5120]{1,0:T(8,128)S(1)}, f32[32,5120]{1,0:T(8,128)S(1)}, u32[]{:S(2)}, u32[]{:S(2)}) %collective-permute-start.5) | collective-permute-done | bytes 655392 | tf_op jit(solution)/shard_map/ppermute | solution.py:64
  101.4 0.3 broadcast_in_dim.126
  101.7 1.2 bitcast_dynamic-update-slice_fusion.7
  103.0 1.5 copy-done.5
  104.5 2.6 %collective-permute-start.10 = (bf16[32,5120]{1,0:T(8,128)(2,1)S(1)}, bf16[32,5120]{1,0:T(8,128)(2,1)}, u32[]{:S(2)}, u32[]{:S(2)}) collective-permute-start(bf16[32,5120]{1,0:T(8,128)(2,1)S(1)} %get-tuple-element.10), channel_id=1, source_target_pairs={{0,3},{1,0},{2,1},{3,2},{4,7},{5,4},{6,5},{7,6},{8,11},{9,8},{10,9... | collective-permute-start | bytes 983048 | tf_op jit(solution)/shard_map/ppermute | solution.py:73
  107.2 0.7 fusion.5
  107.9 1.2 gather_fusion.3
  109.0 11.0 %all-to-all-start.1 = ((f32[64,1,4]{2,1,0:T(1,128)}), f32[64,1,4]{2,1,0:T(1,128)S(1)}, u32[]{:S(2)}, u32[]{:S(2)}) async-start(f32[64,1,4]{2,1,0:T(1,128)} %bitcast.35), calls=%async_computation.1 | async-start | bytes 65536 | tf_op jit(solution)/shard_map/all_to_all | solution.py:108
  120.0 0.7 fusion.18
  120.7 8.6 %all-to-all-done.1 = f32[64,1,4]{2,1,0:T(1,128)S(1)} async-done(((f32[64,1,4]{2,1,0:T(1,128)}), f32[64,1,4]{2,1,0:T(1,128)S(1)}, u32[]{:S(2)}, u32[]{:S(2)}) %all-to-all-start.1) | async-done | bytes 1056 | tf_op jit(solution)/shard_map/all_to_all | solution.py:108
  129.3 1.8 %gather_fusion.5 = f32[128]{0:T(128)} fusion(f32[64,4]{1,0:T(8,128)S(1)} %bitcast.120, s32[128]{0:T(128)S(1)} %fusion.18), kind=kCustom, calls=%fused_computation.5 | custom fusion | bytes 2048 | tf_op jit(solution)/shard_map/gather | solution.py:111
  131.1 2.7 %collective-permute-start.12 = (bf16[32,5120]{1,0:T(8,128)(2,1)}, bf16[32,5120]{1,0:T(8,128)(2,1)S(1)}, u32[]{:S(2)}, u32[]{:S(2)}) collective-permute-start(bf16[32,5120]{1,0:T(8,128)(2,1)} %collective-permute-done.10), channel_id=1, source_target_pairs={{0,3},{1,0},{2,1},{3,2},{4,7},{5,4},{6,5},{7,6},{8,11},{9,8},{10,9... | collective-permute-start | bytes 983048 | tf_op jit(solution)/shard_map/ppermute | solution.py:73
  133.8 1.7 %bitcast_dynamic-update-slice_fusion.5 = bf16[8,32,5120]{2,1,0:T(8,128)(2,1)} fusion(bf16[8,32,5120]{2,1,0:T(8,128)(2,1)} %copy-done.5, s32[]{:T(128)S(6)} %select_n.243, bf16[32,5120]{1,0:T(8,128)(2,1)} %collective-permute-done.9), kind=kLoop, calls=%fused_computation.30 | loop fusion | bytes 655364 | tf_op jit(solution)/shard_map/jit(dynamic_update_index_in_dim)/dynamic_update_slice | solution.py:78
  135.5 1.7 %bitcast_dynamic-update-slice_fusion.4 = bf16[8,32,5120]{2,1,0:T(8,128)(2,1)} fusion(bf16[8,32,5120]{2,1,0:T(8,128)(2,1)} %bitcast_dynamic-update-slice_fusion.5, s32[]{:T(128)S(6)} %select_n.244, bf16[32,5120]{1,0:T(8,128)(2,1)} %collective-permute-done.10), kind=kLoop, calls=%fused_computation.29 | loop fusion | bytes 655364 | tf_op jit(solution)/shard_map/jit(dynamic_update_index_in_dim)/dynamic_update_slice | solution.py:79
  137.3 3.9 %collective-permute-done.11 = bf16[32,5120]{1,0:T(8,128)(2,1)S(1)} collective-permute-done((bf16[32,5120]{1,0:T(8,128)(2,1)}, bf16[32,5120]{1,0:T(8,128)(2,1)S(1)}, u32[]{:S(2)}, u32[]{:S(2)}) %collective-permute-start.11) | collective-permute-done | bytes 327712 | tf_op jit(solution)/shard_map/ppermute | solution.py:72
  141.2 2.7 %collective-permute-start.14 = (bf16[32,5120]{1,0:T(8,128)(2,1)S(1)}, bf16[32,5120]{1,0:T(8,128)(2,1)S(1)}, u32[]{:S(2)}, u32[]{:S(2)}) collective-permute-start(bf16[32,5120]{1,0:T(8,128)(2,1)S(1)} %collective-permute-done.12), channel_id=1, source_target_pairs={{0,3},{1,0},{2,1},{3,2},{4,7},{5,4},{6,5},{7,6},{8,11},{9,8},{10,9... | collective-permute-start | bytes 983048 | tf_op jit(solution)/shard_map/ppermute | solution.py:73
  143.9 0.7 bitcast_dynamic-update-slice_fusion.3
  144.6 0.7 bitcast_dynamic-update-slice_fusion.2
  145.3 4.8 %collective-permute-done.13 = bf16[32,5120]{1,0:T(8,128)(2,1)S(1)} collective-permute-done((bf16[32,5120]{1,0:T(8,128)(2,1)S(1)}, bf16[32,5120]{1,0:T(8,128)(2,1)S(1)}, u32[]{:S(2)}, u32[]{:S(2)}) %collective-permute-start.13) | collective-permute-done | bytes 327712 | tf_op jit(solution)/shard_map/ppermute | solution.py:72
  150.1 0.7 bitcast_dynamic-update-slice_fusion.1
  150.9 0.7 bitcast_dynamic-update-slice_fusion
  (47 shorter events, 1.1 us)
Async XLA Ops:
  0.6 24.7 %copy-start = (bf16[256,5120]{1,0:T(8,128)(2,1)S(1)}, bf16[256,5120]{1,0:T(8,128)(2,1)}, u32[]{:S(2)}) copy-start(bf16[256,5120]{1,0:T(8,128)(2,1)} %param.5) | copy-start | bytes 7864324
  4.5 16.5 %copy-start.6 = (s32[64]{0:T(128)S(1)}, s32[64]{0:T(128)}, u32[]{:S(2)}) copy-start(s32[64]{0:T(128)} %param.6) | copy-start | bytes 772
  4.6 19.0 %copy-start.1 = (s32[64]{0:T(128)S(1)}, s32[64]{0:T(128)}, u32[]{:S(2)}) copy-start(s32[64]{0:T(128)} %param.7) | copy-start | bytes 772
  7.8 27.7 %all-to-all-start = ((bf16[64,4,768]{2,1,0:T(4,128)(2,1)}), bf16[64,4,768]{2,1,0:T(4,128)(2,1)S(1)}, u32[]{:S(2)}, u32[]{:S(2)}) async-start(bf16[64,4,768]{2,1,0:T(4,128)(2,1)} %reshape.312), calls=%async_computation | async-start | bytes 786432 | tf_op jit(solution)/shard_map/all_to_all | solution.py:99
  38.7 6.2 %collective-permute-start = (f32[4,256]{1,0:T(4,128)S(1)}, f32[4,256]{1,0:T(4,128)S(1)}, u32[]{:S(2)}, u32[]{:S(2)}) collective-permute-start(f32[4,256]{1,0:T(4,128)S(1)} %pad_maximum_fusion), channel_id=1, source_target_pairs={{0,1},{1,2},{2,3},{3,0},{4,5},{5,6},{6,7},{7,4},{8,9},{9,10},{10,1... | collective-permute-start | bytes 12296 | tf_op jit(solution)/shard_map/ppermute | solution.py:44
  40.0 4.9 %collective-permute-start.1 = (f32[4,256]{1,0:T(4,128)S(1)}, f32[4,256]{1,0:T(4,128)S(1)}, u32[]{:S(2)}, u32[]{:S(2)}) collective-permute-start(f32[4,256]{1,0:T(4,128)S(1)} %pad_maximum_fusion), channel_id=1, source_target_pairs={{0,2},{1,3},{2,0},{3,1},{4,6},{5,7},{6,4},{7,5},{8,10},{9,11},{10,... | collective-permute-start | bytes 12296 | tf_op jit(solution)/shard_map/ppermute | solution.py:44
  42.5 2.8 %collective-permute-start.2 = (f32[4,256]{1,0:T(4,128)S(1)}, f32[4,256]{1,0:T(4,128)S(1)}, u32[]{:S(2)}, u32[]{:S(2)}) collective-permute-start(f32[4,256]{1,0:T(4,128)S(1)} %pad_maximum_fusion), channel_id=1, source_target_pairs={{0,3},{1,0},{2,1},{3,2},{4,7},{5,4},{6,5},{7,6},{8,11},{9,8},{10,9... | collective-permute-start | bytes 12296 | tf_op jit(solution)/shard_map/ppermute | solution.py:44
  52.9 1.7 %copy-start.2 = (f32[128,5120]{1,0:T(8,128)}, f32[128,5120]{1,0:T(8,128)S(1)}, u32[]{:S(2)}) copy-start(f32[128,5120]{1,0:T(8,128)S(1)} %get-tuple-element.15) | copy-start | bytes 7864324
  52.9 2.7 %copy-start.4 = (f32[128,5120]{1,0:T(8,128)}, f32[128,5120]{1,0:T(8,128)S(1)}, u32[]{:S(2)}) copy-start(f32[128,5120]{1,0:T(8,128)S(1)} %get-tuple-element.16) | copy-start | bytes 7864324
  53.9 16.0 %collective-permute-start.3 = (f32[32,5120]{1,0:T(8,128)}, f32[32,5120]{1,0:T(8,128)}, u32[]{:S(2)}, u32[]{:S(2)}) collective-permute-start(f32[32,5120]{1,0:T(8,128)} %dynamic-slice_bitcast_fusion.1), channel_id=1, source_target_pairs={{0,1},{1,2},{2,3},{3,0},{4,5},{5,6},{6,7},{7,4},{8,9},{9,10},{10,1... | collective-permute-start | bytes 1966088 | tf_op jit(solution)/shard_map/ppermute | solution.py:64
  55.6 15.7 %collective-permute-start.6 = (f32[32,5120]{1,0:T(8,128)}, f32[32,5120]{1,0:T(8,128)S(1)}, u32[]{:S(2)}, u32[]{:S(2)}) collective-permute-start(f32[32,5120]{1,0:T(8,128)} %dynamic-slice_bitcast_fusion), channel_id=1, source_target_pairs={{0,3},{1,0},{2,1},{3,2},{4,7},{5,4},{6,5},{7,6},{8,11},{9,8},{10,9... | collective-permute-start | bytes 1966088 | tf_op jit(solution)/shard_map/ppermute | solution.py:65
  57.9 29.5 %copy-start.3 = (f32[128,5120]{1,0:T(8,128)S(1)}, f32[128,5120]{1,0:T(8,128)}, u32[]{:S(2)}) copy-start(f32[128,5120]{1,0:T(8,128)} %copy-done.2) | copy-start | bytes 7864324
  71.2 14.9 %collective-permute-start.4 = (f32[32,5120]{1,0:T(8,128)S(1)}, f32[32,5120]{1,0:T(8,128)S(1)}, u32[]{:S(2)}, u32[]{:S(2)}) collective-permute-start(f32[32,5120]{1,0:T(8,128)S(1)} %bitcast_add_fusion.5), channel_id=1, source_target_pairs={{0,1},{1,2},{2,3},{3,0},{4,5},{5,6},{6,7},{7,4},{8,9},{9,10},{10,1... | collective-permute-start | bytes 1966088 | tf_op jit(solution)/shard_map/ppermute | solution.py:64
  72.5 14.9 %collective-permute-start.7 = (f32[32,5120]{1,0:T(8,128)S(1)}, f32[32,5120]{1,0:T(8,128)S(1)}, u32[]{:S(2)}, u32[]{:S(2)}) collective-permute-start(f32[32,5120]{1,0:T(8,128)S(1)} %bitcast_add_fusion.2), channel_id=1, source_target_pairs={{0,3},{1,0},{2,1},{3,2},{4,7},{5,4},{6,5},{7,6},{8,11},{9,8},{10,9... | collective-permute-start | bytes 1966088 | tf_op jit(solution)/shard_map/ppermute | solution.py:65
  87.3 14.1 %collective-permute-start.5 = (f32[32,5120]{1,0:T(8,128)S(1)}, f32[32,5120]{1,0:T(8,128)S(1)}, u32[]{:S(2)}, u32[]{:S(2)}) collective-permute-start(f32[32,5120]{1,0:T(8,128)S(1)} %bitcast_add_fusion.4), channel_id=1, source_target_pairs={{0,1},{1,2},{2,3},{3,0},{4,5},{5,6},{6,7},{7,4},{8,9},{9,10},{10,1... | collective-permute-start | bytes 1966088 | tf_op jit(solution)/shard_map/ppermute | solution.py:64
  87.5 15.4 %collective-permute-start.8 = (f32[32,5120]{1,0:T(8,128)S(1)}, f32[32,5120]{1,0:T(8,128)S(1)}, u32[]{:S(2)}, u32[]{:S(2)}) collective-permute-start(f32[32,5120]{1,0:T(8,128)S(1)} %bitcast_add_fusion.1), channel_id=1, source_target_pairs={{0,3},{1,0},{2,1},{3,2},{4,7},{5,4},{6,5},{7,6},{8,11},{9,8},{10,9... | collective-permute-start | bytes 1966088 | tf_op jit(solution)/shard_map/ppermute | solution.py:65
  102.8 28.3 %collective-permute-start.9 = (bf16[32,5120]{1,0:T(8,128)(2,1)S(1)}, bf16[32,5120]{1,0:T(8,128)(2,1)}, u32[]{:S(2)}, u32[]{:S(2)}) collective-permute-start(bf16[32,5120]{1,0:T(8,128)(2,1)S(1)} %get-tuple-element.12), channel_id=1, source_target_pairs={{0,1},{1,2},{2,3},{3,0},{4,5},{5,6},{6,7},{7,4},{8,9},{9,10},{10,1... | collective-permute-start | bytes 983048 | tf_op jit(solution)/shard_map/ppermute | solution.py:72
  103.0 1.5 copy-start.5
  104.5 26.6 %collective-permute-start.10 = (bf16[32,5120]{1,0:T(8,128)(2,1)S(1)}, bf16[32,5120]{1,0:T(8,128)(2,1)}, u32[]{:S(2)}, u32[]{:S(2)}) collective-permute-start(bf16[32,5120]{1,0:T(8,128)(2,1)S(1)} %get-tuple-element.10), channel_id=1, source_target_pairs={{0,3},{1,0},{2,1},{3,2},{4,7},{5,4},{6,5},{7,6},{8,11},{9,8},{10,9... | collective-permute-start | bytes 983048 | tf_op jit(solution)/shard_map/ppermute | solution.py:73
  109.0 20.3 %all-to-all-start.1 = ((f32[64,1,4]{2,1,0:T(1,128)}), f32[64,1,4]{2,1,0:T(1,128)S(1)}, u32[]{:S(2)}, u32[]{:S(2)}) async-start(f32[64,1,4]{2,1,0:T(1,128)} %bitcast.35), calls=%async_computation.1 | async-start | bytes 65536 | tf_op jit(solution)/shard_map/all_to_all | solution.py:108
  131.1 10.0 %collective-permute-start.11 = (bf16[32,5120]{1,0:T(8,128)(2,1)}, bf16[32,5120]{1,0:T(8,128)(2,1)S(1)}, u32[]{:S(2)}, u32[]{:S(2)}) collective-permute-start(bf16[32,5120]{1,0:T(8,128)(2,1)} %collective-permute-done.9), channel_id=1, source_target_pairs={{0,1},{1,2},{2,3},{3,0},{4,5},{5,6},{6,7},{7,4},{8,9},{9,10},{10,1... | collective-permute-start | bytes 983048 | tf_op jit(solution)/shard_map/ppermute | solution.py:72
  131.1 10.0 %collective-permute-start.12 = (bf16[32,5120]{1,0:T(8,128)(2,1)}, bf16[32,5120]{1,0:T(8,128)(2,1)S(1)}, u32[]{:S(2)}, u32[]{:S(2)}) collective-permute-start(bf16[32,5120]{1,0:T(8,128)(2,1)} %collective-permute-done.10), channel_id=1, source_target_pairs={{0,3},{1,0},{2,1},{3,2},{4,7},{5,4},{6,5},{7,6},{8,11},{9,8},{10,9... | collective-permute-start | bytes 983048 | tf_op jit(solution)/shard_map/ppermute | solution.py:73
  141.2 9.0 %collective-permute-start.13 = (bf16[32,5120]{1,0:T(8,128)(2,1)S(1)}, bf16[32,5120]{1,0:T(8,128)(2,1)S(1)}, u32[]{:S(2)}, u32[]{:S(2)}) collective-permute-start(bf16[32,5120]{1,0:T(8,128)(2,1)S(1)} %collective-permute-done.11), channel_id=1, source_target_pairs={{0,1},{1,2},{2,3},{3,0},{4,5},{5,6},{6,7},{7,4},{8,9},{9,10},{10,1... | collective-permute-start | bytes 983048 | tf_op jit(solution)/shard_map/ppermute | solution.py:72
  141.2 9.7 %collective-permute-start.14 = (bf16[32,5120]{1,0:T(8,128)(2,1)S(1)}, bf16[32,5120]{1,0:T(8,128)(2,1)S(1)}, u32[]{:S(2)}, u32[]{:S(2)}) collective-permute-start(bf16[32,5120]{1,0:T(8,128)(2,1)S(1)} %collective-permute-done.12), channel_id=1, source_target_pairs={{0,3},{1,0},{2,1},{3,2},{4,7},{5,4},{6,5},{7,6},{8,11},{9,8},{10,9... | collective-permute-start | bytes 983048 | tf_op jit(solution)/shard_map/ppermute | solution.py:73

commit v9 on v8

--- a/solution.py
+++ b/solution.py
@@ -95,12 +95,16 @@
     first_col = (inverse[myself] - offsets) % shards
     first_slot = (offsets + first_col) // shards
     send_rows = jnp.minimum(first_slot[:, None] + depth[None, :], balanced - 1)
-    outgoing = jnp.take(teacher_logprobs, send_rows, axis=0, mode="clip")
+    positions = jnp.arange(balanced, dtype=jnp.int32)
+    selector = (send_rows.reshape(-1)[:, None] == positions[None, :]).astype(teacher_logprobs.dtype)
+    outgoing = jnp.dot(selector, teacher_logprobs, preferred_element_type=jnp.float32)
+    outgoing = outgoing.astype(teacher_logprobs.dtype)
     arriving = lax.all_to_all(outgoing, "dp", split_axis=0, concat_axis=0, tiled=True)
     own_offset = offsets[myself]
     shard_at = shard_of_class[(own_offset + classes) % shards]
-    teacher_slots = jnp.take(arriving, shard_at, axis=0, mode="clip")
-    teacher_slots = jnp.transpose(teacher_slots, (1, 0, 2)).reshape(source_slots, -1)
+    slot_source = (depth[:, None] + slot_depth * shard_at[None, :]).reshape(-1)
+    picker = (slot_source[:, None] == jnp.arange(source_slots, dtype=jnp.int32)[None, :]).astype(arriving.dtype)
+    teacher_slots = jnp.dot(picker, arriving, preferred_element_type=jnp.float32).astype(arriving.dtype)
     live = jnp.arange(source_slots, dtype=jnp.int32) < plan_lengths[myself]
     row_grad, row_div = divergence(hidden_rows, teacher_slots, live, head_weight)
     column_of = (inverse - own_offset) % shards

time: 153 us -> 150 us (0.980)
  matrix products: 11.8 us -> 16 us
  other arithmetic: 14.5 us -> 11 us
  local copies, waits for them, and re-layouts: 23.7 us -> 20.7 us
    gather x3 -> x0, local copies, waits for them, and re-layouts: 4.1 us -> none  [the longest x2 3.18 us: body(): outgoing = jnp.take(teacher_logprobs, send_rows, axis=0, mode='clip')]
    dot_general x0 -> x2, matrix products: none -> 3.57 us  [the longest x1 2.34 us: body(): jnp.dot(picker, arriving, preferred_element_type=jnp.float32)]
    reduce_sum x2 -> x0, other arithmetic: 1.86 us -> none  [the longest x1 1.53 us: divergence(): own_total = jnp.sum(jnp.exp(logits - own_top[:, None]), axis=1)]
where the time goes in v9:
time: 150 us; the launch traced here: 149 us
  waiting for transfers between devices  54.9 us (37%)
  starting transfers between devices  45.5 us (30%)
  local copies, waits for them, and re-layouts  20.7 us (14%)
  matrix products  16 us (11%)
  other arithmetic  11 us (7%)
    ppermute x6, waiting for transfers between devices, ring_all_reduce(): up = lax.ppermute(up, 'vocab', forward)  42.5 us
    ppermute x6, starting transfers between devices, ring_all_reduce(): down = lax.ppermute(down, 'vocab', backward)  15.7 us
    all_to_all x1, starting transfers between devices, body(): lax.all_to_all(outgoing, 'dp', split_axis=0, concat_axis=0, tiled=True)  13.1 us
    all_to_all x1, starting transfers between devices, body(): lax.all_to_all(div_out, 'dp', split_axis=0, concat_axis=0, tiled=True)  11.5 us
    all_to_all x1, waiting for transfers between devices, body(): lax.all_to_all(div_out, 'dp', split_axis=0, concat_axis=0, tiled=True)  8.61 us
    dot_general x1, matrix products, divergence(): logits = jnp.dot(row_block, weight, preferred_element_type=jnp.float32)  6.3 us
    dot_general x1, matrix products, divergence(): lax.dot_general(grad_logits, weight, (((1,), (1,)), ((), ())), preferred_...  6.11 us
    ppermute x3, starting transfers between devices, exchange_stats(): got = lax.ppermute(local, 'vocab', pairs)  4.89 us
  transfers between devices with their start and end apart: 17, of which 8 were waited for; matrix products, arithmetic and copies ran while one was open for 19% of the time, Pallas kernels for 0%

profile of v9, /device:TPU:1, one launch (start us, length us, event | category | flops | bytes accessed | tf_op | source)
XLA Modules:
  0.0 149.1 jit_solution(10808183057366225370)
XLA Ops:
  0.7 0.9 select_reduce_fusion
  1.6 0.8 copy.16
  2.3 0.1 reduce-window.9
  2.4 0.1 reduce.3
  2.5 0.6 dynamic_slice.37
  3.1 1.3 and_select_fusion.2
  4.5 0.1 min.15
  4.6 1.2 convolution_convert_fusion.1
  5.9 0.8 all_to_all.16
  6.7 13.1 %all-to-all-start = ((bf16[64,4,768]{2,1,0:T(4,128)(2,1)}), bf16[64,4,768]{2,1,0:T(4,128)(2,1)S(1)}, u32[]{:S(2)}, u32[]{:S(2)}) async-start(bf16[64,4,768]{2,1,0:T(4,128)(2,1)} %all_to_all.16), calls=%async_computation | async-start | bytes 786432 | tf_op jit(solution)/shard_map/all_to_all | solution.py:102
  19.9 1.2 dynamic_slice.35
  21.1 0.6 multiply_add_fusion.1
  21.8 0.6 dynamic_slice.36
  22.4 0.7 fusion.16
  23.1 0.8 gather_fusion
  23.9 0.1 convert_reduce_fusion
  24.0 0.6 iota_compare_fusion.5
  24.6 0.1 add.352
  24.7 6.3 %fusion.31 = (f32[256]{0:T(256)S(1)}, f32[256,768]{1,0:T(8,128)}) fusion(bf16[256,5120]{1,0:T(8,128)(2,1)S(1)} %copy-done, bf16[5120,768]{1,0:T(8,128)(2,1)} %param.8), kind=kOutput, calls=%fused_computation.102 | convolution fusion | flops 2013462272 | bytes 11273216 | tf_op jit(solution)/shard_map/dot_general | solution.py:10
  31.0 3.4 %all-to-all-done = bf16[64,4,768]{2,1,0:T(4,128)(2,1)S(1)} async-done(((bf16[64,4,768]{2,1,0:T(4,128)(2,1)}), bf16[64,4,768]{2,1,0:T(4,128)(2,1)S(1)}, u32[]{:S(2)}, u32[]{:S(2)}) %all-to-all-start) | async-done | bytes 393248 | tf_op jit(solution)/shard_map/all_to_all | solution.py:102
  34.4 0.1 all_to_all.18
  34.5 2.3 %exponential_reduce_fusion = (f32[256]{0:T(256)S(1)}, f32[256]{0:T(256)S(1)}, f32[256]{0:T(256)S(1)}, f32[256,768]{1,0:T(8,128)}) fusion(f32[256,768]{1,0:T(8,128)} %get-tuple-element.19, f32[256]{0:T(256)S(1)} %get-tuple-element.18, bf16[256,768]{1,0:T(8,128)(2,1)S(1)} %all_to_all.18, s32[256]{0:T(256)S(1)} %add.352), kind=kOutput, calls=%fused_computation.9 | convolution fusion | flops 102300928 | bytes 1971200 | tf_op jit(solution)/shard_map/dot_general | solution.py:107
  36.9 1.3 collective-permute-start
  38.2 2.5 %collective-permute-start.1 = (f32[4,256]{1,0:T(4,128)S(1)}, f32[4,256]{1,0:T(4,128)S(1)}, u32[]{:S(2)}, u32[]{:S(2)}) collective-permute-start(f32[4,256]{1,0:T(4,128)S(1)} %pad_maximum_fusion), channel_id=1, source_target_pairs={{0,2},{1,3},{2,0},{3,1},{4,6},{5,7},{6,4},{7,5},{8,10},{9,11},{10,... | collective-permute-start | bytes 12296 | tf_op jit(solution)/shard_map/ppermute | solution.py:44
  40.6 1.1 collective-permute-start.2
  41.8 1.2 gather_fusion.2
  43.1 0.3 collective-permute-done.2
  43.5 6.1 %fusion.3 = f32[256,5120]{1,0:T(8,128)S(1)} fusion(bf16[5120,768]{1,0:T(8,128)(2,1)} %param.8, f32[256,768]{1,0:T(8,128)} %get-tuple-element.19, f32[256,768]{1,0:T(8,128)} %get-tuple-element.20, f32[256]{0:T(256)S(1)} %get-tuple-element.9, f32[256]{0:T(256)S(1)} %get-tuple-element.7, pred[256]{0:T(512)(128)(4,1)S(1)} %iota_compare_fusion.5), kind=kOutput, calls=%fused_computation.21 | convolution fusion | flops 2014445568 | bytes 14682368 | tf_op jit(solution)/shard_map/dot_general | solution.py:30
  49.6 0.4 fusion.30
  50.0 1.0 dynamic-slice_bitcast_fusion.1
  51.0 0.7 copy-done.2
  51.7 1.1 dynamic-slice_bitcast_fusion
  52.7 2.1 %collective-permute-start.6 = (f32[32,5120]{1,0:T(8,128)}, f32[32,5120]{1,0:T(8,128)S(1)}, u32[]{:S(2)}, u32[]{:S(2)}) collective-permute-start(f32[32,5120]{1,0:T(8,128)} %dynamic-slice_bitcast_fusion), channel_id=1, source_target_pairs={{0,3},{1,0},{2,1},{3,2},{4,7},{5,4},{6,5},{7,6},{8,11},{9,8},{10,9... | collective-permute-start | bytes 1966088 | tf_op jit(solution)/shard_map/ppermute | solution.py:65
  54.9 0.1 copy.17
  55.0 12.0 %collective-permute-done.3 = f32[32,5120]{1,0:T(8,128)} collective-permute-done((f32[32,5120]{1,0:T(8,128)}, f32[32,5120]{1,0:T(8,128)}, u32[]{:S(2)}, u32[]{:S(2)}) %collective-permute-start.3) | collective-permute-done | bytes 655392 | tf_op jit(solution)/shard_map/ppermute | solution.py:64
  67.0 1.4 bitcast_add_fusion.5
  68.3 0.1 collective-permute-start.4
  68.4 1.2 bitcast_add_fusion.2
  69.6 2.9 %collective-permute-start.7 = (f32[32,5120]{1,0:T(8,128)S(1)}, f32[32,5120]{1,0:T(8,128)S(1)}, u32[]{:S(2)}, u32[]{:S(2)}) collective-permute-start(f32[32,5120]{1,0:T(8,128)S(1)} %bitcast_add_fusion.2), channel_id=1, source_target_pairs={{0,3},{1,0},{2,1},{3,2},{4,7},{5,4},{6,5},{7,6},{8,11},{9,8},{10,9... | collective-permute-start | bytes 1966088 | tf_op jit(solution)/shard_map/ppermute | solution.py:65
  72.6 10.7 %collective-permute-done.4 = f32[32,5120]{1,0:T(8,128)S(1)} collective-permute-done((f32[32,5120]{1,0:T(8,128)S(1)}, f32[32,5120]{1,0:T(8,128)S(1)}, u32[]{:S(2)}, u32[]{:S(2)}) %collective-permute-start.4) | collective-permute-done | bytes 655392 | tf_op jit(solution)/shard_map/ppermute | solution.py:64
  83.3 1.2 bitcast_add_fusion.4
  84.6 2.7 %collective-permute-start.8 = (f32[32,5120]{1,0:T(8,128)S(1)}, f32[32,5120]{1,0:T(8,128)S(1)}, u32[]{:S(2)}, u32[]{:S(2)}) collective-permute-start(f32[32,5120]{1,0:T(8,128)S(1)} %bitcast_add_fusion.1), channel_id=1, source_target_pairs={{0,3},{1,0},{2,1},{3,2},{4,7},{5,4},{6,5},{7,6},{8,11},{9,8},{10,9... | collective-permute-start | bytes 1966088 | tf_op jit(solution)/shard_map/ppermute | solution.py:65
  87.4 11.1 %collective-permute-done.5 = f32[32,5120]{1,0:T(8,128)S(1)} collective-permute-done((f32[32,5120]{1,0:T(8,128)S(1)}, f32[32,5120]{1,0:T(8,128)S(1)}, u32[]{:S(2)}, u32[]{:S(2)}) %collective-permute-start.5) | collective-permute-done | bytes 655392 | tf_op jit(solution)/shard_map/ppermute | solution.py:64
  98.5 0.3 broadcast_in_dim.124
  98.8 1.2 bitcast_dynamic-update-slice_fusion.7
  100.0 0.1 collective-permute-start.9
  100.2 1.5 copy-done.5
  101.7 2.6 %collective-permute-start.10 = (bf16[32,5120]{1,0:T(8,128)(2,1)S(1)}, bf16[32,5120]{1,0:T(8,128)(2,1)}, u32[]{:S(2)}, u32[]{:S(2)}) collective-permute-start(bf16[32,5120]{1,0:T(8,128)(2,1)S(1)} %get-tuple-element.11), channel_id=1, source_target_pairs={{0,3},{1,0},{2,1},{3,2},{4,7},{5,4},{6,5},{7,6},{8,11},{9,8},{10,9... | collective-permute-start | bytes 983048 | tf_op jit(solution)/shard_map/ppermute | solution.py:73
  104.3 0.6 fusion.11
  104.9 1.2 gather_fusion.1
  106.0 11.5 %all-to-all-start.1 = ((f32[64,1,4]{2,1,0:T(1,128)}), f32[64,1,4]{2,1,0:T(1,128)S(1)}, u32[]{:S(2)}, u32[]{:S(2)}) async-start(f32[64,1,4]{2,1,0:T(1,128)} %bitcast.33), calls=%async_computation.1 | async-start | bytes 65536 | tf_op jit(solution)/shard_map/all_to_all | solution.py:112
  117.5 0.7 fusion.24
  118.2 8.6 %all-to-all-done.1 = f32[64,1,4]{2,1,0:T(1,128)S(1)} async-done(((f32[64,1,4]{2,1,0:T(1,128)}), f32[64,1,4]{2,1,0:T(1,128)S(1)}, u32[]{:S(2)}, u32[]{:S(2)}) %all-to-all-start.1) | async-done | bytes 1056 | tf_op jit(solution)/shard_map/all_to_all | solution.py:112
  126.9 1.8 %gather_fusion.3 = f32[128]{0:T(128)} fusion(f32[64,4]{1,0:T(8,128)S(1)} %bitcast.106, s32[128]{0:T(128)S(1)} %fusion.24), kind=kCustom, calls=%fused_computation.3 | custom fusion | bytes 2048 | tf_op jit(solution)/shard_map/gather | solution.py:115
  128.7 2.7 %collective-permute-start.12 = (bf16[32,5120]{1,0:T(8,128)(2,1)}, bf16[32,5120]{1,0:T(8,128)(2,1)S(1)}, u32[]{:S(2)}, u32[]{:S(2)}) collective-permute-start(bf16[32,5120]{1,0:T(8,128)(2,1)} %collective-permute-done.10), channel_id=1, source_target_pairs={{0,3},{1,0},{2,1},{3,2},{4,7},{5,4},{6,5},{7,6},{8,11},{9,8},{10,9... | collective-permute-start | bytes 983048 | tf_op jit(solution)/shard_map/ppermute | solution.py:73
  131.3 1.7 %bitcast_dynamic-update-slice_fusion.5 = bf16[8,32,5120]{2,1,0:T(8,128)(2,1)} fusion(bf16[8,32,5120]{2,1,0:T(8,128)(2,1)} %copy-done.5, s32[]{:T(128)S(6)} %select_n.243, bf16[32,5120]{1,0:T(8,128)(2,1)} %collective-permute-done.9), kind=kLoop, calls=%fused_computation.32 | loop fusion | bytes 655364 | tf_op jit(solution)/shard_map/jit(dynamic_update_index_in_dim)/dynamic_update_slice | solution.py:78
  133.0 1.7 %bitcast_dynamic-update-slice_fusion.4 = bf16[8,32,5120]{2,1,0:T(8,128)(2,1)} fusion(bf16[8,32,5120]{2,1,0:T(8,128)(2,1)} %bitcast_dynamic-update-slice_fusion.5, s32[]{:T(128)S(6)} %select_n.244, bf16[32,5120]{1,0:T(8,128)(2,1)} %collective-permute-done.10), kind=kLoop, calls=%fused_computation.31 | loop fusion | bytes 655364 | tf_op jit(solution)/shard_map/jit(dynamic_update_index_in_dim)/dynamic_update_slice | solution.py:79
  134.8 3.9 %collective-permute-done.11 = bf16[32,5120]{1,0:T(8,128)(2,1)S(1)} collective-permute-done((bf16[32,5120]{1,0:T(8,128)(2,1)}, bf16[32,5120]{1,0:T(8,128)(2,1)S(1)}, u32[]{:S(2)}, u32[]{:S(2)}) %collective-permute-start.11) | collective-permute-done | bytes 327712 | tf_op jit(solution)/shard_map/ppermute | solution.py:72
  138.7 2.7 %collective-permute-start.14 = (bf16[32,5120]{1,0:T(8,128)(2,1)S(1)}, bf16[32,5120]{1,0:T(8,128)(2,1)S(1)}, u32[]{:S(2)}, u32[]{:S(2)}) collective-permute-start(bf16[32,5120]{1,0:T(8,128)(2,1)S(1)} %collective-permute-done.12), channel_id=1, source_target_pairs={{0,3},{1,0},{2,1},{3,2},{4,7},{5,4},{6,5},{7,6},{8,11},{9,8},{10,9... | collective-permute-start | bytes 983048 | tf_op jit(solution)/shard_map/ppermute | solution.py:73
  141.4 0.7 bitcast_dynamic-update-slice_fusion.3
  142.1 0.7 bitcast_dynamic-update-slice_fusion.2
  142.8 4.8 %collective-permute-done.13 = bf16[32,5120]{1,0:T(8,128)(2,1)S(1)} collective-permute-done((bf16[32,5120]{1,0:T(8,128)(2,1)S(1)}, bf16[32,5120]{1,0:T(8,128)(2,1)S(1)}, u32[]{:S(2)}, u32[]{:S(2)}) %collective-permute-start.13) | collective-permute-done | bytes 327712 | tf_op jit(solution)/shard_map/ppermute | solution.py:72
  147.6 0.7 bitcast_dynamic-update-slice_fusion.1
  148.4 0.7 bitcast_dynamic-update-slice_fusion
  (40 shorter events, 0.7 us)
Async XLA Ops:
  0.6 24.1 %copy-start = (bf16[256,5120]{1,0:T(8,128)(2,1)S(1)}, bf16[256,5120]{1,0:T(8,128)(2,1)}, u32[]{:S(2)}) copy-start(bf16[256,5120]{1,0:T(8,128)(2,1)} %param.5) | copy-start | bytes 7864324
  0.6 22.4 %copy-start.1 = (s32[64]{0:T(128)S(1)}, s32[64]{0:T(128)}, u32[]{:S(2)}) copy-start(s32[64]{0:T(128)} %param.7) | copy-start | bytes 772
  6.7 27.7 %all-to-all-start = ((bf16[64,4,768]{2,1,0:T(4,128)(2,1)}), bf16[64,4,768]{2,1,0:T(4,128)(2,1)S(1)}, u32[]{:S(2)}, u32[]{:S(2)}) async-start(bf16[64,4,768]{2,1,0:T(4,128)(2,1)} %all_to_all.16), calls=%async_computation | async-start | bytes 786432 | tf_op jit(solution)/shard_map/all_to_all | solution.py:102
  36.9 6.2 %collective-permute-start = (f32[4,256]{1,0:T(4,128)S(1)}, f32[4,256]{1,0:T(4,128)S(1)}, u32[]{:S(2)}, u32[]{:S(2)}) collective-permute-start(f32[4,256]{1,0:T(4,128)S(1)} %pad_maximum_fusion), channel_id=1, source_target_pairs={{0,1},{1,2},{2,3},{3,0},{4,5},{5,6},{6,7},{7,4},{8,9},{9,10},{10,1... | collective-permute-start | bytes 12296 | tf_op jit(solution)/shard_map/ppermute | solution.py:44
  38.2 4.9 %collective-permute-start.1 = (f32[4,256]{1,0:T(4,128)S(1)}, f32[4,256]{1,0:T(4,128)S(1)}, u32[]{:S(2)}, u32[]{:S(2)}) collective-permute-start(f32[4,256]{1,0:T(4,128)S(1)} %pad_maximum_fusion), channel_id=1, source_target_pairs={{0,2},{1,3},{2,0},{3,1},{4,6},{5,7},{6,4},{7,5},{8,10},{9,11},{10,... | collective-permute-start | bytes 12296 | tf_op jit(solution)/shard_map/ppermute | solution.py:44
  40.6 2.8 %collective-permute-start.2 = (f32[4,256]{1,0:T(4,128)S(1)}, f32[4,256]{1,0:T(4,128)S(1)}, u32[]{:S(2)}, u32[]{:S(2)}) collective-permute-start(f32[4,256]{1,0:T(4,128)S(1)} %pad_maximum_fusion), channel_id=1, source_target_pairs={{0,3},{1,0},{2,1},{3,2},{4,7},{5,4},{6,5},{7,6},{8,11},{9,8},{10,9... | collective-permute-start | bytes 12296 | tf_op jit(solution)/shard_map/ppermute | solution.py:44
  50.0 1.7 %copy-start.2 = (f32[128,5120]{1,0:T(8,128)}, f32[128,5120]{1,0:T(8,128)S(1)}, u32[]{:S(2)}) copy-start(f32[128,5120]{1,0:T(8,128)S(1)} %get-tuple-element.16) | copy-start | bytes 7864324
  50.0 2.7 %copy-start.4 = (f32[128,5120]{1,0:T(8,128)}, f32[128,5120]{1,0:T(8,128)S(1)}, u32[]{:S(2)}) copy-start(f32[128,5120]{1,0:T(8,128)S(1)} %get-tuple-element.17) | copy-start | bytes 7864324
  51.0 16.0 %collective-permute-start.3 = (f32[32,5120]{1,0:T(8,128)}, f32[32,5120]{1,0:T(8,128)}, u32[]{:S(2)}, u32[]{:S(2)}) collective-permute-start(f32[32,5120]{1,0:T(8,128)} %dynamic-slice_bitcast_fusion.1), channel_id=1, source_target_pairs={{0,1},{1,2},{2,3},{3,0},{4,5},{5,6},{6,7},{7,4},{8,9},{9,10},{10,1... | collective-permute-start | bytes 1966088 | tf_op jit(solution)/shard_map/ppermute | solution.py:64
  52.7 15.7 %collective-permute-start.6 = (f32[32,5120]{1,0:T(8,128)}, f32[32,5120]{1,0:T(8,128)S(1)}, u32[]{:S(2)}, u32[]{:S(2)}) collective-permute-start(f32[32,5120]{1,0:T(8,128)} %dynamic-slice_bitcast_fusion), channel_id=1, source_target_pairs={{0,3},{1,0},{2,1},{3,2},{4,7},{5,4},{6,5},{7,6},{8,11},{9,8},{10,9... | collective-permute-start | bytes 1966088 | tf_op jit(solution)/shard_map/ppermute | solution.py:65
  55.0 29.6 %copy-start.3 = (f32[128,5120]{1,0:T(8,128)S(1)}, f32[128,5120]{1,0:T(8,128)}, u32[]{:S(2)}) copy-start(f32[128,5120]{1,0:T(8,128)} %copy-done.2) | copy-start | bytes 7864324
  68.3 14.9 %collective-permute-start.4 = (f32[32,5120]{1,0:T(8,128)S(1)}, f32[32,5120]{1,0:T(8,128)S(1)}, u32[]{:S(2)}, u32[]{:S(2)}) collective-permute-start(f32[32,5120]{1,0:T(8,128)S(1)} %bitcast_add_fusion.5), channel_id=1, source_target_pairs={{0,1},{1,2},{2,3},{3,0},{4,5},{5,6},{6,7},{7,4},{8,9},{9,10},{10,1... | collective-permute-start | bytes 1966088 | tf_op jit(solution)/shard_map/ppermute | solution.py:64
  69.6 14.9 %collective-permute-start.7 = (f32[32,5120]{1,0:T(8,128)S(1)}, f32[32,5120]{1,0:T(8,128)S(1)}, u32[]{:S(2)}, u32[]{:S(2)}) collective-permute-start(f32[32,5120]{1,0:T(8,128)S(1)} %bitcast_add_fusion.2), channel_id=1, source_target_pairs={{0,3},{1,0},{2,1},{3,2},{4,7},{5,4},{6,5},{7,6},{8,11},{9,8},{10,9... | collective-permute-start | bytes 1966088 | tf_op jit(solution)/shard_map/ppermute | solution.py:65
  84.5 14.1 %collective-permute-start.5 = (f32[32,5120]{1,0:T(8,128)S(1)}, f32[32,5120]{1,0:T(8,128)S(1)}, u32[]{:S(2)}, u32[]{:S(2)}) collective-permute-start(f32[32,5120]{1,0:T(8,128)S(1)} %bitcast_add_fusion.4), channel_id=1, source_target_pairs={{0,1},{1,2},{2,3},{3,0},{4,5},{5,6},{6,7},{7,4},{8,9},{9,10},{10,1... | collective-permute-start | bytes 1966088 | tf_op jit(solution)/shard_map/ppermute | solution.py:64
  84.6 15.4 %collective-permute-start.8 = (f32[32,5120]{1,0:T(8,128)S(1)}, f32[32,5120]{1,0:T(8,128)S(1)}, u32[]{:S(2)}, u32[]{:S(2)}) collective-permute-start(f32[32,5120]{1,0:T(8,128)S(1)} %bitcast_add_fusion.1), channel_id=1, source_target_pairs={{0,3},{1,0},{2,1},{3,2},{4,7},{5,4},{6,5},{7,6},{8,11},{9,8},{10,9... | collective-permute-start | bytes 1966088 | tf_op jit(solution)/shard_map/ppermute | solution.py:65
  100.0 28.7 %collective-permute-start.9 = (bf16[32,5120]{1,0:T(8,128)(2,1)S(1)}, bf16[32,5120]{1,0:T(8,128)(2,1)}, u32[]{:S(2)}, u32[]{:S(2)}) collective-permute-start(bf16[32,5120]{1,0:T(8,128)(2,1)S(1)} %get-tuple-element.13), channel_id=1, source_target_pairs={{0,1},{1,2},{2,3},{3,0},{4,5},{5,6},{6,7},{7,4},{8,9},{9,10},{10,1... | collective-permute-start | bytes 983048 | tf_op jit(solution)/shard_map/ppermute | solution.py:72
  100.2 1.5 %copy-start.5 = (bf16[8,32,5120]{2,1,0:T(8,128)(2,1)}, bf16[8,32,5120]{2,1,0:T(8,128)(2,1)S(1)}, u32[]{:S(2)}) copy-start(bf16[8,32,5120]{2,1,0:T(8,128)(2,1)S(1)} %get-tuple-element.10) | copy-start | bytes 7864324
  101.7 27.0 %collective-permute-start.10 = (bf16[32,5120]{1,0:T(8,128)(2,1)S(1)}, bf16[32,5120]{1,0:T(8,128)(2,1)}, u32[]{:S(2)}, u32[]{:S(2)}) collective-permute-start(bf16[32,5120]{1,0:T(8,128)(2,1)S(1)} %get-tuple-element.11), channel_id=1, source_target_pairs={{0,3},{1,0},{2,1},{3,2},{4,7},{5,4},{6,5},{7,6},{8,11},{9,8},{10,9... | collective-permute-start | bytes 983048 | tf_op jit(solution)/shard_map/ppermute | solution.py:73
  106.0 20.8 %all-to-all-start.1 = ((f32[64,1,4]{2,1,0:T(1,128)}), f32[64,1,4]{2,1,0:T(1,128)S(1)}, u32[]{:S(2)}, u32[]{:S(2)}) async-start(f32[64,1,4]{2,1,0:T(1,128)} %bitcast.33), calls=%async_computation.1 | async-start | bytes 65536 | tf_op jit(solution)/shard_map/all_to_all | solution.py:112
  128.6 10.0 %collective-permute-start.11 = (bf16[32,5120]{1,0:T(8,128)(2,1)}, bf16[32,5120]{1,0:T(8,128)(2,1)S(1)}, u32[]{:S(2)}, u32[]{:S(2)}) collective-permute-start(bf16[32,5120]{1,0:T(8,128)(2,1)} %collective-permute-done.9), channel_id=1, source_target_pairs={{0,1},{1,2},{2,3},{3,0},{4,5},{5,6},{6,7},{7,4},{8,9},{9,10},{10,1... | collective-permute-start | bytes 983048 | tf_op jit(solution)/shard_map/ppermute | solution.py:72
  128.7 10.0 %collective-permute-start.12 = (bf16[32,5120]{1,0:T(8,128)(2,1)}, bf16[32,5120]{1,0:T(8,128)(2,1)S(1)}, u32[]{:S(2)}, u32[]{:S(2)}) collective-permute-start(bf16[32,5120]{1,0:T(8,128)(2,1)} %collective-permute-done.10), channel_id=1, source_target_pairs={{0,3},{1,0},{2,1},{3,2},{4,7},{5,4},{6,5},{7,6},{8,11},{9,8},{10,9... | collective-permute-start | bytes 983048 | tf_op jit(solution)/shard_map/ppermute | solution.py:73
  138.7 9.0 %collective-permute-start.13 = (bf16[32,5120]{1,0:T(8,128)(2,1)S(1)}, bf16[32,5120]{1,0:T(8,128)(2,1)S(1)}, u32[]{:S(2)}, u32[]{:S(2)}) collective-permute-start(bf16[32,5120]{1,0:T(8,128)(2,1)S(1)} %collective-permute-done.11), channel_id=1, source_target_pairs={{0,1},{1,2},{2,3},{3,0},{4,5},{5,6},{6,7},{7,4},{8,9},{9,10},{10,1... | collective-permute-start | bytes 983048 | tf_op jit(solution)/shard_map/ppermute | solution.py:72
  138.7 9.7 %collective-permute-start.14 = (bf16[32,5120]{1,0:T(8,128)(2,1)S(1)}, bf16[32,5120]{1,0:T(8,128)(2,1)S(1)}, u32[]{:S(2)}, u32[]{:S(2)}) collective-permute-start(bf16[32,5120]{1,0:T(8,128)(2,1)S(1)} %collective-permute-done.12), channel_id=1, source_target_pairs={{0,3},{1,0},{2,1},{3,2},{4,7},{5,4},{6,5},{7,6},{8,11},{9,8},{10,9... | collective-permute-start | bytes 983048 | tf_op jit(solution)/shard_map/ppermute | solution.py:73

commit v10 on v9

--- a/solution.py
+++ b/solution.py
@@ -111,8 +111,12 @@
     div_out = jnp.take(row_div.reshape(slot_depth, shards), column_of, axis=1, mode="clip").T
     div_in = lax.all_to_all(div_out, "dp", split_axis=0, concat_axis=0, tiled=True)
     packed = jnp.arange(balanced, dtype=jnp.int32) * shards + inverse[myself]
-    owner = jnp.sum((offsets[None, :] <= packed[:, None]).astype(jnp.int32), axis=1) - 1
-    row_kl = div_in[owner, (packed - offsets[owner]) // shards]
+    started = offsets[None, :] <= packed[:, None]
+    owner = jnp.sum(started.astype(jnp.int32), axis=1) - 1
+    owner_offset = jnp.max(jnp.where(started, offsets[None, :], 0), axis=1)
+    flat = owner * slot_depth + (packed - owner_offset) // shards
+    hit = flat[:, None] == jnp.arange(shards * slot_depth, dtype=jnp.int32)[None, :]
+    row_kl = jnp.sum(jnp.where(hit, div_in.reshape(1, -1), 0.0), axis=1)
     return row_grad, row_kl
 
 

time: 150 us -> 136 us (0.907)
  the two profiles are of different devices: /device:TPU:1 before, /device:TPU:6 now
where the time goes in v10:
time: 136 us; the launch traced here: 135 us
  waiting for transfers between devices  46.7 us (34%)
  starting transfers between devices  41.2 us (30%)
  local copies, waits for them, and re-layouts  17.7 us (13%)
  matrix products  16 us (12%)
  other arithmetic  12.3 us (9%)
    ppermute x6, waiting for transfers between devices, ring_all_reduce(): up = lax.ppermute(up, 'vocab', forward)  29.4 us
    ppermute x6, starting transfers between devices, ring_all_reduce(): up = lax.ppermute(up, 'vocab', forward)  17.8 us
    all_to_all x1, starting transfers between devices, body(): lax.all_to_all(outgoing, 'dp', split_axis=0, concat_axis=0, tiled=True)  12.1 us
    ppermute x6, waiting for transfers between devices, ring_all_reduce(): down = lax.ppermute(down, 'vocab', backward)  9.07 us
    all_to_all x1, starting transfers between devices, body(): lax.all_to_all(div_out, 'dp', split_axis=0, concat_axis=0, tiled=True)  6.98 us
    dot_general x1, matrix products, divergence(): logits = jnp.dot(row_block, weight, preferred_element_type=jnp.float32)  6.3 us
    dot_general x1, matrix products, divergence(): lax.dot_general(grad_logits, weight, (((1,), (1,)), ((), ())), preferred_...  6.11 us
    ppermute x3, waiting for transfers between devices, exchange_stats(): got = lax.ppermute(local, 'vocab', pairs)  4.81 us
  transfers between devices with their start and end apart: 17, of which 13 were waited for; matrix products, arithmetic and copies ran while one was open for 20% of the time, Pallas kernels for 0%

profile of v10, /device:TPU:6, one launch (start us, length us, event | category | flops | bytes accessed | tf_op | source)
XLA Modules:
  0.0 134.9 jit_solution(16817172967110200898)
XLA Ops:
  0.7 0.9 select_reduce_fusion.1
  1.6 0.8 copy.16
  2.4 0.1 reduce.3
  2.5 0.6 dynamic_slice.37
  3.1 1.3 and_select_fusion.2
  4.5 0.1 min.15
  4.6 1.2 convolution_convert_fusion.1
  5.9 0.8 all_to_all.14
  6.7 12.1 %all-to-all-start = ((bf16[64,4,768]{2,1,0:T(4,128)(2,1)}), bf16[64,4,768]{2,1,0:T(4,128)(2,1)S(1)}, u32[]{:S(2)}, u32[]{:S(2)}) async-start(bf16[64,4,768]{2,1,0:T(4,128)(2,1)} %all_to_all.14), calls=%async_computation | async-start | bytes 786432 | tf_op jit(solution)/shard_map/all_to_all | solution.py:102
  18.9 1.2 dynamic_slice.35
  20.1 0.6 multiply_add_fusion.1
  20.8 0.6 dynamic_slice.36
  21.4 0.7 fusion.18
  22.0 0.8 gather_fusion
  23.0 0.6 iota_compare_fusion.6
  23.7 6.3 %fusion.29 = (f32[256]{0:T(256)S(1)}, f32[256,768]{1,0:T(8,128)}) fusion(bf16[256,5120]{1,0:T(8,128)(2,1)S(1)} %copy-done, bf16[5120,768]{1,0:T(8,128)(2,1)} %param.8), kind=kOutput, calls=%fused_computation.97 | convolution fusion | flops 2013462272 | bytes 11273216 | tf_op jit(solution)/shard_map/dot_general | solution.py:10
  30.0 3.3 %all-to-all-done = bf16[64,4,768]{2,1,0:T(4,128)(2,1)S(1)} async-done(((bf16[64,4,768]{2,1,0:T(4,128)(2,1)}), bf16[64,4,768]{2,1,0:T(4,128)(2,1)S(1)}, u32[]{:S(2)}, u32[]{:S(2)}) %all-to-all-start) | async-done | bytes 393248 | tf_op jit(solution)/shard_map/all_to_all | solution.py:102
  33.4 2.3 %exponential_reduce_fusion = (f32[256]{0:T(256)S(1)}, f32[256]{0:T(256)S(1)}, f32[256]{0:T(256)S(1)}, f32[256,768]{1,0:T(8,128)}) fusion(f32[256,768]{1,0:T(8,128)} %get-tuple-element.21, f32[256]{0:T(256)S(1)} %get-tuple-element.20, bf16[256,768]{1,0:T(8,128)(2,1)S(1)} %all_to_all.16, s32[256]{0:T(256)S(1)} %add.312), kind=kOutput, calls=%fused_computation.7 | convolution fusion | flops 102300928 | bytes 1971200 | tf_op jit(solution)/shard_map/dot_general | solution.py:107
  35.8 0.6 collective-permute-start
  36.3 2.4 %collective-permute-start.1 = (f32[4,256]{1,0:T(4,128)S(1)}, f32[4,256]{1,0:T(4,128)S(1)}, u32[]{:S(2)}, u32[]{:S(2)}) collective-permute-start(f32[4,256]{1,0:T(4,128)S(1)} %pad_maximum_fusion), channel_id=1, source_target_pairs={{0,2},{1,3},{2,0},{3,1},{4,6},{5,7},{6,4},{7,5},{8,10},{9,11},{10,... | collective-permute-start | bytes 12296 | tf_op jit(solution)/shard_map/ppermute | solution.py:44
  38.7 0.7 collective-permute-done
  39.5 2.0 %collective-permute-done.1 = f32[4,256]{1,0:T(4,128)S(1)} collective-permute-done((f32[4,256]{1,0:T(4,128)S(1)}, f32[4,256]{1,0:T(4,128)S(1)}, u32[]{:S(2)}, u32[]{:S(2)}) %collective-permute-start.1) | collective-permute-done | bytes 4128 | tf_op jit(solution)/shard_map/ppermute | solution.py:44
  41.4 2.1 %collective-permute-done.2 = f32[4,256]{1,0:T(4,128)S(1)} collective-permute-done((f32[4,256]{1,0:T(4,128)S(1)}, f32[4,256]{1,0:T(4,128)S(1)}, u32[]{:S(2)}, u32[]{:S(2)}) %collective-permute-start.2) | collective-permute-done | bytes 4128 | tf_op jit(solution)/shard_map/ppermute | solution.py:44
  43.7 6.1 %fusion.3 = f32[256,5120]{1,0:T(8,128)S(1)} fusion(bf16[5120,768]{1,0:T(8,128)(2,1)} %param.8, f32[256,768]{1,0:T(8,128)} %get-tuple-element.21, f32[256,768]{1,0:T(8,128)} %get-tuple-element.22, f32[256]{0:T(256)S(1)} %get-tuple-element.11, f32[256]{0:T(256)S(1)} %get-tuple-element.7, pred[256]{0:T(512)(128)(4,1)S(1)} %iota_compare_fusion.6), kind=kOutput, calls=%fused_computation.19 | convolution fusion | flops 2014445568 | bytes 14682368 | tf_op jit(solution)/shard_map/dot_general | solution.py:30
  49.8 0.4 fusion.28
  50.2 1.0 dynamic-slice_bitcast_fusion.1
  51.2 0.6 collective-permute-start.3
  51.8 0.1 copy-done.2
  51.9 1.1 dynamic-slice_bitcast_fusion
  52.9 1.1 collective-permute-start.6
  54.3 0.6 fusion.13
  54.8 1.2 gather_fusion.1
  56.0 7.0 %all-to-all-start.1 = ((f32[64,1,4]{2,1,0:T(1,128)}), f32[64,1,4]{2,1,0:T(1,128)S(1)}, u32[]{:S(2)}, u32[]{:S(2)}) async-start(f32[64,1,4]{2,1,0:T(1,128)} %bitcast.33), calls=%async_computation.1 | async-start | bytes 65536 | tf_op jit(solution)/shard_map/all_to_all | solution.py:112
  63.0 3.5 %collective-permute-done.3 = f32[32,5120]{1,0:T(8,128)} collective-permute-done((f32[32,5120]{1,0:T(8,128)}, f32[32,5120]{1,0:T(8,128)}, u32[]{:S(2)}, u32[]{:S(2)}) %collective-permute-start.3) | collective-permute-done | bytes 655392 | tf_op jit(solution)/shard_map/ppermute | solution.py:64
  66.5 1.4 %bitcast_add_fusion.5 = f32[32,5120]{1,0:T(8,128)S(1)} fusion(f32[32,5120]{1,0:T(8,128)} %collective-permute-done.3, f32[4,32,5120]{2,1,0:T(8,128)} %bitcast.80, s32[]{:T(128)S(6)} %select_n.214), kind=kLoop, calls=%fused_computation.16 | loop fusion | flops 163840 | bytes 1966084 | tf_op jit(solution)/shard_map/add | solution.py:66
  67.9 2.4 %collective-permute-start.4 = (f32[32,5120]{1,0:T(8,128)S(1)}, f32[32,5120]{1,0:T(8,128)S(1)}, u32[]{:S(2)}, u32[]{:S(2)}) collective-permute-start(f32[32,5120]{1,0:T(8,128)S(1)} %bitcast_add_fusion.5), channel_id=1, source_target_pairs={{0,1},{1,2},{2,3},{3,0},{4,5},{5,6},{6,7},{7,4},{8,9},{9,10},{10,1... | collective-permute-start | bytes 1966088 | tf_op jit(solution)/shard_map/ppermute | solution.py:64
  70.3 1.2 bitcast_add_fusion.2
  71.5 10.8 %collective-permute-done.4 = f32[32,5120]{1,0:T(8,128)S(1)} collective-permute-done((f32[32,5120]{1,0:T(8,128)S(1)}, f32[32,5120]{1,0:T(8,128)S(1)}, u32[]{:S(2)}, u32[]{:S(2)}) %collective-permute-start.4) | collective-permute-done | bytes 655392 | tf_op jit(solution)/shard_map/ppermute | solution.py:64
  82.3 1.2 bitcast_add_fusion.4
  83.5 3.7 %collective-permute-start.5 = (f32[32,5120]{1,0:T(8,128)S(1)}, f32[32,5120]{1,0:T(8,128)S(1)}, u32[]{:S(2)}, u32[]{:S(2)}) collective-permute-start(f32[32,5120]{1,0:T(8,128)S(1)} %bitcast_add_fusion.4), channel_id=1, source_target_pairs={{0,1},{1,2},{2,3},{3,0},{4,5},{5,6},{6,7},{7,4},{8,9},{9,10},{10,1... | collective-permute-start | bytes 1966088 | tf_op jit(solution)/shard_map/ppermute | solution.py:64
  87.3 11.0 %collective-permute-done.5 = f32[32,5120]{1,0:T(8,128)S(1)} collective-permute-done((f32[32,5120]{1,0:T(8,128)S(1)}, f32[32,5120]{1,0:T(8,128)S(1)}, u32[]{:S(2)}, u32[]{:S(2)}) %collective-permute-start.5) | collective-permute-done | bytes 655392 | tf_op jit(solution)/shard_map/ppermute | solution.py:64
  98.3 0.3 broadcast_in_dim.148
  98.6 1.2 bitcast_dynamic-update-slice_fusion.7
  99.8 3.8 %collective-permute-start.9 = (bf16[32,5120]{1,0:T(8,128)(2,1)S(1)}, bf16[32,5120]{1,0:T(8,128)(2,1)}, u32[]{:S(2)}, u32[]{:S(2)}) collective-permute-start(bf16[32,5120]{1,0:T(8,128)(2,1)S(1)} %get-tuple-element.15), channel_id=1, source_target_pairs={{0,1},{1,2},{2,3},{3,0},{4,5},{5,6},{6,7},{7,4},{8,9},{9,10},{10,1... | collective-permute-start | bytes 983048 | tf_op jit(solution)/shard_map/ppermute | solution.py:72
  103.7 1.5 %copy-done.5 = bf16[8,32,5120]{2,1,0:T(8,128)(2,1)} copy-done((bf16[8,32,5120]{2,1,0:T(8,128)(2,1)}, bf16[8,32,5120]{2,1,0:T(8,128)(2,1)S(1)}, u32[]{:S(2)}) %copy-start.5) | copy-done | bytes 2621464
  105.1 0.7 fusion.23
  105.8 0.5 broadcast.261
  106.4 0.7 reduce.7
  107.1 0.1 broadcast_in_dim.170
  107.2 0.7 select_reduce_fusion
  107.9 1.2 collective-permute-done.9
  109.1 3.8 %collective-permute-start.11 = (bf16[32,5120]{1,0:T(8,128)(2,1)}, bf16[32,5120]{1,0:T(8,128)(2,1)S(1)}, u32[]{:S(2)}, u32[]{:S(2)}) collective-permute-start(bf16[32,5120]{1,0:T(8,128)(2,1)} %collective-permute-done.9), channel_id=1, source_target_pairs={{0,1},{1,2},{2,3},{3,0},{4,5},{5,6},{6,7},{7,4},{8,9},{9,10},{10,1... | collective-permute-start | bytes 983048 | tf_op jit(solution)/shard_map/ppermute | solution.py:72
  112.9 1.9 %collective-permute-done.10 = bf16[32,5120]{1,0:T(8,128)(2,1)} collective-permute-done((bf16[32,5120]{1,0:T(8,128)(2,1)S(1)}, bf16[32,5120]{1,0:T(8,128)(2,1)}, u32[]{:S(2)}, u32[]{:S(2)}) %collective-permute-start.10) | collective-permute-done | bytes 327712 | tf_op jit(solution)/shard_map/ppermute | solution.py:73
  114.7 1.7 %bitcast_dynamic-update-slice_fusion.5 = bf16[8,32,5120]{2,1,0:T(8,128)(2,1)} fusion(bf16[8,32,5120]{2,1,0:T(8,128)(2,1)} %copy-done.5, s32[]{:T(128)S(6)} %select_n.227, bf16[32,5120]{1,0:T(8,128)(2,1)} %collective-permute-done.9), kind=kLoop, calls=%fused_computation.30 | loop fusion | bytes 655364 | tf_op jit(solution)/shard_map/jit(dynamic_update_index_in_dim)/dynamic_update_slice | solution.py:78
  116.4 1.7 %bitcast_dynamic-update-slice_fusion.4 = bf16[8,32,5120]{2,1,0:T(8,128)(2,1)} fusion(bf16[8,32,5120]{2,1,0:T(8,128)(2,1)} %bitcast_dynamic-update-slice_fusion.5, s32[]{:T(128)S(6)} %select_n.228, bf16[32,5120]{1,0:T(8,128)(2,1)} %collective-permute-done.10), kind=kLoop, calls=%fused_computation.29 | loop fusion | bytes 655364 | tf_op jit(solution)/shard_map/jit(dynamic_update_index_in_dim)/dynamic_update_slice | solution.py:79
  118.1 2.0 %collective-permute-done.11 = bf16[32,5120]{1,0:T(8,128)(2,1)S(1)} collective-permute-done((bf16[32,5120]{1,0:T(8,128)(2,1)}, bf16[32,5120]{1,0:T(8,128)(2,1)S(1)}, u32[]{:S(2)}, u32[]{:S(2)}) %collective-permute-start.11) | collective-permute-done | bytes 327712 | tf_op jit(solution)/shard_map/ppermute | solution.py:72
  120.1 3.6 %collective-permute-start.13 = (bf16[32,5120]{1,0:T(8,128)(2,1)S(1)}, bf16[32,5120]{1,0:T(8,128)(2,1)S(1)}, u32[]{:S(2)}, u32[]{:S(2)}) collective-permute-start(bf16[32,5120]{1,0:T(8,128)(2,1)S(1)} %collective-permute-done.11), channel_id=1, source_target_pairs={{0,1},{1,2},{2,3},{3,0},{4,5},{5,6},{6,7},{7,4},{8,9},{9,10},{10,1... | collective-permute-start | bytes 983048 | tf_op jit(solution)/shard_map/ppermute | solution.py:72
  123.7 2.1 %collective-permute-done.12 = bf16[32,5120]{1,0:T(8,128)(2,1)S(1)} collective-permute-done((bf16[32,5120]{1,0:T(8,128)(2,1)}, bf16[32,5120]{1,0:T(8,128)(2,1)S(1)}, u32[]{:S(2)}, u32[]{:S(2)}) %collective-permute-start.12) | collective-permute-done | bytes 327712 | tf_op jit(solution)/shard_map/ppermute | solution.py:73
  125.8 0.7 bitcast_dynamic-update-slice_fusion.3
  126.6 0.7 bitcast_dynamic-update-slice_fusion.2
  127.3 1.0 collective-permute-done.13
  128.3 0.7 bitcast_dynamic-update-slice_fusion.1
  129.0 5.1 %collective-permute-done.14 = bf16[32,5120]{1,0:T(8,128)(2,1)S(1)} collective-permute-done((bf16[32,5120]{1,0:T(8,128)(2,1)S(1)}, bf16[32,5120]{1,0:T(8,128)(2,1)S(1)}, u32[]{:S(2)}, u32[]{:S(2)}) %collective-permute-start.14) | collective-permute-done | bytes 327712 | tf_op jit(solution)/shard_map/ppermute | solution.py:73
  134.1 0.7 bitcast_dynamic-update-slice_fusion
  (40 shorter events, 1.2 us)
Async XLA Ops:
  0.6 23.0 %copy-start = (bf16[256,5120]{1,0:T(8,128)(2,1)S(1)}, bf16[256,5120]{1,0:T(8,128)(2,1)}, u32[]{:S(2)}) copy-start(bf16[256,5120]{1,0:T(8,128)(2,1)} %param.5) | copy-start | bytes 7864324
  0.6 21.4 %copy-start.1 = (s32[64]{0:T(128)S(1)}, s32[64]{0:T(128)}, u32[]{:S(2)}) copy-start(s32[64]{0:T(128)} %param.7) | copy-start | bytes 772
  6.7 26.6 %all-to-all-start = ((bf16[64,4,768]{2,1,0:T(4,128)(2,1)}), bf16[64,4,768]{2,1,0:T(4,128)(2,1)S(1)}, u32[]{:S(2)}, u32[]{:S(2)}) async-start(bf16[64,4,768]{2,1,0:T(4,128)(2,1)} %all_to_all.14), calls=%async_computation | async-start | bytes 786432 | tf_op jit(solution)/shard_map/all_to_all | solution.py:102
  35.8 3.7 %collective-permute-start = (f32[4,256]{1,0:T(4,128)S(1)}, f32[4,256]{1,0:T(4,128)S(1)}, u32[]{:S(2)}, u32[]{:S(2)}) collective-permute-start(f32[4,256]{1,0:T(4,128)S(1)} %pad_maximum_fusion), channel_id=1, source_target_pairs={{0,1},{1,2},{2,3},{3,0},{4,5},{5,6},{6,7},{7,4},{8,9},{9,10},{10,1... | collective-permute-start | bytes 12296 | tf_op jit(solution)/shard_map/ppermute | solution.py:44
  36.3 5.1 %collective-permute-start.1 = (f32[4,256]{1,0:T(4,128)S(1)}, f32[4,256]{1,0:T(4,128)S(1)}, u32[]{:S(2)}, u32[]{:S(2)}) collective-permute-start(f32[4,256]{1,0:T(4,128)S(1)} %pad_maximum_fusion), channel_id=1, source_target_pairs={{0,2},{1,3},{2,0},{3,1},{4,6},{5,7},{6,4},{7,5},{8,10},{9,11},{10,... | collective-permute-start | bytes 12296 | tf_op jit(solution)/shard_map/ppermute | solution.py:44
  38.7 4.8 %collective-permute-start.2 = (f32[4,256]{1,0:T(4,128)S(1)}, f32[4,256]{1,0:T(4,128)S(1)}, u32[]{:S(2)}, u32[]{:S(2)}) collective-permute-start(f32[4,256]{1,0:T(4,128)S(1)} %pad_maximum_fusion), channel_id=1, source_target_pairs={{0,3},{1,0},{2,1},{3,2},{4,7},{5,4},{6,5},{7,6},{8,11},{9,8},{10,9... | collective-permute-start | bytes 12296 | tf_op jit(solution)/shard_map/ppermute | solution.py:44
  50.2 1.7 %copy-start.2 = (f32[128,5120]{1,0:T(8,128)}, f32[128,5120]{1,0:T(8,128)S(1)}, u32[]{:S(2)}) copy-start(f32[128,5120]{1,0:T(8,128)S(1)} %get-tuple-element.18) | copy-start | bytes 7864324
  50.2 2.7 %copy-start.4 = (f32[128,5120]{1,0:T(8,128)}, f32[128,5120]{1,0:T(8,128)S(1)}, u32[]{:S(2)}) copy-start(f32[128,5120]{1,0:T(8,128)S(1)} %get-tuple-element.19) | copy-start | bytes 7864324
  51.2 15.4 %collective-permute-start.3 = (f32[32,5120]{1,0:T(8,128)}, f32[32,5120]{1,0:T(8,128)}, u32[]{:S(2)}, u32[]{:S(2)}) collective-permute-start(f32[32,5120]{1,0:T(8,128)} %dynamic-slice_bitcast_fusion.1), channel_id=1, source_target_pairs={{0,1},{1,2},{2,3},{3,0},{4,5},{5,6},{6,7},{7,4},{8,9},{9,10},{10,1... | collective-permute-start | bytes 1966088 | tf_op jit(solution)/shard_map/ppermute | solution.py:64
  52.9 17.3 %collective-permute-start.6 = (f32[32,5120]{1,0:T(8,128)}, f32[32,5120]{1,0:T(8,128)S(1)}, u32[]{:S(2)}, u32[]{:S(2)}) collective-permute-start(f32[32,5120]{1,0:T(8,128)} %dynamic-slice_bitcast_fusion), channel_id=1, source_target_pairs={{0,3},{1,0},{2,1},{3,2},{4,7},{5,4},{6,5},{7,6},{8,11},{9,8},{10,9... | collective-permute-start | bytes 1966088 | tf_op jit(solution)/shard_map/ppermute | solution.py:65
  56.0 49.8 %all-to-all-start.1 = ((f32[64,1,4]{2,1,0:T(1,128)}), f32[64,1,4]{2,1,0:T(1,128)S(1)}, u32[]{:S(2)}, u32[]{:S(2)}) async-start(f32[64,1,4]{2,1,0:T(1,128)} %bitcast.33), calls=%async_computation.1 | async-start | bytes 65536 | tf_op jit(solution)/shard_map/all_to_all | solution.py:112
  63.0 24.2 %copy-start.3 = (f32[128,5120]{1,0:T(8,128)S(1)}, f32[128,5120]{1,0:T(8,128)}, u32[]{:S(2)}) copy-start(f32[128,5120]{1,0:T(8,128)} %copy-done.2) | copy-start | bytes 7864324
  67.9 14.4 %collective-permute-start.4 = (f32[32,5120]{1,0:T(8,128)S(1)}, f32[32,5120]{1,0:T(8,128)S(1)}, u32[]{:S(2)}, u32[]{:S(2)}) collective-permute-start(f32[32,5120]{1,0:T(8,128)S(1)} %bitcast_add_fusion.5), channel_id=1, source_target_pairs={{0,1},{1,2},{2,3},{3,0},{4,5},{5,6},{6,7},{7,4},{8,9},{9,10},{10,1... | collective-permute-start | bytes 1966088 | tf_op jit(solution)/shard_map/ppermute | solution.py:64
  71.4 15.8 %collective-permute-start.7 = (f32[32,5120]{1,0:T(8,128)S(1)}, f32[32,5120]{1,0:T(8,128)S(1)}, u32[]{:S(2)}, u32[]{:S(2)}) collective-permute-start(f32[32,5120]{1,0:T(8,128)S(1)} %bitcast_add_fusion.2), channel_id=1, source_target_pairs={{0,3},{1,0},{2,1},{3,2},{4,7},{5,4},{6,5},{7,6},{8,11},{9,8},{10,9... | collective-permute-start | bytes 1966088 | tf_op jit(solution)/shard_map/ppermute | solution.py:65
  83.5 14.8 %collective-permute-start.5 = (f32[32,5120]{1,0:T(8,128)S(1)}, f32[32,5120]{1,0:T(8,128)S(1)}, u32[]{:S(2)}, u32[]{:S(2)}) collective-permute-start(f32[32,5120]{1,0:T(8,128)S(1)} %bitcast_add_fusion.4), channel_id=1, source_target_pairs={{0,1},{1,2},{2,3},{3,0},{4,5},{5,6},{6,7},{7,4},{8,9},{9,10},{10,1... | collective-permute-start | bytes 1966088 | tf_op jit(solution)/shard_map/ppermute | solution.py:64
  87.3 16.3 %collective-permute-start.8 = (f32[32,5120]{1,0:T(8,128)S(1)}, f32[32,5120]{1,0:T(8,128)S(1)}, u32[]{:S(2)}, u32[]{:S(2)}) collective-permute-start(f32[32,5120]{1,0:T(8,128)S(1)} %bitcast_add_fusion.1), channel_id=1, source_target_pairs={{0,3},{1,0},{2,1},{3,2},{4,7},{5,4},{6,5},{7,6},{8,11},{9,8},{10,9... | collective-permute-start | bytes 1966088 | tf_op jit(solution)/shard_map/ppermute | solution.py:65
  99.8 9.3 %collective-permute-start.9 = (bf16[32,5120]{1,0:T(8,128)(2,1)S(1)}, bf16[32,5120]{1,0:T(8,128)(2,1)}, u32[]{:S(2)}, u32[]{:S(2)}) collective-permute-start(bf16[32,5120]{1,0:T(8,128)(2,1)S(1)} %get-tuple-element.15), channel_id=1, source_target_pairs={{0,1},{1,2},{2,3},{3,0},{4,5},{5,6},{6,7},{7,4},{8,9},{9,10},{10,1... | collective-permute-start | bytes 983048 | tf_op jit(solution)/shard_map/ppermute | solution.py:72
  103.6 1.5 %copy-start.5 = (bf16[8,32,5120]{2,1,0:T(8,128)(2,1)}, bf16[8,32,5120]{2,1,0:T(8,128)(2,1)S(1)}, u32[]{:S(2)}) copy-start(bf16[8,32,5120]{2,1,0:T(8,128)(2,1)S(1)} %get-tuple-element.12) | copy-start | bytes 7864324
  105.1 9.6 %collective-permute-start.10 = (bf16[32,5120]{1,0:T(8,128)(2,1)S(1)}, bf16[32,5120]{1,0:T(8,128)(2,1)}, u32[]{:S(2)}, u32[]{:S(2)}) collective-permute-start(bf16[32,5120]{1,0:T(8,128)(2,1)S(1)} %get-tuple-element.13), channel_id=1, source_target_pairs={{0,3},{1,0},{2,1},{3,2},{4,7},{5,4},{6,5},{7,6},{8,11},{9,8},{10,9... | collective-permute-start | bytes 983048 | tf_op jit(solution)/shard_map/ppermute | solution.py:73
  109.1 11.1 %collective-permute-start.11 = (bf16[32,5120]{1,0:T(8,128)(2,1)}, bf16[32,5120]{1,0:T(8,128)(2,1)S(1)}, u32[]{:S(2)}, u32[]{:S(2)}) collective-permute-start(bf16[32,5120]{1,0:T(8,128)(2,1)} %collective-permute-done.9), channel_id=1, source_target_pairs={{0,1},{1,2},{2,3},{3,0},{4,5},{5,6},{6,7},{7,4},{8,9},{9,10},{10,1... | collective-permute-start | bytes 983048 | tf_op jit(solution)/shard_map/ppermute | solution.py:72
  114.7 11.1 %collective-permute-start.12 = (bf16[32,5120]{1,0:T(8,128)(2,1)}, bf16[32,5120]{1,0:T(8,128)(2,1)S(1)}, u32[]{:S(2)}, u32[]{:S(2)}) collective-permute-start(bf16[32,5120]{1,0:T(8,128)(2,1)} %collective-permute-done.10), channel_id=1, source_target_pairs={{0,3},{1,0},{2,1},{3,2},{4,7},{5,4},{6,5},{7,6},{8,11},{9,8},{10,9... | collective-permute-start | bytes 983048 | tf_op jit(solution)/shard_map/ppermute | solution.py:73
  120.1 8.2 %collective-permute-start.13 = (bf16[32,5120]{1,0:T(8,128)(2,1)S(1)}, bf16[32,5120]{1,0:T(8,128)(2,1)S(1)}, u32[]{:S(2)}, u32[]{:S(2)}) collective-permute-start(bf16[32,5120]{1,0:T(8,128)(2,1)S(1)} %collective-permute-done.11), channel_id=1, source_target_pairs={{0,1},{1,2},{2,3},{3,0},{4,5},{5,6},{6,7},{7,4},{8,9},{9,10},{10,1... | collective-permute-start | bytes 983048 | tf_op jit(solution)/shard_map/ppermute | solution.py:72
  125.8 8.3 %collective-permute-start.14 = (bf16[32,5120]{1,0:T(8,128)(2,1)S(1)}, bf16[32,5120]{1,0:T(8,128)(2,1)S(1)}, u32[]{:S(2)}, u32[]{:S(2)}) collective-permute-start(bf16[32,5120]{1,0:T(8,128)(2,1)S(1)} %collective-permute-done.12), channel_id=1, source_target_pairs={{0,3},{1,0},{2,1},{3,2},{4,7},{5,4},{6,5},{7,6},{8,11},{9,8},{10,9... | collective-permute-start | bytes 983048 | tf_op jit(solution)/shard_map/ppermute | solution.py:73

commit v11 on v9

--- a/solution.py
+++ b/solution.py
@@ -86,8 +86,8 @@
     source_slots = hidden_rows.shape[0]
     slot_depth = source_slots // shards
     balanced = teacher_logprobs.shape[0]
-    offsets = jnp.cumsum(plan_lengths) - plan_lengths
     classes = jnp.arange(shards, dtype=jnp.int32)
+    offsets = jnp.sum(jnp.where(classes[None, :] < classes[:, None], plan_lengths[None, :], 0), axis=1)
     inverse = jnp.sum(
         jnp.where(shard_of_class[None, :] == classes[:, None], classes[None, :], 0), axis=1
     )
@@ -108,7 +108,8 @@
     live = jnp.arange(source_slots, dtype=jnp.int32) < plan_lengths[myself]
     row_grad, row_div = divergence(hidden_rows, teacher_slots, live, head_weight)
     column_of = (inverse - own_offset) % shards
-    div_out = jnp.take(row_div.reshape(slot_depth, shards), column_of, axis=1, mode="clip").T
+    chosen = column_of[:, None, None] == classes[None, None, :]
+    div_out = jnp.sum(jnp.where(chosen, row_div.reshape(1, slot_depth, shards), 0.0), axis=2)
     div_in = lax.all_to_all(div_out, "dp", split_axis=0, concat_axis=0, tiled=True)
     packed = jnp.arange(balanced, dtype=jnp.int32) * shards + inverse[myself]
     owner = jnp.sum((offsets[None, :] <= packed[:, None]).astype(jnp.int32), axis=1) - 1

time: 150 us -> 147 us (0.980)
    ppermute x6, waiting for transfers between devices: 42.5 us -> 40.8 us  [ring_all_reduce(): up = lax.ppermute(up, 'vocab', forward)]
  transfers between devices with their start and end apart: 17 -> 17, of which waited for: 8 -> 9; matrix products, arithmetic and copies ran while one was open for 19% -> 18% of each run, Pallas kernels for 0% -> 0%
where the time goes in v11:
time: 147 us; the launch traced here: 146 us
  waiting for transfers between devices  54 us (37%)
  starting transfers between devices  46.2 us (31%)
  local copies, waits for them, and re-layouts  19.4 us (13%)
  matrix products  16 us (11%)
  other arithmetic  9.56 us (7%)
    ppermute x6, waiting for transfers between devices, ring_all_reduce(): up = lax.ppermute(up, 'vocab', forward)  40.8 us
    ppermute x6, starting transfers between devices, ring_all_reduce(): down = lax.ppermute(down, 'vocab', backward)  16.9 us
    all_to_all x1, starting transfers between devices, body(): lax.all_to_all(outgoing, 'dp', split_axis=0, concat_axis=0, tiled=True)  13.1 us
    all_to_all x1, starting transfers between devices, body(): lax.all_to_all(div_out, 'dp', split_axis=0, concat_axis=0, tiled=True)  11 us
    all_to_all x1, waiting for transfers between devices, body(): lax.all_to_all(div_out, 'dp', split_axis=0, concat_axis=0, tiled=True)  8.7 us
    dot_general x1, matrix products, divergence(): logits = jnp.dot(row_block, weight, preferred_element_type=jnp.float32)  6.31 us
    dot_general x1, matrix products, divergence(): lax.dot_general(grad_logits, weight, (((1,), (1,)), ((), ())), preferred_...  6.1 us
    ppermute x3, starting transfers between devices, exchange_stats(): got = lax.ppermute(local, 'vocab', pairs)  4.89 us
  transfers between devices with their start and end apart: 17, of which 9 were waited for; matrix products, arithmetic and copies ran while one was open for 18% of the time, Pallas kernels for 0%

profile of v11, /device:TPU:1, one launch (start us, length us, event | category | flops | bytes accessed | tf_op | source)
XLA Modules:
  0.0 146.2 jit_solution(12873858621238809148)
XLA Ops:
  0.7 0.9 select_reduce_fusion.2
  1.6 0.8 select_reduce_fusion.1
  2.4 0.6 dynamic_slice.36
  2.9 0.6 dynamic_slice.37
  3.5 1.2 and_select_fusion.1
  4.8 0.1 min.15
  4.9 1.2 convolution_convert_fusion.1
  6.2 0.8 all_to_all.16
  7.0 13.1 %all-to-all-start = ((bf16[64,4,768]{2,1,0:T(4,128)(2,1)}), bf16[64,4,768]{2,1,0:T(4,128)(2,1)S(1)}, u32[]{:S(2)}, u32[]{:S(2)}) async-start(bf16[64,4,768]{2,1,0:T(4,128)(2,1)} %all_to_all.16), calls=%async_computation | async-start | bytes 786432 | tf_op jit(solution)/shard_map/all_to_all | solution.py:102
  20.2 0.7 fusion.19
  20.9 1.2 dynamic_slice.35
  22.1 0.6 multiply_add_fusion.1
  22.7 0.8 gather_fusion
  23.6 0.1 convert_reduce_fusion
  23.7 0.7 iota_compare_fusion.7
  24.4 0.1 add.370
  24.5 6.3 %fusion.30 = (f32[256]{0:T(256)S(1)}, f32[256,768]{1,0:T(8,128)}) fusion(bf16[256,5120]{1,0:T(8,128)(2,1)S(1)} %copy-done, bf16[5120,768]{1,0:T(8,128)(2,1)} %param.8), kind=kOutput, calls=%fused_computation.103 | convolution fusion | flops 2013462272 | bytes 11273216 | tf_op jit(solution)/shard_map/dot_general | solution.py:10
  30.8 3.9 %all-to-all-done = bf16[64,4,768]{2,1,0:T(4,128)(2,1)S(1)} async-done(((bf16[64,4,768]{2,1,0:T(4,128)(2,1)}), bf16[64,4,768]{2,1,0:T(4,128)(2,1)S(1)}, u32[]{:S(2)}, u32[]{:S(2)}) %all-to-all-start) | async-done | bytes 393248 | tf_op jit(solution)/shard_map/all_to_all | solution.py:102
  34.7 0.1 all_to_all.18
  34.8 2.3 %exponential_reduce_fusion = (f32[256]{0:T(256)S(1)}, f32[256]{0:T(256)S(1)}, f32[256]{0:T(256)S(1)}, f32[256,768]{1,0:T(8,128)}) fusion(f32[256,768]{1,0:T(8,128)} %get-tuple-element.17, f32[256]{0:T(256)S(1)} %get-tuple-element.16, bf16[256,768]{1,0:T(8,128)(2,1)S(1)} %all_to_all.18, s32[256]{0:T(256)S(1)} %add.370), kind=kOutput, calls=%fused_computation.8 | convolution fusion | flops 102300928 | bytes 1971200 | tf_op jit(solution)/shard_map/dot_general | solution.py:107
  37.2 1.3 collective-permute-start
  38.5 2.4 %collective-permute-start.1 = (f32[4,256]{1,0:T(4,128)S(1)}, f32[4,256]{1,0:T(4,128)S(1)}, u32[]{:S(2)}, u32[]{:S(2)}) collective-permute-start(f32[4,256]{1,0:T(4,128)S(1)} %pad_maximum_fusion), channel_id=1, source_target_pairs={{0,2},{1,3},{2,0},{3,1},{4,6},{5,7},{6,4},{7,5},{8,10},{9,11},{10,... | collective-permute-start | bytes 12296 | tf_op jit(solution)/shard_map/ppermute | solution.py:44
  40.9 1.2 collective-permute-start.2
  42.1 1.2 gather_fusion.1
  43.4 0.3 collective-permute-done.2
  43.8 6.1 %fusion.3 = f32[256,5120]{1,0:T(8,128)S(1)} fusion(bf16[5120,768]{1,0:T(8,128)(2,1)} %param.8, f32[256,768]{1,0:T(8,128)} %get-tuple-element.17, f32[256,768]{1,0:T(8,128)} %get-tuple-element.18, f32[256]{0:T(256)S(1)} %get-tuple-element.9, f32[256]{0:T(256)S(1)} %get-tuple-element.7, pred[256]{0:T(512)(128)(4,1)S(1)} %iota_compare_fusion.7), kind=kOutput, calls=%fused_computation.20 | convolution fusion | flops 2014445568 | bytes 14682368 | tf_op jit(solution)/shard_map/dot_general | solution.py:30
  49.9 0.4 fusion.29
  50.3 1.0 dynamic-slice_bitcast_fusion.1
  51.3 0.7 copy-done.2
  52.0 1.1 dynamic-slice_bitcast_fusion
  53.0 2.1 %collective-permute-start.6 = (f32[32,5120]{1,0:T(8,128)}, f32[32,5120]{1,0:T(8,128)S(1)}, u32[]{:S(2)}, u32[]{:S(2)}) collective-permute-start(f32[32,5120]{1,0:T(8,128)} %dynamic-slice_bitcast_fusion), channel_id=1, source_target_pairs={{0,3},{1,0},{2,1},{3,2},{4,7},{5,4},{6,5},{7,6},{8,11},{9,8},{10,9... | collective-permute-start | bytes 1966088 | tf_op jit(solution)/shard_map/ppermute | solution.py:65
  55.1 0.1 add.414
  55.2 0.8 fusion.14
  56.0 11.3 %collective-permute-done.3 = f32[32,5120]{1,0:T(8,128)} collective-permute-done((f32[32,5120]{1,0:T(8,128)}, f32[32,5120]{1,0:T(8,128)}, u32[]{:S(2)}, u32[]{:S(2)}) %collective-permute-start.3) | collective-permute-done | bytes 655392 | tf_op jit(solution)/shard_map/ppermute | solution.py:64
  67.3 1.4 bitcast_add_fusion.5
  68.6 0.1 collective-permute-start.4
  68.7 1.2 bitcast_add_fusion.2
  69.9 2.9 %collective-permute-start.7 = (f32[32,5120]{1,0:T(8,128)S(1)}, f32[32,5120]{1,0:T(8,128)S(1)}, u32[]{:S(2)}, u32[]{:S(2)}) collective-permute-start(f32[32,5120]{1,0:T(8,128)S(1)} %bitcast_add_fusion.2), channel_id=1, source_target_pairs={{0,3},{1,0},{2,1},{3,2},{4,7},{5,4},{6,5},{7,6},{8,11},{9,8},{10,9... | collective-permute-start | bytes 1966088 | tf_op jit(solution)/shard_map/ppermute | solution.py:65
  72.8 10.7 %collective-permute-done.4 = f32[32,5120]{1,0:T(8,128)S(1)} collective-permute-done((f32[32,5120]{1,0:T(8,128)S(1)}, f32[32,5120]{1,0:T(8,128)S(1)}, u32[]{:S(2)}, u32[]{:S(2)}) %collective-permute-start.4) | collective-permute-done | bytes 655392 | tf_op jit(solution)/shard_map/ppermute | solution.py:64
  83.5 0.1 bitcast_add_fusion.4
  83.6 0.1 collective-permute-start.5
  83.7 0.3 collective-permute-done.7
  84.0 3.5 %collective-permute-start.8 = (f32[32,5120]{1,0:T(8,128)S(1)}, f32[32,5120]{1,0:T(8,128)S(1)}, u32[]{:S(2)}, u32[]{:S(2)}) collective-permute-start(f32[32,5120]{1,0:T(8,128)S(1)} %bitcast_add_fusion.1), channel_id=1, source_target_pairs={{0,3},{1,0},{2,1},{3,2},{4,7},{5,4},{6,5},{7,6},{8,11},{9,8},{10,9... | collective-permute-start | bytes 1966088 | tf_op jit(solution)/shard_map/ppermute | solution.py:65
  87.5 10.1 %collective-permute-done.5 = f32[32,5120]{1,0:T(8,128)S(1)} collective-permute-done((f32[32,5120]{1,0:T(8,128)S(1)}, f32[32,5120]{1,0:T(8,128)S(1)}, u32[]{:S(2)}, u32[]{:S(2)}) %collective-permute-start.5) | collective-permute-done | bytes 655392 | tf_op jit(solution)/shard_map/ppermute | solution.py:64
  97.7 0.3 broadcast_in_dim.151
  98.1 0.1 collective-permute-start.9
  98.3 1.5 %copy-done.6 = bf16[8,32,5120]{2,1,0:T(8,128)(2,1)} copy-done((bf16[8,32,5120]{2,1,0:T(8,128)(2,1)}, bf16[8,32,5120]{2,1,0:T(8,128)(2,1)S(1)}, u32[]{:S(2)}) %copy-start.6) | copy-done | bytes 2621464
  99.7 3.1 %collective-permute-start.10 = (bf16[32,5120]{1,0:T(8,128)(2,1)S(1)}, bf16[32,5120]{1,0:T(8,128)(2,1)}, u32[]{:S(2)}, u32[]{:S(2)}) collective-permute-start(bf16[32,5120]{1,0:T(8,128)(2,1)S(1)} %get-tuple-element.11), channel_id=1, source_target_pairs={{0,3},{1,0},{2,1},{3,2},{4,7},{5,4},{6,5},{7,6},{8,11},{9,8},{10,9... | collective-permute-start | bytes 983048 | tf_op jit(solution)/shard_map/ppermute | solution.py:73
  102.8 0.1 select_reduce_fusion
  102.9 0.7 copy.10
  103.6 11.0 %all-to-all-start.1 = ((f32[64,1,4]{2,1,0:T(1,128)}), f32[64,1,4]{2,1,0:T(1,128)S(1)}, u32[]{:S(2)}, u32[]{:S(2)}) async-start(f32[64,1,4]{2,1,0:T(1,128)} %copy.10), calls=%async_computation.1 | async-start | bytes 65536 | tf_op jit(solution)/shard_map/all_to_all | solution.py:113
  114.6 0.6 fusion.23
  115.2 8.7 %all-to-all-done.1 = f32[64,1,4]{2,1,0:T(1,128)S(1)} async-done(((f32[64,1,4]{2,1,0:T(1,128)}), f32[64,1,4]{2,1,0:T(1,128)S(1)}, u32[]{:S(2)}, u32[]{:S(2)}) %all-to-all-start.1) | async-done | bytes 1056 | tf_op jit(solution)/shard_map/all_to_all | solution.py:113
  123.9 1.8 %gather_fusion.2 = f32[128]{0:T(128)} fusion(f32[64,4]{1,0:T(8,128)S(1)} %bitcast.99, s32[128]{0:T(128)S(1)} %fusion.23), kind=kCustom, calls=%fused_computation.2 | custom fusion | bytes 2048 | tf_op jit(solution)/shard_map/gather | solution.py:116
  125.8 2.7 %collective-permute-start.12 = (bf16[32,5120]{1,0:T(8,128)(2,1)}, bf16[32,5120]{1,0:T(8,128)(2,1)S(1)}, u32[]{:S(2)}, u32[]{:S(2)}) collective-permute-start(bf16[32,5120]{1,0:T(8,128)(2,1)} %collective-permute-done.10), channel_id=1, source_target_pairs={{0,3},{1,0},{2,1},{3,2},{4,7},{5,4},{6,5},{7,6},{8,11},{9,8},{10,9... | collective-permute-start | bytes 983048 | tf_op jit(solution)/shard_map/ppermute | solution.py:73
  128.4 1.7 %bitcast_dynamic-update-slice_fusion.5 = bf16[8,32,5120]{2,1,0:T(8,128)(2,1)} fusion(bf16[8,32,5120]{2,1,0:T(8,128)(2,1)} %copy-done.6, s32[]{:T(128)S(6)} %select_n.259, bf16[32,5120]{1,0:T(8,128)(2,1)} %collective-permute-done.9), kind=kLoop, calls=%fused_computation.31 | loop fusion | bytes 655364 | tf_op jit(solution)/shard_map/jit(dynamic_update_index_in_dim)/dynamic_update_slice | solution.py:78
  130.1 1.7 %bitcast_dynamic-update-slice_fusion.4 = bf16[8,32,5120]{2,1,0:T(8,128)(2,1)} fusion(bf16[8,32,5120]{2,1,0:T(8,128)(2,1)} %bitcast_dynamic-update-slice_fusion.5, s32[]{:T(128)S(6)} %select_n.260, bf16[32,5120]{1,0:T(8,128)(2,1)} %collective-permute-done.10), kind=kLoop, calls=%fused_computation.30 | loop fusion | bytes 655364 | tf_op jit(solution)/shard_map/jit(dynamic_update_index_in_dim)/dynamic_update_slice | solution.py:79
  131.9 3.9 %collective-permute-done.11 = bf16[32,5120]{1,0:T(8,128)(2,1)S(1)} collective-permute-done((bf16[32,5120]{1,0:T(8,128)(2,1)}, bf16[32,5120]{1,0:T(8,128)(2,1)S(1)}, u32[]{:S(2)}, u32[]{:S(2)}) %collective-permute-start.11) | collective-permute-done | bytes 327712 | tf_op jit(solution)/shard_map/ppermute | solution.py:72
  135.8 2.7 %collective-permute-start.14 = (bf16[32,5120]{1,0:T(8,128)(2,1)S(1)}, bf16[32,5120]{1,0:T(8,128)(2,1)S(1)}, u32[]{:S(2)}, u32[]{:S(2)}) collective-permute-start(bf16[32,5120]{1,0:T(8,128)(2,1)S(1)} %collective-permute-done.12), channel_id=1, source_target_pairs={{0,3},{1,0},{2,1},{3,2},{4,7},{5,4},{6,5},{7,6},{8,11},{9,8},{10,9... | collective-permute-start | bytes 983048 | tf_op jit(solution)/shard_map/ppermute | solution.py:73
  138.5 0.7 bitcast_dynamic-update-slice_fusion.3
  139.2 0.7 bitcast_dynamic-update-slice_fusion.2
  139.9 4.8 %collective-permute-done.13 = bf16[32,5120]{1,0:T(8,128)(2,1)S(1)} collective-permute-done((bf16[32,5120]{1,0:T(8,128)(2,1)S(1)}, bf16[32,5120]{1,0:T(8,128)(2,1)S(1)}, u32[]{:S(2)}, u32[]{:S(2)}) %collective-permute-start.13) | collective-permute-done | bytes 327712 | tf_op jit(solution)/shard_map/ppermute | solution.py:72
  144.7 0.7 bitcast_dynamic-update-slice_fusion.1
  145.5 0.7 bitcast_dynamic-update-slice_fusion
  (40 shorter events, 0.7 us)
Async XLA Ops:
  0.6 23.9 %copy-start = (bf16[256,5120]{1,0:T(8,128)(2,1)S(1)}, bf16[256,5120]{1,0:T(8,128)(2,1)}, u32[]{:S(2)}) copy-start(bf16[256,5120]{1,0:T(8,128)(2,1)} %param.5) | copy-start | bytes 7864324
  0.6 22.1 %copy-start.1 = (s32[64]{0:T(128)S(1)}, s32[64]{0:T(128)}, u32[]{:S(2)}) copy-start(s32[64]{0:T(128)} %param.7) | copy-start | bytes 772
  7.0 27.7 %all-to-all-start = ((bf16[64,4,768]{2,1,0:T(4,128)(2,1)}), bf16[64,4,768]{2,1,0:T(4,128)(2,1)S(1)}, u32[]{:S(2)}, u32[]{:S(2)}) async-start(bf16[64,4,768]{2,1,0:T(4,128)(2,1)} %all_to_all.16), calls=%async_computation | async-start | bytes 786432 | tf_op jit(solution)/shard_map/all_to_all | solution.py:102
  37.2 6.2 %collective-permute-start = (f32[4,256]{1,0:T(4,128)S(1)}, f32[4,256]{1,0:T(4,128)S(1)}, u32[]{:S(2)}, u32[]{:S(2)}) collective-permute-start(f32[4,256]{1,0:T(4,128)S(1)} %pad_maximum_fusion), channel_id=1, source_target_pairs={{0,1},{1,2},{2,3},{3,0},{4,5},{5,6},{6,7},{7,4},{8,9},{9,10},{10,1... | collective-permute-start | bytes 12296 | tf_op jit(solution)/shard_map/ppermute | solution.py:44
  38.5 4.9 %collective-permute-start.1 = (f32[4,256]{1,0:T(4,128)S(1)}, f32[4,256]{1,0:T(4,128)S(1)}, u32[]{:S(2)}, u32[]{:S(2)}) collective-permute-start(f32[4,256]{1,0:T(4,128)S(1)} %pad_maximum_fusion), channel_id=1, source_target_pairs={{0,2},{1,3},{2,0},{3,1},{4,6},{5,7},{6,4},{7,5},{8,10},{9,11},{10,... | collective-permute-start | bytes 12296 | tf_op jit(solution)/shard_map/ppermute | solution.py:44
  40.9 2.8 %collective-permute-start.2 = (f32[4,256]{1,0:T(4,128)S(1)}, f32[4,256]{1,0:T(4,128)S(1)}, u32[]{:S(2)}, u32[]{:S(2)}) collective-permute-start(f32[4,256]{1,0:T(4,128)S(1)} %pad_maximum_fusion), channel_id=1, source_target_pairs={{0,3},{1,0},{2,1},{3,2},{4,7},{5,4},{6,5},{7,6},{8,11},{9,8},{10,9... | collective-permute-start | bytes 12296 | tf_op jit(solution)/shard_map/ppermute | solution.py:44
  50.3 1.7 %copy-start.2 = (f32[128,5120]{1,0:T(8,128)}, f32[128,5120]{1,0:T(8,128)S(1)}, u32[]{:S(2)}) copy-start(f32[128,5120]{1,0:T(8,128)S(1)} %get-tuple-element.14) | copy-start | bytes 7864324
  50.3 2.7 %copy-start.4 = (f32[128,5120]{1,0:T(8,128)}, f32[128,5120]{1,0:T(8,128)S(1)}, u32[]{:S(2)}) copy-start(f32[128,5120]{1,0:T(8,128)S(1)} %get-tuple-element.15) | copy-start | bytes 7864324
  51.3 16.0 %collective-permute-start.3 = (f32[32,5120]{1,0:T(8,128)}, f32[32,5120]{1,0:T(8,128)}, u32[]{:S(2)}, u32[]{:S(2)}) collective-permute-start(f32[32,5120]{1,0:T(8,128)} %dynamic-slice_bitcast_fusion.1), channel_id=1, source_target_pairs={{0,1},{1,2},{2,3},{3,0},{4,5},{5,6},{6,7},{7,4},{8,9},{9,10},{10,1... | collective-permute-start | bytes 1966088 | tf_op jit(solution)/shard_map/ppermute | solution.py:64
  53.0 15.7 %collective-permute-start.6 = (f32[32,5120]{1,0:T(8,128)}, f32[32,5120]{1,0:T(8,128)S(1)}, u32[]{:S(2)}, u32[]{:S(2)}) collective-permute-start(f32[32,5120]{1,0:T(8,128)} %dynamic-slice_bitcast_fusion), channel_id=1, source_target_pairs={{0,3},{1,0},{2,1},{3,2},{4,7},{5,4},{6,5},{7,6},{8,11},{9,8},{10,9... | collective-permute-start | bytes 1966088 | tf_op jit(solution)/shard_map/ppermute | solution.py:65
  55.2 28.3 %copy-start.5 = (f32[128,5120]{1,0:T(8,128)S(1)}, f32[128,5120]{1,0:T(8,128)}, u32[]{:S(2)}) copy-start(f32[128,5120]{1,0:T(8,128)} %copy-done.4) | copy-start | bytes 7864324
  56.0 28.0 %copy-start.3 = (f32[128,5120]{1,0:T(8,128)S(1)}, f32[128,5120]{1,0:T(8,128)}, u32[]{:S(2)}) copy-start(f32[128,5120]{1,0:T(8,128)} %copy-done.2) | copy-start | bytes 7864324
  68.6 14.9 %collective-permute-start.4 = (f32[32,5120]{1,0:T(8,128)S(1)}, f32[32,5120]{1,0:T(8,128)S(1)}, u32[]{:S(2)}, u32[]{:S(2)}) collective-permute-start(f32[32,5120]{1,0:T(8,128)S(1)} %bitcast_add_fusion.5), channel_id=1, source_target_pairs={{0,1},{1,2},{2,3},{3,0},{4,5},{5,6},{6,7},{7,4},{8,9},{9,10},{10,1... | collective-permute-start | bytes 1966088 | tf_op jit(solution)/shard_map/ppermute | solution.py:64
  69.9 14.0 %collective-permute-start.7 = (f32[32,5120]{1,0:T(8,128)S(1)}, f32[32,5120]{1,0:T(8,128)S(1)}, u32[]{:S(2)}, u32[]{:S(2)}) collective-permute-start(f32[32,5120]{1,0:T(8,128)S(1)} %bitcast_add_fusion.2), channel_id=1, source_target_pairs={{0,3},{1,0},{2,1},{3,2},{4,7},{5,4},{6,5},{7,6},{8,11},{9,8},{10,9... | collective-permute-start | bytes 1966088 | tf_op jit(solution)/shard_map/ppermute | solution.py:65
  83.6 14.1 %collective-permute-start.5 = (f32[32,5120]{1,0:T(8,128)S(1)}, f32[32,5120]{1,0:T(8,128)S(1)}, u32[]{:S(2)}, u32[]{:S(2)}) collective-permute-start(f32[32,5120]{1,0:T(8,128)S(1)} %bitcast_add_fusion.4), channel_id=1, source_target_pairs={{0,1},{1,2},{2,3},{3,0},{4,5},{5,6},{6,7},{7,4},{8,9},{9,10},{10,1... | collective-permute-start | bytes 1966088 | tf_op jit(solution)/shard_map/ppermute | solution.py:64
  84.0 14.1 %collective-permute-start.8 = (f32[32,5120]{1,0:T(8,128)S(1)}, f32[32,5120]{1,0:T(8,128)S(1)}, u32[]{:S(2)}, u32[]{:S(2)}) collective-permute-start(f32[32,5120]{1,0:T(8,128)S(1)} %bitcast_add_fusion.1), channel_id=1, source_target_pairs={{0,3},{1,0},{2,1},{3,2},{4,7},{5,4},{6,5},{7,6},{8,11},{9,8},{10,9... | collective-permute-start | bytes 1966088 | tf_op jit(solution)/shard_map/ppermute | solution.py:65
  98.1 27.7 %collective-permute-start.9 = (bf16[32,5120]{1,0:T(8,128)(2,1)S(1)}, bf16[32,5120]{1,0:T(8,128)(2,1)}, u32[]{:S(2)}, u32[]{:S(2)}) collective-permute-start(bf16[32,5120]{1,0:T(8,128)(2,1)S(1)} %get-tuple-element.13), channel_id=1, source_target_pairs={{0,1},{1,2},{2,3},{3,0},{4,5},{5,6},{6,7},{7,4},{8,9},{9,10},{10,1... | collective-permute-start | bytes 983048 | tf_op jit(solution)/shard_map/ppermute | solution.py:72
  98.2 1.5 %copy-start.6 = (bf16[8,32,5120]{2,1,0:T(8,128)(2,1)}, bf16[8,32,5120]{2,1,0:T(8,128)(2,1)S(1)}, u32[]{:S(2)}) copy-start(bf16[8,32,5120]{2,1,0:T(8,128)(2,1)S(1)} %get-tuple-element.10) | copy-start | bytes 7864324
  99.7 26.0 %collective-permute-start.10 = (bf16[32,5120]{1,0:T(8,128)(2,1)S(1)}, bf16[32,5120]{1,0:T(8,128)(2,1)}, u32[]{:S(2)}, u32[]{:S(2)}) collective-permute-start(bf16[32,5120]{1,0:T(8,128)(2,1)S(1)} %get-tuple-element.11), channel_id=1, source_target_pairs={{0,3},{1,0},{2,1},{3,2},{4,7},{5,4},{6,5},{7,6},{8,11},{9,8},{10,9... | collective-permute-start | bytes 983048 | tf_op jit(solution)/shard_map/ppermute | solution.py:73
  103.6 20.3 %all-to-all-start.1 = ((f32[64,1,4]{2,1,0:T(1,128)}), f32[64,1,4]{2,1,0:T(1,128)S(1)}, u32[]{:S(2)}, u32[]{:S(2)}) async-start(f32[64,1,4]{2,1,0:T(1,128)} %copy.10), calls=%async_computation.1 | async-start | bytes 65536 | tf_op jit(solution)/shard_map/all_to_all | solution.py:113
  125.7 10.0 %collective-permute-start.11 = (bf16[32,5120]{1,0:T(8,128)(2,1)}, bf16[32,5120]{1,0:T(8,128)(2,1)S(1)}, u32[]{:S(2)}, u32[]{:S(2)}) collective-permute-start(bf16[32,5120]{1,0:T(8,128)(2,1)} %collective-permute-done.9), channel_id=1, source_target_pairs={{0,1},{1,2},{2,3},{3,0},{4,5},{5,6},{6,7},{7,4},{8,9},{9,10},{10,1... | collective-permute-start | bytes 983048 | tf_op jit(solution)/shard_map/ppermute | solution.py:72
  125.8 10.0 %collective-permute-start.12 = (bf16[32,5120]{1,0:T(8,128)(2,1)}, bf16[32,5120]{1,0:T(8,128)(2,1)S(1)}, u32[]{:S(2)}, u32[]{:S(2)}) collective-permute-start(bf16[32,5120]{1,0:T(8,128)(2,1)} %collective-permute-done.10), channel_id=1, source_target_pairs={{0,3},{1,0},{2,1},{3,2},{4,7},{5,4},{6,5},{7,6},{8,11},{9,8},{10,9... | collective-permute-start | bytes 983048 | tf_op jit(solution)/shard_map/ppermute | solution.py:73
  135.8 9.0 %collective-permute-start.13 = (bf16[32,5120]{1,0:T(8,128)(2,1)S(1)}, bf16[32,5120]{1,0:T(8,128)(2,1)S(1)}, u32[]{:S(2)}, u32[]{:S(2)}) collective-permute-start(bf16[32,5120]{1,0:T(8,128)(2,1)S(1)} %collective-permute-done.11), channel_id=1, source_target_pairs={{0,1},{1,2},{2,3},{3,0},{4,5},{5,6},{6,7},{7,4},{8,9},{9,10},{10,1... | collective-permute-start | bytes 983048 | tf_op jit(solution)/shard_map/ppermute | solution.py:72
  135.8 9.7 %collective-permute-start.14 = (bf16[32,5120]{1,0:T(8,128)(2,1)S(1)}, bf16[32,5120]{1,0:T(8,128)(2,1)S(1)}, u32[]{:S(2)}, u32[]{:S(2)}) collective-permute-start(bf16[32,5120]{1,0:T(8,128)(2,1)S(1)} %collective-permute-done.12), channel_id=1, source_target_pairs={{0,3},{1,0},{2,1},{3,2},{4,7},{5,4},{6,5},{7,6},{8,11},{9,8},{10,9... | collective-permute-start | bytes 983048 | tf_op jit(solution)/shard_map/ppermute | solution.py:73
